TPU v7x, 32 devices: a whole 2x2x4 slice. The times are simulated.
32 devices in a mesh: grp: 2 (over x), ctx: 8 (over z, y), ch: 2 (over core).
Axes of the slice: x: 2, y: 2, z: 4, core: 2. Of those that a mesh axis runs over, the one named last changes fastest.
Arguments:
- inputs: bfloat16 [4096, 4096], P(('grp', 'ctx'), 'ch'), parts along dimension 0, may hold values from -0.125 to 0.125
- out_grad: bfloat16 [4096, 4096], P(('grp', 'ctx'), 'ch'), parts along dimension 0, may hold values from -50 to 50
- w_in: float32 [33, 64], replicated, may hold values from -1 to 1
- b_in: float32 [64], replicated, may hold values from -1 to 1
- w_mid: float32 [64, 64], replicated, may hold values from -0.75 to 0.75
- act_freq: float32 [64], replicated, may hold values from 1 to 24
- w_out: float32 [64, 4096], P(None, 'ch'), may hold values from -1 to 1
- decay_rate: float32 [4096], P('ch'), may hold values from 0.000234375 to 0.034
Outputs:
- grad_inputs: bfloat16 [4096, 4096], P(('grp', 'ctx'), 'ch'), parts along dimension 0
- grad_filter: float32 [2048, 4096], P(('grp', 'ctx'), 'ch'), parts along dimension 0
There are 2 independent parts, one for each index of `grp`. A program takes and returns all parts, laid end to end along the dimension named above; an argument that names none is the same for every part. Nothing has to cross between parts.
All inputs are finite; a program needn't handle non-finite values.
Results may differ from a plain program's by a relative error of at most 0.009.
Values may be sent and summed in bfloat16 or wider, within the bound.
No kernel may reach another device: no remote copies, remote signals or barrier semaphores. Data moves between devices by JAX's collectives and lax.ppermute only.
A program may use at most 128 MiB of HBM per device.

v0:
```python
import math

import jax
import jax.numpy as jnp
from jax import lax
from jax.sharding import PartitionSpec as P

LAG_BLOCKS = 4


def from_behind(value, axis, steps):
    count = lax.axis_size(axis)
    leading, last = (max(0, -steps), min(count, count - steps))
    return lax.ppermute(value, axis, [(source, source + steps) for source in range(leading, last)])


def swap_pairs(value, axis, from_side):
    count = lax.axis_size(axis)
    return lax.ppermute(
        value, axis, [(source, source ^ 1) for source in range(from_side, count, 2)]
    )


def gather_later(block):
    side_zero = lax.axis_index("ctx") % 2 == 0
    two_on = from_behind(block, "ctx", -2)
    partner_own = swap_pairs(block, "ctx", 1)
    four_on = from_behind(two_on, "ctx", -2)
    partner_two_on = lax.ppermute(
        two_on, "ctx", [(source, source ^ 1) for source in range(lax.axis_size("ctx"))]
    )
    partner_four_on = swap_pairs(four_on, "ctx", 0)
    one_on = jnp.where(side_zero, partner_own, partner_two_on)
    three_on = jnp.where(side_zero, partner_two_on, partner_four_on)
    return [block, one_on, two_on, three_on, four_on]


def dft_tables(tok_rows):
    freq_ids = jnp.arange(tok_rows, dtype=jnp.int32)
    product = freq_ids[:, None] * freq_ids[None, :] % (2 * tok_rows)
    angles = jnp.float32(math.pi) * product.astype(jnp.float32) / tok_rows
    cosine = jnp.cos(angles)
    sine_table = jnp.sin(angles)
    parity = jnp.where(freq_ids % 2 == 0, 1.0, -1.0).astype(jnp.float32)
    dc_row = (freq_ids == 0)[:, None]
    weights = jnp.where(dc_row, 1.0, 2.0).astype(jnp.float32)
    fwd_re = cosine.astype(jnp.bfloat16)
    fwd_im = jnp.where(dc_row, parity[None, :], -sine_table).astype(jnp.bfloat16)
    inv_re = ((weights * cosine).T / (2 * tok_rows)).astype(jnp.bfloat16)
    inv_im = (jnp.where(dc_row, parity[None, :], -2.0 * sine_table).T / (2 * tok_rows)).astype(
        jnp.bfloat16
    )
    return (fwd_re, fwd_im, inv_re, inv_im, parity, dc_row)


def filter_taps(lag_ids, lag_total, w_in, b_in, w_mid, act_freq, w_out, decay_rate):
    band_count = (w_in.shape[0] - 1) // 2
    harmonic = jnp.arange(1, band_count + 1, dtype=jnp.int32)
    phases = lag_ids[:, None] * harmonic[None, :] % lag_total
    angles = 2.0 * math.pi * phases.astype(jnp.float32) / lag_total
    lag_pos = lag_ids.astype(jnp.float32)[:, None]
    features = jnp.concatenate([lag_pos / lag_total, jnp.cos(angles), jnp.sin(angles)], axis=1)
    first_act = jnp.sin(
        act_freq
        * (
            jnp.dot(
                features, w_in, precision=lax.Precision.HIGHEST, preferred_element_type=jnp.float32
            )
            + b_in
        )
    )
    second_act = jnp.sin(
        act_freq
        * jnp.dot(
            first_act, w_mid, precision=lax.Precision.HIGHEST, preferred_element_type=jnp.float32
        )
    )
    raw_taps = jnp.dot(
        second_act, w_out, precision=lax.Precision.HIGHEST, preferred_element_type=jnp.float32
    )
    return (raw_taps * jnp.exp(-decay_rate[None, :] * lag_pos)).astype(jnp.bfloat16)


def conj_product(left_re, left_im, right_re, right_im, dc_row):
    cross_term = left_im * right_im
    real_part = left_re * right_re + jnp.where(dc_row, 0.0, cross_term)
    imag_part = jnp.where(dc_row, cross_term, left_re * right_im - left_im * right_re)
    return (real_part, imag_part)


def slab_spectrum(fwd_re, fwd_im, slab_data):
    real_part = jnp.dot(fwd_re, slab_data, preferred_element_type=jnp.float32).astype(jnp.bfloat16)
    imag_part = jnp.dot(fwd_im, slab_data, preferred_element_type=jnp.float32).astype(jnp.bfloat16)
    return (real_part, imag_part)


def on_device(inputs, out_grad, w_in, b_in, w_mid, act_freq, w_out, decay_rate):
    tok_rows, chan_width = out_grad.shape
    fwd_re, fwd_im, inv_re, inv_im, parity, dc_row = dft_tables(tok_rows)
    parity_col = parity[:, None]
    lag_total = LAG_BLOCKS * tok_rows
    later_grads = gather_later(out_grad)
    all_lags = jnp.arange(lag_total, dtype=jnp.int32)
    filter_rows = filter_taps(all_lags, lag_total, w_in, b_in, w_mid, act_freq, w_out, decay_rate)
    spectra = [slab_spectrum(fwd_re, fwd_im, received) for received in later_grads]
    pair_list = []
    for lag_block in range(LAG_BLOCKS):
        near_re, near_im = spectra[lag_block]
        far_re, far_im = spectra[lag_block + 1]
        pair_list.append(
            (
                near_re.astype(jnp.float32) + parity_col * far_re.astype(jnp.float32),
                near_im.astype(jnp.float32) + parity_col * far_im.astype(jnp.float32),
            )
        )
    sum_re = jnp.zeros((tok_rows, chan_width), jnp.float32)
    sum_im = jnp.zeros((tok_rows, chan_width), jnp.float32)
    for lag_block in range(LAG_BLOCKS):
        tap_re, tap_im = slab_spectrum(
            fwd_re, fwd_im, filter_rows[lag_block * tok_rows : (lag_block + 1) * tok_rows]
        )
        part_re, part_im = conj_product(
            tap_re.astype(jnp.float32),
            tap_im.astype(jnp.float32),
            pair_list[lag_block][0],
            pair_list[lag_block][1],
            dc_row,
        )
        sum_re = sum_re + part_re
        sum_im = sum_im + part_im
    mix_re = sum_re.astype(jnp.bfloat16)
    mix_im = sum_im.astype(jnp.bfloat16)
    grad_inputs = (
        jnp.dot(inv_re, mix_re, preferred_element_type=jnp.float32)
        + jnp.dot(inv_im, mix_im, preferred_element_type=jnp.float32)
    ).astype(jnp.bfloat16)
    input_re, input_im = slab_spectrum(fwd_re, fwd_im, inputs)
    grad_rows = []
    for lag_block in range(LAG_BLOCKS):
        term_re, term_im = conj_product(
            input_re.astype(jnp.float32),
            input_im.astype(jnp.float32),
            pair_list[lag_block][0],
            pair_list[lag_block][1],
            dc_row,
        )
        grad_rows.append(
            jnp.dot(inv_re, term_re.astype(jnp.bfloat16), preferred_element_type=jnp.float32)
            + jnp.dot(inv_im, term_im.astype(jnp.bfloat16), preferred_element_type=jnp.float32)
        )
    grad_filter = lax.psum_scatter(
        jnp.concatenate(grad_rows, axis=0).astype(jnp.bfloat16),
        "ctx",
        scatter_dimension=0,
        tiled=True,
    ).astype(jnp.float32)
    return (grad_inputs, grad_filter)


def solution(mesh):
    placed = (
        P(("grp", "ctx"), "ch"),
        P(("grp", "ctx"), "ch"),
        P(),
        P(),
        P(),
        P(),
        P(None, "ch"),
        P("ch"),
    )
    return jax.shard_map(
        on_device,
        mesh=mesh,
        in_specs=placed,
        out_specs=(P(("grp", "ctx"), "ch"), P(("grp", "ctx"), "ch")),
        check_vma=False,
    )
```

profile of v0, /device:TPU:0, one launch (start us, length us, event | category | flops | bytes accessed | tf_op | source)
XLA Modules:
  0.0 211.2 jit_solution(5559951192795552327)
XLA Ops:
  7.2 0.0 copy-start
  7.2 0.0 reduce-scatter.2.cloned.1.call-start
  7.2 1.4 collective-permute-start.1
  8.7 1.3 collective-permute-start
  10.0 25.8 %collective-permute-done.1 = bf16[256,2048]{1,0:T(8,128)(2,1)} collective-permute-done((bf16[256,2048]{1,0:T(8,128)(2,1)}, bf16[256,2048]{1,0:T(8,128)(2,1)}, u32[]{:S(2)}, u32[]{:S(2)}) %collective-permute-start.1) | collective-permute-done | bytes 1048608 | tf_op jit(solution)/shard_map/ppermute | solution.py:14
  35.8 1.7 collective-permute-start.2
  37.4 1.4 convolution_convert_fusion.1
  38.8 1.4 convolution_convert_fusion
  40.2 1.5 collective-permute-start.3
  41.7 2.6 %convolution_convert_fusion.12 = bf16[256,2048]{1,0:T(8,128)(2,1)S(1)} fusion(bf16[256,2048]{1,0:T(8,128)(2,1)} %collective-permute-done.1), kind=kOutput, calls=%fused_computation.68 | convolution fusion | flops 269942784 | bytes 2097152 | tf_op jit(solution)/shard_map/dot_general | solution.py:92
  44.3 0.0 copy-start.16
  44.3 3.0 %convolution_convert_fusion.10 = bf16[256,2048]{1,0:T(8,128)(2,1)S(1)} fusion(bf16[256,2048]{1,0:T(8,128)(2,1)} %collective-permute-done.1, f32[256]{0:T(256)S(1)} %get-tuple-element.4, pred[256]{0:T(512)(128)(4,1)S(1)} %iota_compare_fusion), kind=kOutput, calls=%fused_computation.66 | convolution fusion | flops 270008320 | bytes 2098432 | tf_op jit(solution)/shard_map/dot_general | solution.py:93
  47.3 0.0 copy-start.7
  47.3 0.0 collective-permute-done
  47.3 0.0 copy-start.25
  47.3 13.0 %collective-permute-done.2 = bf16[256,2048]{1,0:T(8,128)(2,1)S(1)} collective-permute-done((bf16[256,2048]{1,0:T(8,128)(2,1)}, bf16[256,2048]{1,0:T(8,128)(2,1)S(1)}, u32[]{:S(2)}, u32[]{:S(2)}) %collective-permute-start.2) | collective-permute-done | bytes 1048608 | tf_op jit(solution)/shard_map/ppermute | solution.py:29
  60.3 1.4 convolution_convert_fusion.14
  61.7 0.0 copy-start.26
  61.8 1.4 fusion.23
  63.2 0.2 copy-done.26
  63.4 1.4 convolution_convert_fusion.17
  64.7 0.0 copy-start.10
  64.7 1.4 fusion.22
  66.1 1.8 fusion.66
  67.9 2.8 %fusion.63 = f32[256,2048]{1,0:T(8,128)S(1)} fusion(bf16[256,2048]{1,0:T(8,128)(2,1)S(1)} %convolution_convert_fusion.1, bf16[256,2048]{1,0:T(8,128)(2,1)S(1)} %convolution_convert_fusion, bf16[256,2048]{1,0:T(8,128)(2,1)S(1)} %convolution_convert_fusion.12, bf16[256,2048]{1,0:T(8,128)(2,1)S(1)} %convolution_convert_fusion.17, ...), kind=kOutput, calls=%fused_computation.131 | convolution fusion | flops 277413888 | bytes 8390912 | tf_op jit(solution)/shard_map/dot_general | solution.py:148
  70.7 0.0 collective-permute-done.3
  70.8 3.3 %collective-permute-start.4 = (bf16[256,2048]{1,0:T(8,128)(2,1)S(1)}, bf16[256,2048]{1,0:T(8,128)(2,1)S(1)}, u32[]{:S(2)}, u32[]{:S(2)}) collective-permute-start(bf16[256,2048]{1,0:T(8,128)(2,1)S(1)} %collective-permute-done.3), channel_id=1, source_target_pairs={{0,2},{4,6},{8,10},{12,14},{1,3},{5,7},{9,11},{13,15},{16,18},{20,... | collective-permute-start | bytes 3145736 | tf_op jit(solution)/shard_map/ppermute | solution.py:19
  74.1 0.0 copy-done.1
  74.1 2.0 fusion.1
  76.1 0.0 copy-done.8
  76.2 0.0 copy-done.10
  76.2 2.6 %fusion.2 = bf16[256,2048]{1,0:T(8,128)(2,1)S(1)} fusion(f32[256,2048]{1,0:T(8,128)S(1)} %fusion.63, bf16[256,2048]{1,0:T(8,128)(2,1)S(1)} %convolution_convert_fusion.1, bf16[256,2048]{1,0:T(8,128)(2,1)S(1)} %convolution_convert_fusion, bf16[256,2048]{1,0:T(8,128)(2,1)S(1)} %convolution_convert_fusion.12, ...), kind=kOutput, calls=%fused_computation.53 | convolution fusion | flops 279052288 | bytes 9438464 | tf_op jit(solution)/shard_map/dot_general | solution.py:149
  78.7 15.9 %collective-permute-done.4 = bf16[256,2048]{1,0:T(8,128)(2,1)S(1)} collective-permute-done((bf16[256,2048]{1,0:T(8,128)(2,1)S(1)}, bf16[256,2048]{1,0:T(8,128)(2,1)S(1)}, u32[]{:S(2)}, u32[]{:S(2)}) %collective-permute-start.4) | collective-permute-done | bytes 1048608 | tf_op jit(solution)/shard_map/ppermute | solution.py:19
  94.7 1.4 convolution_convert_fusion.8
  96.0 1.4 convolution_convert_fusion.6
  97.5 2.3 %fusion.60 = f32[256,2048]{1,0:T(8,128)S(1)} fusion(bf16[256,2048]{1,0:T(8,128)(2,1)S(1)} %convolution_convert_fusion.1, bf16[256,2048]{1,0:T(8,128)(2,1)S(1)} %convolution_convert_fusion, bf16[256,2048]{1,0:T(8,128)(2,1)S(1)} %convolution_convert_fusion.8, bf16[256,2048]{1,0:T(8,128)(2,1)S(1)} %convolution_convert_fusion.12, ...), kind=kOutput, calls=%fused_computation.130 | convolution fusion | flops 277413888 | bytes 8390912 | tf_op jit(solution)/shard_map/dot_general | solution.py:148
  99.8 1.4 convert_add_fusion.1
  101.2 1.6 convert_add_fusion
  102.8 1.7 fusion.57
  104.6 2.0 fusion.4
  106.6 2.6 %fusion.3 = bf16[256,2048]{1,0:T(8,128)(2,1)S(1)} fusion(f32[256,2048]{1,0:T(8,128)S(1)} %fusion.60, bf16[256,2048]{1,0:T(8,128)(2,1)S(1)} %convolution_convert_fusion.1, bf16[256,2048]{1,0:T(8,128)(2,1)S(1)} %convolution_convert_fusion, bf16[256,2048]{1,0:T(8,128)(2,1)S(1)} %convolution_convert_fusion.8, ...), kind=kOutput, calls=%fused_computation.54 | convolution fusion | flops 279052288 | bytes 9438464 | tf_op jit(solution)/shard_map/dot_general | solution.py:149
  109.1 2.2 %pad_maximum_fusion = bf16[1024,2048]{1,0:T(8,128)(2,1)} fusion(bf16[256,2048]{1,0:T(8,128)(2,1)S(1)} %fusion.4, bf16[256,2048]{1,0:T(8,128)(2,1)S(1)} %fusion.3, bf16[256,2048]{1,0:T(8,128)(2,1)S(1)} %fusion.2, bf16[256,2048]{1,0:T(8,128)(2,1)S(1)} %fusion.1), kind=kLoop, calls=%fused_computation.17 | loop fusion | flops 16777216 | bytes 8388608 | tf_op jit(solution)/shard_map/concatenate | solution.py:152
  111.4 0.0 copy-start.20
  111.4 0.0 reduce-scatter.2.cloned.1.call-update
  111.4 0.6 copy-done.22
  112.1 0.3 fusion.143
  112.5 2.5 %fusion.55 = f32[1024,64]{1,0:T(8,128)S(1)} fusion(f32[33,64]{1,0:T(8,128)S(1)} %copy-done.21, f32[64]{0:T(128)S(1)} %copy-done.24, f32[64]{0:T(128)S(1)} %copy-done.23, f32[1024,16]{0,1:T(8,128)S(1)} %get-tuple-element.3, f32[1024,16]{0,1:T(8,128)S(1)} %get-tuple-element.2, f32[1024,1]{0,1:T(1,128)S(1)} %convert_multiply_fusion.38), kind=kOutput, calls=%fused_computation.128 | convolution fusion | flops 26150912 | bytes 406272 | tf_op jit(solution)/shard_map/dot_general | solution.py:66
  115.0 2.2 %fusion.53 = f32[1024,64]{1,0:T(8,128)S(1)} fusion(f32[1024,64]{1,0:T(8,128)S(1)} %fusion.55, f32[64,64]{1,0:T(8,128)S(1)} %copy-done.20, f32[64]{0:T(128)S(1)} %copy-done.23), kind=kOutput, calls=%fused_computation.126 | convolution fusion | flops 50397184 | bytes 540928 | tf_op jit(solution)/shard_map/dot_general | solution.py:74
  117.2 8.7 %multiply_convert_fusion = bf16[1024,2048]{1,0:T(8,128)(2,1)S(1)} fusion(f32[1024,64]{1,0:T(8,128)S(1)} %fusion.53, f32[64,2048]{1,0:T(8,128)} %param.14, f32[1024]{0:T(1024)S(1)} %iota_convert_fusion, f32[2048]{0:T(1024)S(1)} %neg.25), kind=kOutput, calls=%fused_computation | convolution fusion | flops 1616904192 | bytes 4993024 | tf_op jit(solution)/shard_map/dot_general | solution.py:78
  125.9 1.4 convolution_convert_fusion.19
  127.3 1.3 convolution_convert_fusion.13
  128.6 1.4 convolution_convert_fusion.9
  130.0 1.3 convolution_convert_fusion.5
  131.4 0.0 copy-start.17
  131.4 1.4 convolution_convert_fusion.16
  132.8 0.0 copy-start.11
  132.8 1.4 convolution_convert_fusion.11
  134.2 1.4 convolution_convert_fusion.7
  135.6 1.4 convolution_convert_fusion.3
  137.1 0.3 copy-done.2
  137.4 4.6 %fusion.85 = f32[256,2048]{1,0:T(8,128)S(1)} fusion(f32[256,2048]{1,0:T(8,128)S(1)} %copy-done.2, bf16[256,2048]{1,0:T(8,128)(2,1)S(1)} %convolution_convert_fusion.19, bf16[256,2048]{1,0:T(8,128)(2,1)S(1)} %convolution_convert_fusion.13, bf16[256,2048]{1,0:T(8,128)(2,1)S(1)} %convolution_convert_fusion.9, f32[256,2048]{1,0:T(8,128)S(1)} %copy-done.4, ...), kind=kOutput, calls=%fused_computation.151 | convolution fusion | flops 291569664 | bytes 25168128 | tf_op jit(solution)/shard_map/dot_general | solution.py:134
  142.0 5.7 %fusion = bf16[256,2048]{1,0:T(8,128)(2,1)} fusion(f32[256,2048]{1,0:T(8,128)S(1)} %fusion.85, f32[256,2048]{1,0:T(8,128)S(1)} %fusion.23, bf16[256,2048]{1,0:T(8,128)(2,1)S(1)} %convolution_convert_fusion.19, f32[256,2048]{1,0:T(8,128)S(1)} %copy-done.2, bf16[256,2048]{1,0:T(8,128)(2,1)S(1)} %convolution_convert_fusion.16, ...), kind=kOutput, calls=%fused_computation.51 | convolution fusion | flops 294780928 | bytes 26215680 | tf_op jit(solution)/shard_map/dot_general | solution.py:135
  147.7 54.1 %reduce-scatter.2.cloned.1.call-done = bf16[128,2048]{1,0:T(8,128)(2,1)} async-done(((bf16[1024,2048]{1,0:T(8,128)(2,1)}), bf16[128,2048]{1,0:T(8,128)(2,1)}) %reduce-scatter.2.cloned.1.call-update) | async-done | bytes 524304 | tf_op jit(solution)/shard_map/reduce_scatter | solution.py:151
  201.8 2.1 %convert_element_type.379 = f32[128,2048]{1,0:T(8,128)} convert(bf16[128,2048]{1,0:T(8,128)(2,1)} %reduce-scatter.2.cloned.1.call-done) | non-fusion elementwise | flops 262144 | bytes 1572864 | tf_op jit(solution)/shard_map/convert_element_type | solution.py:156
  (45 shorter events, 0.1 us)
Async XLA Ops:
  7.2 30.3 %copy-start = (bf16[256,2048]{1,0:T(8,128)(2,1)S(1)}, bf16[256,2048]{1,0:T(8,128)(2,1)}, u32[]{:S(2)}) copy-start(bf16[256,2048]{1,0:T(8,128)(2,1)} %param.8) | copy-start | bytes 3145732
  7.2 194.6 %reduce-scatter.2.cloned.1.call-start = ((), (), s32[]{:S(2)}) async-start(), calls=%async_computation.1 | async-start | bytes 4718592 | tf_op jit(solution)/shard_map/reduce_scatter | solution.py:151
  7.2 28.5 %collective-permute-start.1 = (bf16[256,2048]{1,0:T(8,128)(2,1)}, bf16[256,2048]{1,0:T(8,128)(2,1)}, u32[]{:S(2)}, u32[]{:S(2)}) collective-permute-start(bf16[256,2048]{1,0:T(8,128)(2,1)} %param.9), channel_id=1, source_target_pairs={{4,0},{6,2},{8,4},{10,6},{12,8},{14,10},{5,1},{7,3},{9,5},{11,7},{... | collective-permute-start | bytes 3145736 | tf_op jit(solution)/shard_map/ppermute | solution.py:14
  8.7 38.7 %collective-permute-start = (bf16[256,2048]{1,0:T(8,128)(2,1)}, bf16[256,2048]{1,0:T(8,128)(2,1)S(1)}, u32[]{:S(2)}, u32[]{:S(2)}) collective-permute-start(bf16[256,2048]{1,0:T(8,128)(2,1)} %param.9), channel_id=1, source_target_pairs={{2,0},{6,4},{10,8},{14,12},{3,1},{7,5},{11,9},{15,13},{18,16},{22,... | collective-permute-start | bytes 3145736 | tf_op jit(solution)/shard_map/ppermute | solution.py:19
  35.8 24.6 %collective-permute-start.2 = (bf16[256,2048]{1,0:T(8,128)(2,1)}, bf16[256,2048]{1,0:T(8,128)(2,1)S(1)}, u32[]{:S(2)}, u32[]{:S(2)}) collective-permute-start(bf16[256,2048]{1,0:T(8,128)(2,1)} %collective-permute-done.1), channel_id=1, source_target_pairs={{0,2},{2,0},{4,6},{6,4},{8,10},{10,8},{12,14},{14,12},{1,3},{3,1},... | collective-permute-start | bytes 3145736 | tf_op jit(solution)/shard_map/ppermute | solution.py:29
  40.2 30.6 %collective-permute-start.3 = (bf16[256,2048]{1,0:T(8,128)(2,1)}, bf16[256,2048]{1,0:T(8,128)(2,1)S(1)}, u32[]{:S(2)}, u32[]{:S(2)}) collective-permute-start(bf16[256,2048]{1,0:T(8,128)(2,1)} %collective-permute-done.1), channel_id=1, source_target_pairs={{4,0},{6,2},{8,4},{10,6},{12,8},{14,10},{5,1},{7,3},{9,5},{11,7},{... | collective-permute-start | bytes 3145736 | tf_op jit(solution)/shard_map/ppermute | solution.py:14
  44.3 62.2 %copy-start.16 = (bf16[256,2048]{1,0:T(8,128)(2,1)}, bf16[256,2048]{1,0:T(8,128)(2,1)S(1)}, u32[]{:S(2)}) copy-start(bf16[256,2048]{1,0:T(8,128)(2,1)S(1)} %convolution_convert_fusion.12) | copy-start | bytes 3145732
  47.3 59.2 %copy-start.18 = (bf16[256,2048]{1,0:T(8,128)(2,1)}, bf16[256,2048]{1,0:T(8,128)(2,1)S(1)}, u32[]{:S(2)}) copy-start(bf16[256,2048]{1,0:T(8,128)(2,1)S(1)} %convolution_convert_fusion.10) | copy-start | bytes 3145732
  47.3 14.4 %copy-start.7 = (bf16[256,2048]{1,0:T(8,128)(2,1)S(1)}, bf16[256,2048]{1,0:T(8,128)(2,1)}, u32[]{:S(2)}) copy-start(bf16[256,2048]{1,0:T(8,128)(2,1)} %param.9) | copy-start | bytes 3145732
  47.3 13.0 %copy-start.25 = (bf16[256,2048]{1,0:T(8,128)(2,1)}, bf16[256,2048]{1,0:T(8,128)(2,1)S(1)}, u32[]{:S(2)}) copy-start(bf16[256,2048]{1,0:T(8,128)(2,1)S(1)} %collective-permute-done) | copy-start | bytes 3145732
  61.7 14.4 %copy-start.8 = (bf16[256,2048]{1,0:T(8,128)(2,1)}, bf16[256,2048]{1,0:T(8,128)(2,1)S(1)}, u32[]{:S(2)}) copy-start(bf16[256,2048]{1,0:T(8,128)(2,1)S(1)} %convolution_convert_fusion.14) | copy-start | bytes 3145732
  61.7 1.6 copy-start.26
  64.7 11.4 %copy-start.10 = (bf16[256,2048]{1,0:T(8,128)(2,1)}, bf16[256,2048]{1,0:T(8,128)(2,1)S(1)}, u32[]{:S(2)}) copy-start(bf16[256,2048]{1,0:T(8,128)(2,1)S(1)} %convolution_convert_fusion.17) | copy-start | bytes 3145732
  66.1 8.0 %copy-start.1 = (f32[256,2048]{1,0:T(8,128)}, f32[256,2048]{1,0:T(8,128)S(1)}, u32[]{:S(2)}) copy-start(f32[256,2048]{1,0:T(8,128)S(1)} %fusion.22) | copy-start | bytes 6291460
  70.8 23.9 %collective-permute-start.4 = (bf16[256,2048]{1,0:T(8,128)(2,1)S(1)}, bf16[256,2048]{1,0:T(8,128)(2,1)S(1)}, u32[]{:S(2)}, u32[]{:S(2)}) collective-permute-start(bf16[256,2048]{1,0:T(8,128)(2,1)S(1)} %collective-permute-done.3), channel_id=1, source_target_pairs={{0,2},{4,6},{8,10},{12,14},{1,3},{5,7},{9,11},{13,15},{16,18},{20,... | collective-permute-start | bytes 3145736 | tf_op jit(solution)/shard_map/ppermute | solution.py:19
  96.0 10.5 %copy-start.12 = (bf16[256,2048]{1,0:T(8,128)(2,1)}, bf16[256,2048]{1,0:T(8,128)(2,1)S(1)}, u32[]{:S(2)}) copy-start(bf16[256,2048]{1,0:T(8,128)(2,1)S(1)} %convolution_convert_fusion.8) | copy-start | bytes 3145732
  97.5 9.1 %copy-start.14 = (bf16[256,2048]{1,0:T(8,128)(2,1)}, bf16[256,2048]{1,0:T(8,128)(2,1)S(1)}, u32[]{:S(2)}) copy-start(bf16[256,2048]{1,0:T(8,128)(2,1)S(1)} %convolution_convert_fusion.6) | copy-start | bytes 3145732
  101.2 3.4 %copy-start.3 = (f32[256,2048]{1,0:T(8,128)}, f32[256,2048]{1,0:T(8,128)S(1)}, u32[]{:S(2)}) copy-start(f32[256,2048]{1,0:T(8,128)S(1)} %convert_add_fusion.1) | copy-start | bytes 6291460
  102.8 1.8 copy-start.5
  111.4 0.7 copy-start.22
  111.4 1.1 copy-start.21
  111.4 1.1 copy-start.23
  111.4 1.1 copy-start.24
  111.4 3.6 %copy-start.20 = (f32[64,64]{1,0:T(8,128)S(1)}, f32[64,64]{1,0:T(8,128)}, u32[]{:S(2)}) copy-start(f32[64,64]{1,0:T(8,128)} %param.12) | copy-start | bytes 49156
  130.0 7.0 %copy-start.19 = (bf16[256,2048]{1,0:T(8,128)(2,1)S(1)}, bf16[256,2048]{1,0:T(8,128)(2,1)}, u32[]{:S(2)}) copy-start(bf16[256,2048]{1,0:T(8,128)(2,1)} %copy-done.18) | copy-start | bytes 3145732
  131.4 5.6 %copy-start.13 = (bf16[256,2048]{1,0:T(8,128)(2,1)S(1)}, bf16[256,2048]{1,0:T(8,128)(2,1)}, u32[]{:S(2)}) copy-start(bf16[256,2048]{1,0:T(8,128)(2,1)} %copy-done.12) | copy-start | bytes 3145732
  131.4 5.6 %copy-start.15 = (bf16[256,2048]{1,0:T(8,128)(2,1)S(1)}, bf16[256,2048]{1,0:T(8,128)(2,1)}, u32[]{:S(2)}) copy-start(bf16[256,2048]{1,0:T(8,128)(2,1)} %copy-done.14) | copy-start | bytes 3145732
  131.4 5.6 %copy-start.17 = (bf16[256,2048]{1,0:T(8,128)(2,1)S(1)}, bf16[256,2048]{1,0:T(8,128)(2,1)}, u32[]{:S(2)}) copy-start(bf16[256,2048]{1,0:T(8,128)(2,1)} %copy-done.16) | copy-start | bytes 3145732
  132.8 4.3 %copy-start.6 = (f32[256,2048]{1,0:T(8,128)S(1)}, f32[256,2048]{1,0:T(8,128)}, u32[]{:S(2)}) copy-start(f32[256,2048]{1,0:T(8,128)} %copy-done.5) | copy-start | bytes 6291460
  132.8 4.3 %copy-start.11 = (bf16[256,2048]{1,0:T(8,128)(2,1)S(1)}, bf16[256,2048]{1,0:T(8,128)(2,1)}, u32[]{:S(2)}) copy-start(bf16[256,2048]{1,0:T(8,128)(2,1)} %copy-done.10) | copy-start | bytes 3145732
  134.2 2.9 %copy-start.4 = (f32[256,2048]{1,0:T(8,128)S(1)}, f32[256,2048]{1,0:T(8,128)}, u32[]{:S(2)}) copy-start(f32[256,2048]{1,0:T(8,128)} %copy-done.3) | copy-start | bytes 6291460
  134.2 2.9 %copy-start.9 = (bf16[256,2048]{1,0:T(8,128)(2,1)S(1)}, bf16[256,2048]{1,0:T(8,128)(2,1)}, u32[]{:S(2)}) copy-start(bf16[256,2048]{1,0:T(8,128)(2,1)} %copy-done.8) | copy-start | bytes 3145732
  135.6 1.8 copy-start.2
Sparse Core Ops, SparseCore 0:
  111.6 90.1 reduce-scatter.1
where the time goes:
time: 215 us; the launch traced here: 211 us
  waiting for transfers between devices  109 us (51%)
  matrix products  72 us (33%)
  between operations  15.1 us (7%)
  starting transfers between devices  9.27 us (4%)
  other arithmetic  4.74 us (2%)
    reduce_scatter x1, waiting for transfers between devices, on_device(): lax.psum_scatter(jnp.concatenate(grad_rows, axis=0).astype(jnp.bfloat16),...  54.1 us
    ppermute x2, waiting for transfers between devices, from_behind(): lax.ppermute(value, axis, [(source, source + steps) for source in range(l...  25.8 us
    ppermute x2, waiting for transfers between devices, swap_pairs(): lax.ppermute(value, axis, [(source, source ^ 1) for source in range(from_...  15.9 us
    dot_general x10, matrix products, slab_spectrum(): jnp.dot(fwd_im, slab_data, preferred_element_type=jnp.float32)  15.7 us
    dot_general x10, matrix products, slab_spectrum(): jnp.dot(fwd_re, slab_data, preferred_element_type=jnp.float32)  14.8 us
    ppermute x1, waiting for transfers between devices, gather_later(): lax.ppermute(two_on, 'ctx', [(source, source ^ 1) for source in range(lax...  13 us
    dot_general x4, matrix products, on_device(): jnp.dot(inv_im, term_im.astype(jnp.bfloat16), preferred_element_type=jnp....  9.11 us
    dot_general x1, matrix products, filter_taps(): jnp.dot(second_act, w_out, precision=lax.Precision.HIGHEST, preferred_ele...  8.72 us
  transfers between devices with their start and end apart: 6, of which 4 were waited for; matrix products, arithmetic and copies ran while one was open for 27% of the time, Pallas kernels for 0%

commit v1 on v0

--- a/solution.py
+++ b/solution.py
@@ -89,9 +89,22 @@
 
 
 def slab_spectrum(fwd_re, fwd_im, slab_data):
-    real_part = jnp.dot(fwd_re, slab_data, preferred_element_type=jnp.float32).astype(jnp.bfloat16)
-    imag_part = jnp.dot(fwd_im, slab_data, preferred_element_type=jnp.float32).astype(jnp.bfloat16)
-    return (real_part, imag_part)
+    rows = fwd_re.shape[0]
+    both = jnp.dot(
+        jnp.concatenate([fwd_re, fwd_im], axis=0), slab_data, preferred_element_type=jnp.float32
+    ).astype(jnp.bfloat16)
+    return (both[:rows], both[rows:])
+
+
+def batch_spectrum(fwd_re, fwd_im, slabs):
+    rows = fwd_re.shape[0]
+    both = jnp.einsum(
+        "fs,jsc->jfc",
+        jnp.concatenate([fwd_re, fwd_im], axis=0),
+        slabs,
+        preferred_element_type=jnp.float32,
+    ).astype(jnp.bfloat16)
+    return (both[:, :rows], both[:, rows:])
 
 
 def on_device(inputs, out_grad, w_in, b_in, w_mid, act_freq, w_out, decay_rate):
@@ -115,10 +128,11 @@
         )
     sum_re = jnp.zeros((tok_rows, chan_width), jnp.float32)
     sum_im = jnp.zeros((tok_rows, chan_width), jnp.float32)
+    taps_re, taps_im = batch_spectrum(
+        fwd_re, fwd_im, filter_rows.reshape(LAG_BLOCKS, tok_rows, chan_width)
+    )
     for lag_block in range(LAG_BLOCKS):
-        tap_re, tap_im = slab_spectrum(
-            fwd_re, fwd_im, filter_rows[lag_block * tok_rows : (lag_block + 1) * tok_rows]
-        )
+        tap_re, tap_im = taps_re[lag_block], taps_im[lag_block]
         part_re, part_im = conj_product(
             tap_re.astype(jnp.float32),
             tap_im.astype(jnp.float32),
@@ -130,9 +144,9 @@
         sum_im = sum_im + part_im
     mix_re = sum_re.astype(jnp.bfloat16)
     mix_im = sum_im.astype(jnp.bfloat16)
-    grad_inputs = (
-        jnp.dot(inv_re, mix_re, preferred_element_type=jnp.float32)
-        + jnp.dot(inv_im, mix_im, preferred_element_type=jnp.float32)
+    inv_both = jnp.concatenate([inv_re, inv_im], axis=1)
+    grad_inputs = jnp.dot(
+        inv_both, jnp.concatenate([mix_re, mix_im], axis=0), preferred_element_type=jnp.float32
     ).astype(jnp.bfloat16)
     input_re, input_im = slab_spectrum(fwd_re, fwd_im, inputs)
     grad_rows = []
@@ -145,8 +159,11 @@
             dc_row,
         )
         grad_rows.append(
-            jnp.dot(inv_re, term_re.astype(jnp.bfloat16), preferred_element_type=jnp.float32)
-            + jnp.dot(inv_im, term_im.astype(jnp.bfloat16), preferred_element_type=jnp.float32)
+            jnp.dot(
+                inv_both,
+                jnp.concatenate([term_re, term_im], axis=0).astype(jnp.bfloat16),
+                preferred_element_type=jnp.float32,
+            )
         )
     grad_filter = lax.psum_scatter(
         jnp.concatenate(grad_rows, axis=0).astype(jnp.bfloat16),

time: 215 us -> 197 us (0.916); the launches traced: 211 us -> 197 us
  matrix products: 72 us -> 31.2 us
  other arithmetic: 4.74 us -> 24.2 us
  waiting for transfers between devices: 109 us -> 116 us
    dot_general x30 -> x12, matrix products: 58.6 us -> 16.2 us  [the longest x6 9.31 us: slab_spectrum(): jnp.dot(jnp.concatenate([fwd_re, fwd_im], axis=0), slab_data, preferred_e...]
    convert_element_type x0 -> x5, other arithmetic: none -> 12.8 us  [the longest x1 4.59 us: on_device(): mix_im = sum_im.astype(jnp.bfloat16)]
    another operation x0 -> x4, other arithmetic: none -> 6.59 us
    reduce_scatter x1, waiting for transfers between devices: 54.1 us -> 57.3 us  [on_device(): lax.psum_scatter(jnp.concatenate(grad_rows, axis=0).astype(jnp.bfloat16),...]
  transfers between devices with their start and end apart: 6 -> 6, of which waited for: 4 -> 5; matrix products, arithmetic and copies ran while one was open for 27% -> 22% of each run, Pallas kernels for 0% -> 0%
where the time goes in v1:
time: 197 us
  waiting for transfers between devices  116 us (59%)
  matrix products  31.2 us (16%)
  other arithmetic  24.2 us (12%)
  between operations  14.4 us (7%)
  starting transfers between devices  8.53 us (4%)
  local copies, waits for them, and re-layouts  2.87 us (1%)
    reduce_scatter x1, waiting for transfers between devices, on_device(): lax.psum_scatter(jnp.concatenate(grad_rows, axis=0).astype(jnp.bfloat16),...  57.3 us
    ppermute x2, waiting for transfers between devices, from_behind(): lax.ppermute(value, axis, [(source, source + steps) for source in range(l...  27.9 us
    ppermute x2, waiting for transfers between devices, swap_pairs(): lax.ppermute(value, axis, [(source, source ^ 1) for source in range(from_...  16.5 us
    ppermute x1, waiting for transfers between devices, gather_later(): lax.ppermute(two_on, 'ctx', [(source, source ^ 1) for source in range(lax...  14 us
    dot_general x6, matrix products, slab_spectrum(): jnp.dot(jnp.concatenate([fwd_re, fwd_im], axis=0), slab_data, preferred_e...  9.31 us
    dot_general x1, matrix products, filter_taps(): jnp.dot(second_act, w_out, precision=lax.Precision.HIGHEST, preferred_ele...  8.73 us
    another operation x4, other arithmetic  6.59 us
    convert_element_type x1, other arithmetic, on_device(): mix_im = sum_im.astype(jnp.bfloat16)  4.59 us
  transfers between devices with their start and end apart: 6, of which 5 were waited for; matrix products, arithmetic and copies ran while one was open for 22% of the time, Pallas kernels for 0%

profile of v1, /device:TPU:0, one launch (start us, length us, event | category | flops | bytes accessed | tf_op | source)
XLA Modules:
  0.0 196.9 jit_solution(5012818922080951378)
XLA Ops:
  7.2 0.0 copy-start
  7.2 0.0 reduce-scatter.2.cloned.1.call-start
  7.2 1.4 collective-permute-start.1
  8.7 1.3 collective-permute-start
  10.0 1.8 multiply_convert_fusion.1
  11.8 23.9 %collective-permute-done.1 = bf16[256,2048]{1,0:T(8,128)(2,1)} collective-permute-done((bf16[256,2048]{1,0:T(8,128)(2,1)}, bf16[256,2048]{1,0:T(8,128)(2,1)}, u32[]{:S(2)}, u32[]{:S(2)}) %collective-permute-start.1) | collective-permute-done | bytes 1048608 | tf_op jit(solution)/shard_map/ppermute | solution.py:14
  35.8 1.7 collective-permute-start.2
  37.4 1.0 select_convert_fusion
  38.5 1.0 fusion.78
  39.5 1.9 convolution_convert_fusion.5
  41.4 0.0 copy-done
  41.4 0.0 copy-start.5
  41.5 0.7 convolution_convert_fusion
  42.2 1.3 collective-permute-start.3
  43.5 2.0 convolution_convert_fusion.3
  45.4 0.0 copy-start.3
  45.4 0.0 collective-permute-done
  45.5 0.0 copy-start.9
  45.5 1.0 copy-done.9
  46.5 14.0 %collective-permute-done.2 = bf16[256,2048]{1,0:T(8,128)(2,1)} collective-permute-done((bf16[256,2048]{1,0:T(8,128)(2,1)}, bf16[256,2048]{1,0:T(8,128)(2,1)}, u32[]{:S(2)}, u32[]{:S(2)}) %collective-permute-start.2) | collective-permute-done | bytes 1048608 | tf_op jit(solution)/shard_map/ppermute | solution.py:29
  60.4 2.0 %convolution_convert_fusion.4 = bf16[512,2048]{1,0:T(8,128)(2,1)S(1)} fusion(bf16[256,2048]{1,0:T(8,128)(2,1)} %copy-done.9, bf16[256,2048]{1,0:T(8,128)(2,1)} %collective-permute-done.2, pred[]{:T(512)S(6)} %eq.88, bf16[256,256]{1,0:T(8,128)(2,1)S(1)} %select_convert_fusion, bf16[256,256]{1,0:T(8,128)(2,1)S(1)} %fusion.78), kind=kOutput, calls=%fused_computation.23 | convolution fusion | flops 538968064 | bytes 4456449 | tf_op jit(solution)/shard_map/dot_general | solution.py:93
  62.4 0.0 copy-start.10
  62.4 1.7 fusion.28
  64.1 4.0 %collective-permute-done.3 = bf16[256,2048]{1,0:T(8,128)(2,1)S(1)} collective-permute-done((bf16[256,2048]{1,0:T(8,128)(2,1)}, bf16[256,2048]{1,0:T(8,128)(2,1)S(1)}, u32[]{:S(2)}, u32[]{:S(2)}) %collective-permute-start.3) | collective-permute-done | bytes 1048608 | tf_op jit(solution)/shard_map/ppermute | solution.py:14
  68.0 2.8 %collective-permute-start.4 = (bf16[256,2048]{1,0:T(8,128)(2,1)S(1)}, bf16[256,2048]{1,0:T(8,128)(2,1)S(1)}, u32[]{:S(2)}, u32[]{:S(2)}) collective-permute-start(bf16[256,2048]{1,0:T(8,128)(2,1)S(1)} %collective-permute-done.3), channel_id=1, source_target_pairs={{0,2},{4,6},{8,10},{12,14},{1,3},{5,7},{9,11},{13,15},{16,18},{20,... | collective-permute-start | bytes 3145736 | tf_op jit(solution)/shard_map/ppermute | solution.py:19
  70.8 0.0 copy-done.10
  70.9 0.7 convolution_convert_fusion.8
  71.6 0.0 copy-done.5
  71.6 1.6 fusion.23
  73.2 0.7 convolution_convert_fusion.9
  74.0 0.7 convolution_convert_fusion.1
  74.7 0.0 copy-start.7
  74.7 16.5 %collective-permute-done.4 = bf16[256,2048]{1,0:T(8,128)(2,1)S(1)} collective-permute-done((bf16[256,2048]{1,0:T(8,128)(2,1)S(1)}, bf16[256,2048]{1,0:T(8,128)(2,1)S(1)}, u32[]{:S(2)}, u32[]{:S(2)}) %collective-permute-start.4) | collective-permute-done | bytes 1048608 | tf_op jit(solution)/shard_map/ppermute | solution.py:19
  91.2 2.0 %convolution_convert_fusion.2 = bf16[512,2048]{1,0:T(8,128)(2,1)S(1)} fusion(bf16[256,2048]{1,0:T(8,128)(2,1)} %collective-permute-done.2, bf16[256,2048]{1,0:T(8,128)(2,1)S(1)} %collective-permute-done.4, pred[]{:T(512)S(6)} %eq.88, bf16[256,256]{1,0:T(8,128)(2,1)S(1)} %select_convert_fusion, bf16[256,256]{1,0:T(8,128)(2,1)S(1)} %fusion.78), kind=kOutput, calls=%fused_computation.21 | convolution fusion | flops 538968064 | bytes 4456449 | tf_op jit(solution)/shard_map/dot_general | solution.py:93
  93.3 0.0 copy-done.3
  93.3 0.0 copy-start.1
  93.3 1.6 fusion.33
  94.9 0.0 copy-done.7
  94.9 0.0 copy-done.1
  94.9 1.7 fusion.38
  96.6 0.7 convolution_convert_fusion.6
  97.3 0.7 convolution_convert_fusion.7
  98.0 2.3 %pad_maximum_fusion = bf16[1024,2048]{1,0:T(8,128)(2,1)} fusion(bf16[256,2048]{1,0:T(8,128)(2,1)S(1)} %convolution_convert_fusion.6, bf16[256,2048]{1,0:T(8,128)(2,1)S(1)} %convolution_convert_fusion.7, bf16[256,2048]{1,0:T(8,128)(2,1)S(1)} %convolution_convert_fusion.8, bf16[256,2048]{1,0:T(8,128)(2,1)S(1)} %convolution_convert_fusion.9), kind=kLoop, calls=%fused_computation.18 | loop fusion | flops 16777216 | bytes 8388608 | tf_op jit(solution)/shard_map/concatenate | solution.py:169
  100.3 0.0 reduce-scatter.2.cloned.1.call-update
  100.4 0.7 copy-done.12
  101.1 0.3 fusion.86
  101.4 3.3 %fusion.59 = f32[1024,64]{1,0:T(8,128)S(1)} fusion(f32[33,64]{1,0:T(8,128)} %param.10, f32[64]{0:T(128)} %param.11, f32[64]{0:T(128)} %param.13, f32[1024,16]{0,1:T(8,128)S(1)} %get-tuple-element.11, f32[1024,16]{0,1:T(8,128)S(1)} %get-tuple-element.10, f32[1024,1]{0,1:T(1,128)S(1)} %convert_multiply_fusion.38), kind=kOutput, calls=%fused_computation.119 | convolution fusion | flops 26150912 | bytes 406272 | tf_op jit(solution)/shard_map/dot_general | solution.py:66
  104.7 2.9 %fusion.57 = f32[1024,64]{1,0:T(8,128)S(1)} fusion(f32[1024,64]{1,0:T(8,128)S(1)} %fusion.59, f32[64,64]{1,0:T(8,128)} %param.12, f32[64]{0:T(128)} %param.13), kind=kOutput, calls=%fused_computation.117 | convolution fusion | flops 50397184 | bytes 540928 | tf_op jit(solution)/shard_map/dot_general | solution.py:74
  107.6 8.7 %multiply_convert_fusion = bf16[1024,2048]{1,0:T(8,128)(2,1)S(1)} fusion(f32[1024,64]{1,0:T(8,128)S(1)} %fusion.57, f32[64,2048]{1,0:T(8,128)} %param.14, f32[1024]{0:T(1024)S(1)} %iota_convert_fusion, f32[2048]{0:T(1024)S(1)} %neg.7), kind=kOutput, calls=%fused_computation.1 | convolution fusion | flops 1616904192 | bytes 4993024 | tf_op jit(solution)/shard_map/dot_general | solution.py:78
  116.3 0.0 copy-start.2
  116.4 0.0 copy-start.4
  116.4 0.0 copy-start.6
  116.4 0.0 copy-start.8
  116.4 2.4 %convert_bitcast_fusion = bf16[4,512,2048]{2,1,0:T(8,128)(2,1)S(1)} fusion(bf16[4,256,2048]{2,1,0:T(8,128)(2,1)S(1)} %bitcast.72, bf16[256,256]{1,0:T(8,128)(2,1)S(1)} %select_convert_fusion, bf16[256,256]{1,0:T(8,128)(2,1)S(1)} %fusion.78), kind=kOutput, calls=%fused_computation | convolution fusion | flops 2152202240 | bytes 12845056 | tf_op jit(solution)/shard_map/fs,jsc->jfc/dot_general | solution.py:101
  118.8 0.0 copy-done.2
  118.8 0.0 copy-done.4
  118.8 0.5 copy-done.6
  119.3 0.6 copy-done.8
  119.9 4.4 %fusion.6 = bf16[256,2048]{1,0:T(8,128)(2,1)S(1)} fusion(f32[256]{0:T(256)S(1)} %compare_select_fusion, pred[256]{0:T(512)(128)(4,1)S(1)} %iota_compare_fusion, bf16[4,512,2048]{2,1,0:T(8,128)(2,1)S(1)} %convert_bitcast_fusion, bf16[512,2048]{1,0:T(8,128)(2,1)S(1)} %copy-done.8, bf16[512,2048]{1,0:T(8,128)(2,1)S(1)} %copy-done.6, ...), kind=kLoop, calls=%fused_computation.64 | loop fusion | flops 28311552 | bytes 19924224 | tf_op jit(solution)/shard_map/convert_element_type | solution.py:145
  124.3 0.0 copy-start.11
  124.3 4.6 %fusion.12 = bf16[256,2048]{1,0:T(8,128)(2,1)S(1)} fusion(f32[256]{0:T(256)S(1)} %compare_select_fusion, pred[256]{0:T(512)(128)(4,1)S(1)} %iota_compare_fusion, bf16[4,512,2048]{2,1,0:T(8,128)(2,1)S(1)} %convert_bitcast_fusion, bf16[512,2048]{1,0:T(8,128)(2,1)S(1)} %copy-done.8, bf16[512,2048]{1,0:T(8,128)(2,1)S(1)} %copy-done.6, ...), kind=kLoop, calls=%fused_computation.70 | loop fusion | flops 30408704 | bytes 19924224 | tf_op jit(solution)/shard_map/convert_element_type | solution.py:146
  128.9 1.7 convolution_convert_fusion.10
  130.6 57.3 %reduce-scatter.2.cloned.1.call-done = bf16[128,2048]{1,0:T(8,128)(2,1)} async-done(((bf16[1024,2048]{1,0:T(8,128)(2,1)}), bf16[128,2048]{1,0:T(8,128)(2,1)}) %reduce-scatter.2.cloned.1.call-update) | async-done | bytes 524304 | tf_op jit(solution)/shard_map/reduce_scatter | solution.py:168
  187.9 2.1 %convert_element_type.231 = f32[128,2048]{1,0:T(8,128)} convert(bf16[128,2048]{1,0:T(8,128)(2,1)} %reduce-scatter.2.cloned.1.call-done) | non-fusion elementwise | flops 262144 | bytes 1572864 | tf_op jit(solution)/shard_map/convert_element_type | solution.py:173
  (9 shorter events, 0.0 us)
Async XLA Ops:
  7.2 34.3 %copy-start = (bf16[256,2048]{1,0:T(8,128)(2,1)S(1)}, bf16[256,2048]{1,0:T(8,128)(2,1)}, u32[]{:S(2)}) copy-start(bf16[256,2048]{1,0:T(8,128)(2,1)} %param.8) | copy-start | bytes 3145732
  7.2 180.7 %reduce-scatter.2.cloned.1.call-start = ((), (), s32[]{:S(2)}) async-start(), calls=%async_computation.1 | async-start | bytes 4718592 | tf_op jit(solution)/shard_map/reduce_scatter | solution.py:168
  7.2 28.5 %collective-permute-start.1 = (bf16[256,2048]{1,0:T(8,128)(2,1)}, bf16[256,2048]{1,0:T(8,128)(2,1)}, u32[]{:S(2)}, u32[]{:S(2)}) collective-permute-start(bf16[256,2048]{1,0:T(8,128)(2,1)} %param.9), channel_id=1, source_target_pairs={{4,0},{6,2},{8,4},{10,6},{12,8},{14,10},{5,1},{7,3},{9,5},{11,7},{... | collective-permute-start | bytes 3145736 | tf_op jit(solution)/shard_map/ppermute | solution.py:14
  8.7 36.8 %collective-permute-start = (bf16[256,2048]{1,0:T(8,128)(2,1)}, bf16[256,2048]{1,0:T(8,128)(2,1)S(1)}, u32[]{:S(2)}, u32[]{:S(2)}) collective-permute-start(bf16[256,2048]{1,0:T(8,128)(2,1)} %param.9), channel_id=1, source_target_pairs={{2,0},{6,4},{10,8},{14,12},{3,1},{7,5},{11,9},{15,13},{18,16},{22,... | collective-permute-start | bytes 3145736 | tf_op jit(solution)/shard_map/ppermute | solution.py:19
  35.8 24.7 %collective-permute-start.2 = (bf16[256,2048]{1,0:T(8,128)(2,1)}, bf16[256,2048]{1,0:T(8,128)(2,1)}, u32[]{:S(2)}, u32[]{:S(2)}) collective-permute-start(bf16[256,2048]{1,0:T(8,128)(2,1)} %collective-permute-done.1), channel_id=1, source_target_pairs={{0,2},{2,0},{4,6},{6,4},{8,10},{10,8},{12,14},{14,12},{1,3},{3,1},... | collective-permute-start | bytes 3145736 | tf_op jit(solution)/shard_map/ppermute | solution.py:29
  41.4 30.1 %copy-start.5 = (bf16[512,2048]{1,0:T(8,128)(2,1)}, bf16[512,2048]{1,0:T(8,128)(2,1)S(1)}, u32[]{:S(2)}) copy-start(bf16[512,2048]{1,0:T(8,128)(2,1)S(1)} %convolution_convert_fusion.5) | copy-start | bytes 6291460
  42.2 25.9 %collective-permute-start.3 = (bf16[256,2048]{1,0:T(8,128)(2,1)}, bf16[256,2048]{1,0:T(8,128)(2,1)S(1)}, u32[]{:S(2)}, u32[]{:S(2)}) collective-permute-start(bf16[256,2048]{1,0:T(8,128)(2,1)} %collective-permute-done.1), channel_id=1, source_target_pairs={{4,0},{6,2},{8,4},{10,6},{12,8},{14,10},{5,1},{7,3},{9,5},{11,7},{... | collective-permute-start | bytes 3145736 | tf_op jit(solution)/shard_map/ppermute | solution.py:14
  45.4 47.8 %copy-start.3 = (bf16[512,2048]{1,0:T(8,128)(2,1)}, bf16[512,2048]{1,0:T(8,128)(2,1)S(1)}, u32[]{:S(2)}) copy-start(bf16[512,2048]{1,0:T(8,128)(2,1)S(1)} %convolution_convert_fusion.3) | copy-start | bytes 6291460
  45.5 1.0 copy-start.9
  62.4 8.4 %copy-start.10 = (bf16[256,256]{1,0:T(8,128)(2,1)S(1)}, bf16[256,256]{1,0:T(8,128)(2,1)}, u32[]{:S(2)}) copy-start(bf16[256,256]{1,0:T(8,128)(2,1)} %get-tuple-element.13) | copy-start | bytes 393220
  68.0 23.2 %collective-permute-start.4 = (bf16[256,2048]{1,0:T(8,128)(2,1)S(1)}, bf16[256,2048]{1,0:T(8,128)(2,1)S(1)}, u32[]{:S(2)}, u32[]{:S(2)}) collective-permute-start(bf16[256,2048]{1,0:T(8,128)(2,1)S(1)} %collective-permute-done.3), channel_id=1, source_target_pairs={{0,2},{4,6},{8,10},{12,14},{1,3},{5,7},{9,11},{13,15},{16,18},{20,... | collective-permute-start | bytes 3145736 | tf_op jit(solution)/shard_map/ppermute | solution.py:19
  74.7 20.2 %copy-start.7 = (bf16[512,2048]{1,0:T(8,128)(2,1)}, bf16[512,2048]{1,0:T(8,128)(2,1)S(1)}, u32[]{:S(2)}) copy-start(bf16[512,2048]{1,0:T(8,128)(2,1)S(1)} %convolution_convert_fusion.1) | copy-start | bytes 6291460
  93.3 1.7 copy-start.1
  100.3 0.7 copy-start.12
  116.3 2.4 %copy-start.2 = (bf16[512,2048]{1,0:T(8,128)(2,1)S(1)}, bf16[512,2048]{1,0:T(8,128)(2,1)}, u32[]{:S(2)}) copy-start(bf16[512,2048]{1,0:T(8,128)(2,1)} %copy-done.1) | copy-start | bytes 6291460
  116.4 2.4 %copy-start.4 = (bf16[512,2048]{1,0:T(8,128)(2,1)S(1)}, bf16[512,2048]{1,0:T(8,128)(2,1)}, u32[]{:S(2)}) copy-start(bf16[512,2048]{1,0:T(8,128)(2,1)} %copy-done.3) | copy-start | bytes 6291460
  116.4 2.9 %copy-start.6 = (bf16[512,2048]{1,0:T(8,128)(2,1)S(1)}, bf16[512,2048]{1,0:T(8,128)(2,1)}, u32[]{:S(2)}) copy-start(bf16[512,2048]{1,0:T(8,128)(2,1)} %copy-done.5) | copy-start | bytes 6291460
  116.4 3.5 %copy-start.8 = (bf16[512,2048]{1,0:T(8,128)(2,1)S(1)}, bf16[512,2048]{1,0:T(8,128)(2,1)}, u32[]{:S(2)}) copy-start(bf16[512,2048]{1,0:T(8,128)(2,1)} %copy-done.7) | copy-start | bytes 6291460
  124.3 4.6 %copy-start.11 = (bf16[256,256]{1,0:T(8,128)(2,1)S(1)}, bf16[256,256]{1,0:T(8,128)(2,1)}, u32[]{:S(2)}) copy-start(bf16[256,256]{1,0:T(8,128)(2,1)} %get-tuple-element.13) | copy-start | bytes 393220
Sparse Core Ops, SparseCore 0:
  100.5 87.3 reduce-scatter.1

commit v2 on v1

--- a/solution.py
+++ b/solution.py
@@ -6,6 +6,7 @@
 from jax.sharding import PartitionSpec as P
 
 LAG_BLOCKS = 4
+SEQ_AXES = ("row", "side")
 
 
 def from_behind(value, axis, steps):
@@ -22,14 +23,14 @@
 
 
 def gather_later(block):
-    side_zero = lax.axis_index("ctx") % 2 == 0
-    two_on = from_behind(block, "ctx", -2)
-    partner_own = swap_pairs(block, "ctx", 1)
-    four_on = from_behind(two_on, "ctx", -2)
+    side_zero = lax.axis_index(SEQ_AXES) % 2 == 0
+    two_on = from_behind(block, SEQ_AXES, -2)
+    partner_own = swap_pairs(block, SEQ_AXES, 1)
+    four_on = from_behind(two_on, SEQ_AXES, -2)
     partner_two_on = lax.ppermute(
-        two_on, "ctx", [(source, source ^ 1) for source in range(lax.axis_size("ctx"))]
-    )
-    partner_four_on = swap_pairs(four_on, "ctx", 0)
+        two_on, SEQ_AXES, [(source, source ^ 1) for source in range(lax.axis_size(SEQ_AXES))]
+    )
+    partner_four_on = swap_pairs(four_on, SEQ_AXES, 0)
     one_on = jnp.where(side_zero, partner_own, partner_two_on)
     three_on = jnp.where(side_zero, partner_two_on, partner_four_on)
     return [block, one_on, two_on, three_on, four_on]
@@ -165,19 +166,24 @@
                 preferred_element_type=jnp.float32,
             )
         )
-    grad_filter = lax.psum_scatter(
-        jnp.concatenate(grad_rows, axis=0).astype(jnp.bfloat16),
-        "ctx",
-        scatter_dimension=0,
-        tiled=True,
-    ).astype(jnp.float32)
+    row_count = lax.axis_size("row")
+    partial = jnp.concatenate(grad_rows, axis=0).astype(jnp.bfloat16)
+    share = partial.shape[0] // (row_count * 2)
+    staged = partial.reshape(row_count, 2, share, chan_width).transpose(1, 0, 2, 3)
+    by_side = lax.psum_scatter(staged, "side", scatter_dimension=0, tiled=True)
+    by_row = lax.psum_scatter(by_side, "row", scatter_dimension=1, tiled=True)
+    grad_filter = by_row.reshape(share, chan_width).astype(jnp.float32)
     return (grad_inputs, grad_filter)
 
 
 def solution(mesh):
+    groups, blocks, cores = mesh.devices.shape
+    mesh = jax.sharding.Mesh(
+        mesh.devices.reshape(groups, blocks // 2, 2, cores), ("grp", "row", "side", "ch")
+    )
     placed = (
-        P(("grp", "ctx"), "ch"),
-        P(("grp", "ctx"), "ch"),
+        P(("grp", "row", "side"), "ch"),
+        P(("grp", "row", "side"), "ch"),
         P(),
         P(),
         P(),
@@ -189,6 +195,6 @@
         on_device,
         mesh=mesh,
         in_specs=placed,
-        out_specs=(P(("grp", "ctx"), "ch"), P(("grp", "ctx"), "ch")),
+        out_specs=(P(("grp", "row", "side"), "ch"), P(("grp", "row", "side"), "ch")),
         check_vma=False,
     )

time: 197 us -> 210 us (1.066)
  waiting for transfers between devices: 116 us -> 129 us
    reduce_scatter x1 -> x2, waiting for transfers between devices: 57.3 us -> 70.6 us  [the longest x1 53.9 us: on_device(): by_side = lax.psum_scatter(staged, 'side', scatter_dimension=0, tiled=True)]
    convert_element_type x0 -> x1, local copies, waits for them, and re-layouts: none -> 2.26 us  [on_device(): partial = jnp.concatenate(grad_rows, axis=0).astype(jnp.bfloat16)]
  transfers between devices with their start and end apart: 6 -> 7, of which waited for: 5 -> 6; matrix products, arithmetic and copies ran while one was open for 22% -> 21% of each run, Pallas kernels for 0% -> 0%
where the time goes in v2:
time: 210 us
  waiting for transfers between devices  129 us (61%)
  matrix products  31.2 us (15%)
  other arithmetic  22.3 us (11%)
  between operations  14.5 us (7%)
  starting transfers between devices  8.57 us (4%)
  local copies, waits for them, and re-layouts  4.41 us (2%)
    reduce_scatter x1, waiting for transfers between devices, on_device(): by_side = lax.psum_scatter(staged, 'side', scatter_dimension=0, tiled=True)  53.9 us
    ppermute x2, waiting for transfers between devices, from_behind(): lax.ppermute(value, axis, [(source, source + steps) for source in range(l...  27.9 us
    reduce_scatter x1, waiting for transfers between devices, on_device(): by_row = lax.psum_scatter(by_side, 'row', scatter_dimension=1, tiled=True)  16.6 us
    ppermute x2, waiting for transfers between devices, swap_pairs(): lax.ppermute(value, axis, [(source, source ^ 1) for source in range(from_...  16.5 us
    ppermute x1, waiting for transfers between devices, gather_later(): lax.ppermute(two_on, SEQ_AXES, [(source, source ^ 1) for source in range(...  14 us
    dot_general x6, matrix products, slab_spectrum(): jnp.dot(jnp.concatenate([fwd_re, fwd_im], axis=0), slab_data, preferred_e...  9.31 us
    dot_general x1, matrix products, filter_taps(): jnp.dot(second_act, w_out, precision=lax.Precision.HIGHEST, preferred_ele...  8.74 us
    another operation x4, other arithmetic  6.59 us
  transfers between devices with their start and end apart: 7, of which 6 were waited for; matrix products, arithmetic and copies ran while one was open for 21% of the time, Pallas kernels for 0%

profile of v2, /device:TPU:0, one launch (start us, length us, event | category | flops | bytes accessed | tf_op | source)
XLA Modules:
  0.0 209.9 jit_solution(7804195587480347313)
XLA Ops:
  7.2 0.0 copy-start
  7.2 0.0 reduce-scatter.3.cloned.1.call-start
  7.2 1.4 collective-permute-start.1
  8.7 1.3 collective-permute-start
  10.0 1.8 multiply_convert_fusion.1
  11.8 23.9 %collective-permute-done.1 = bf16[256,2048]{1,0:T(8,128)(2,1)} collective-permute-done((bf16[256,2048]{1,0:T(8,128)(2,1)}, bf16[256,2048]{1,0:T(8,128)(2,1)}, u32[]{:S(2)}, u32[]{:S(2)}) %collective-permute-start.1) | collective-permute-done | bytes 1048608 | tf_op jit(solution)/shard_map/ppermute | solution.py:15
  35.8 1.7 collective-permute-start.2
  37.4 1.0 select_convert_fusion
  38.5 1.0 fusion.78
  39.5 1.9 convolution_convert_fusion.5
  41.4 0.0 copy-done
  41.4 0.0 copy-start.5
  41.5 0.7 convolution_convert_fusion
  42.2 1.3 collective-permute-start.3
  43.5 1.9 convolution_convert_fusion.3
  45.4 0.0 copy-start.3
  45.4 0.0 collective-permute-done
  45.5 0.0 copy-start.9
  45.5 1.0 copy-done.9
  46.5 14.0 %collective-permute-done.2 = bf16[256,2048]{1,0:T(8,128)(2,1)} collective-permute-done((bf16[256,2048]{1,0:T(8,128)(2,1)}, bf16[256,2048]{1,0:T(8,128)(2,1)}, u32[]{:S(2)}, u32[]{:S(2)}) %collective-permute-start.2) | collective-permute-done | bytes 1048608 | tf_op jit(solution)/shard_map/ppermute | solution.py:30
  60.4 2.0 convolution_convert_fusion.4
  62.4 0.0 copy-start.10
  62.4 1.7 fusion.28
  64.1 4.0 %collective-permute-done.3 = bf16[256,2048]{1,0:T(8,128)(2,1)S(1)} collective-permute-done((bf16[256,2048]{1,0:T(8,128)(2,1)}, bf16[256,2048]{1,0:T(8,128)(2,1)S(1)}, u32[]{:S(2)}, u32[]{:S(2)}) %collective-permute-start.3) | collective-permute-done | bytes 1048608 | tf_op jit(solution)/shard_map/ppermute | solution.py:15
  68.0 2.8 %collective-permute-start.4 = (bf16[256,2048]{1,0:T(8,128)(2,1)S(1)}, bf16[256,2048]{1,0:T(8,128)(2,1)S(1)}, u32[]{:S(2)}, u32[]{:S(2)}) collective-permute-start(bf16[256,2048]{1,0:T(8,128)(2,1)S(1)} %collective-permute-done.3), channel_id=1, source_target_pairs={{0,2},{4,6},{8,10},{12,14},{1,3},{5,7},{9,11},{13,15},{16,18},{20,... | collective-permute-start | bytes 3145736 | tf_op jit(solution)/shard_map/ppermute | solution.py:20
  70.8 0.0 copy-done.10
  70.9 0.7 convolution_convert_fusion.8
  71.6 0.0 copy-done.5
  71.6 1.6 fusion.23
  73.3 0.7 convolution_convert_fusion.9
  74.0 0.7 convolution_convert_fusion.1
  74.7 0.0 copy-start.7
  74.7 16.5 %collective-permute-done.4 = bf16[256,2048]{1,0:T(8,128)(2,1)S(1)} collective-permute-done((bf16[256,2048]{1,0:T(8,128)(2,1)S(1)}, bf16[256,2048]{1,0:T(8,128)(2,1)S(1)}, u32[]{:S(2)}, u32[]{:S(2)}) %collective-permute-start.4) | collective-permute-done | bytes 1048608 | tf_op jit(solution)/shard_map/ppermute | solution.py:20
  91.2 2.0 convolution_convert_fusion.2
  93.3 0.0 copy-done.3
  93.3 0.0 copy-start.1
  93.3 1.6 fusion.33
  94.9 0.0 copy-done.7
  94.9 0.0 copy-done.1
  94.9 1.7 fusion.38
  96.6 0.7 convolution_convert_fusion.6
  97.3 0.7 convolution_convert_fusion.7
  98.0 0.4 pad_maximum_fusion
  98.5 2.3 %copy.13 = bf16[4,2,128,2048]{3,2,0,1:T(8,128)(2,1)} copy(bf16[4,2,128,2048]{3,2,1,0:T(8,128)(2,1)S(1)} %bitcast.80) | data formatting | bytes 8388608 | tf_op jit(solution)/shard_map/convert_element_type | solution.py:170
  100.7 0.0 reduce-scatter.3.cloned.1.call-update
  100.7 0.0 copy-start.12
  100.7 0.0 reduce-scatter.5.cloned.1.call-start
  100.8 53.9 %reduce-scatter.3.cloned.1.call-done = bf16[1,4,128,2048]{3,2,1,0:T(8,128)(2,1)} async-done(((bf16[2,4,128,2048]{3,2,1,0:T(8,128)(2,1)}), bf16[1,4,128,2048]{3,2,1,0:T(8,128)(2,1)}) %reduce-scatter.3.cloned.1.call-update) | async-done | bytes 2097168 | tf_op jit(solution)/shard_map/reduce_scatter | solution.py:173
  154.7 0.0 reduce-scatter.5.cloned.1.call-update
  154.7 0.0 copy-done.12
  154.8 0.3 fusion.86
  155.1 3.3 %fusion.59 = f32[1024,64]{1,0:T(8,128)S(1)} fusion(f32[33,64]{1,0:T(8,128)} %param.10, f32[64]{0:T(128)} %param.11, f32[64]{0:T(128)} %param.13, f32[1024,16]{0,1:T(8,128)S(1)} %get-tuple-element.11, f32[1024,16]{0,1:T(8,128)S(1)} %get-tuple-element.10, f32[1024,1]{0,1:T(1,128)S(1)} %convert_multiply_fusion.38), kind=kOutput, calls=%fused_computation.120 | convolution fusion | flops 26150912 | bytes 406272 | tf_op jit(solution)/shard_map/dot_general | solution.py:67
  158.4 2.9 %fusion.57 = f32[1024,64]{1,0:T(8,128)S(1)} fusion(f32[1024,64]{1,0:T(8,128)S(1)} %fusion.59, f32[64,64]{1,0:T(8,128)} %param.12, f32[64]{0:T(128)} %param.13), kind=kOutput, calls=%fused_computation.118 | convolution fusion | flops 50397184 | bytes 540928 | tf_op jit(solution)/shard_map/dot_general | solution.py:75
  161.3 8.7 %multiply_convert_fusion = bf16[1024,2048]{1,0:T(8,128)(2,1)S(1)} fusion(f32[1024,64]{1,0:T(8,128)S(1)} %fusion.57, f32[64,2048]{1,0:T(8,128)} %param.14, f32[1024]{0:T(1024)S(1)} %iota_convert_fusion, f32[2048]{0:T(1024)S(1)} %neg.7), kind=kOutput, calls=%fused_computation.1 | convolution fusion | flops 1616904192 | bytes 4993024 | tf_op jit(solution)/shard_map/dot_general | solution.py:79
  170.1 0.0 copy-start.2
  170.1 2.4 %convert_bitcast_fusion = bf16[4,512,2048]{2,1,0:T(8,128)(2,1)S(1)} fusion(bf16[4,256,2048]{2,1,0:T(8,128)(2,1)S(1)} %bitcast.81, bf16[256,256]{1,0:T(8,128)(2,1)S(1)} %select_convert_fusion, bf16[256,256]{1,0:T(8,128)(2,1)S(1)} %fusion.78), kind=kOutput, calls=%fused_computation | convolution fusion | flops 2152202240 | bytes 12845056 | tf_op jit(solution)/shard_map/fs,jsc->jfc/dot_general | solution.py:102
  172.5 0.4 copy-done.6
  173.0 0.6 copy-done.8
  173.6 4.4 %fusion.6 = bf16[256,2048]{1,0:T(8,128)(2,1)S(1)} fusion(f32[256]{0:T(256)S(1)} %compare_select_fusion, pred[256]{0:T(512)(128)(4,1)S(1)} %iota_compare_fusion, bf16[4,512,2048]{2,1,0:T(8,128)(2,1)S(1)} %convert_bitcast_fusion, bf16[512,2048]{1,0:T(8,128)(2,1)S(1)} %copy-done.8, bf16[512,2048]{1,0:T(8,128)(2,1)S(1)} %copy-done.6, ...), kind=kLoop, calls=%fused_computation.65 | loop fusion | flops 28311552 | bytes 19924224 | tf_op jit(solution)/shard_map/convert_element_type | solution.py:146
  178.0 0.0 copy-start.11
  178.0 4.6 %fusion.12 = bf16[256,2048]{1,0:T(8,128)(2,1)S(1)} fusion(f32[256]{0:T(256)S(1)} %compare_select_fusion, pred[256]{0:T(512)(128)(4,1)S(1)} %iota_compare_fusion, bf16[4,512,2048]{2,1,0:T(8,128)(2,1)S(1)} %convert_bitcast_fusion, bf16[512,2048]{1,0:T(8,128)(2,1)S(1)} %copy-done.8, bf16[512,2048]{1,0:T(8,128)(2,1)S(1)} %copy-done.6, ...), kind=kLoop, calls=%fused_computation.71 | loop fusion | flops 30408704 | bytes 19924224 | tf_op jit(solution)/shard_map/convert_element_type | solution.py:147
  182.6 1.7 convolution_convert_fusion.10
  184.3 16.6 %reduce-scatter.5.cloned.1.call-done = bf16[1,1,128,2048]{3,2,1,0:T(8,128)(2,1)} async-done(((bf16[1,4,128,2048]{3,2,1,0:T(8,128)(2,1)}), bf16[1,1,128,2048]{3,2,1,0:T(8,128)(2,1)}) %reduce-scatter.5.cloned.1.call-update) | async-done | bytes 524304 | tf_op jit(solution)/shard_map/reduce_scatter | solution.py:174
  200.9 2.1 %bitcast_convert_fusion = f32[128,2048]{1,0:T(8,128)} fusion(bf16[1,1,128,2048]{3,2,1,0:T(8,128)(2,1)} %reduce-scatter.5.cloned.1.call-done), kind=kLoop, calls=%fused_computation.133 | loop fusion | flops 262144 | bytes 1572864 | tf_op jit(solution)/shard_map/convert_element_type | solution.py:175
  (13 shorter events, 0.0 us)
Async XLA Ops:
  7.2 34.3 %copy-start = (bf16[256,2048]{1,0:T(8,128)(2,1)S(1)}, bf16[256,2048]{1,0:T(8,128)(2,1)}, u32[]{:S(2)}) copy-start(bf16[256,2048]{1,0:T(8,128)(2,1)} %param.8) | copy-start | bytes 3145732
  7.2 147.5 %reduce-scatter.3.cloned.1.call-start = ((), (), s32[]{:S(2)}) async-start(), calls=%async_computation.2 | async-start | bytes 6291456 | tf_op jit(solution)/shard_map/reduce_scatter | solution.py:173
  7.2 28.5 %collective-permute-start.1 = (bf16[256,2048]{1,0:T(8,128)(2,1)}, bf16[256,2048]{1,0:T(8,128)(2,1)}, u32[]{:S(2)}, u32[]{:S(2)}) collective-permute-start(bf16[256,2048]{1,0:T(8,128)(2,1)} %param.9), channel_id=1, source_target_pairs={{4,0},{6,2},{8,4},{10,6},{12,8},{14,10},{5,1},{7,3},{9,5},{11,7},{... | collective-permute-start | bytes 3145736 | tf_op jit(solution)/shard_map/ppermute | solution.py:15
  8.7 36.8 %collective-permute-start = (bf16[256,2048]{1,0:T(8,128)(2,1)}, bf16[256,2048]{1,0:T(8,128)(2,1)S(1)}, u32[]{:S(2)}, u32[]{:S(2)}) collective-permute-start(bf16[256,2048]{1,0:T(8,128)(2,1)} %param.9), channel_id=1, source_target_pairs={{2,0},{6,4},{10,8},{14,12},{3,1},{7,5},{11,9},{15,13},{18,16},{22,... | collective-permute-start | bytes 3145736 | tf_op jit(solution)/shard_map/ppermute | solution.py:20
  35.8 24.7 %collective-permute-start.2 = (bf16[256,2048]{1,0:T(8,128)(2,1)}, bf16[256,2048]{1,0:T(8,128)(2,1)}, u32[]{:S(2)}, u32[]{:S(2)}) collective-permute-start(bf16[256,2048]{1,0:T(8,128)(2,1)} %collective-permute-done.1), channel_id=1, source_target_pairs={{0,2},{2,0},{4,6},{6,4},{8,10},{10,8},{12,14},{14,12},{1,3},{3,1},... | collective-permute-start | bytes 3145736 | tf_op jit(solution)/shard_map/ppermute | solution.py:30
  41.4 30.1 %copy-start.5 = (bf16[512,2048]{1,0:T(8,128)(2,1)}, bf16[512,2048]{1,0:T(8,128)(2,1)S(1)}, u32[]{:S(2)}) copy-start(bf16[512,2048]{1,0:T(8,128)(2,1)S(1)} %convolution_convert_fusion.5) | copy-start | bytes 6291460
  42.2 25.9 %collective-permute-start.3 = (bf16[256,2048]{1,0:T(8,128)(2,1)}, bf16[256,2048]{1,0:T(8,128)(2,1)S(1)}, u32[]{:S(2)}, u32[]{:S(2)}) collective-permute-start(bf16[256,2048]{1,0:T(8,128)(2,1)} %collective-permute-done.1), channel_id=1, source_target_pairs={{4,0},{6,2},{8,4},{10,6},{12,8},{14,10},{5,1},{7,3},{9,5},{11,7},{... | collective-permute-start | bytes 3145736 | tf_op jit(solution)/shard_map/ppermute | solution.py:15
  45.4 47.8 %copy-start.3 = (bf16[512,2048]{1,0:T(8,128)(2,1)}, bf16[512,2048]{1,0:T(8,128)(2,1)S(1)}, u32[]{:S(2)}) copy-start(bf16[512,2048]{1,0:T(8,128)(2,1)S(1)} %convolution_convert_fusion.3) | copy-start | bytes 6291460
  45.5 1.0 copy-start.9
  62.4 8.4 %copy-start.10 = (bf16[256,256]{1,0:T(8,128)(2,1)S(1)}, bf16[256,256]{1,0:T(8,128)(2,1)}, u32[]{:S(2)}) copy-start(bf16[256,256]{1,0:T(8,128)(2,1)} %get-tuple-element.13) | copy-start | bytes 393220
  68.0 23.2 %collective-permute-start.4 = (bf16[256,2048]{1,0:T(8,128)(2,1)S(1)}, bf16[256,2048]{1,0:T(8,128)(2,1)S(1)}, u32[]{:S(2)}, u32[]{:S(2)}) collective-permute-start(bf16[256,2048]{1,0:T(8,128)(2,1)S(1)} %collective-permute-done.3), channel_id=1, source_target_pairs={{0,2},{4,6},{8,10},{12,14},{1,3},{5,7},{9,11},{13,15},{16,18},{20,... | collective-permute-start | bytes 3145736 | tf_op jit(solution)/shard_map/ppermute | solution.py:20
  74.7 20.2 %copy-start.7 = (bf16[512,2048]{1,0:T(8,128)(2,1)}, bf16[512,2048]{1,0:T(8,128)(2,1)S(1)}, u32[]{:S(2)}) copy-start(bf16[512,2048]{1,0:T(8,128)(2,1)S(1)} %convolution_convert_fusion.1) | copy-start | bytes 6291460
  93.3 1.7 copy-start.1
  100.7 54.0 %copy-start.12 = (f32[2048]{0:T(1024)S(1)}, f32[2048]{0:T(1024)}, u32[]{:S(2)}) copy-start(f32[2048]{0:T(1024)} %param.15) | copy-start | bytes 24580
  100.7 100.2 %reduce-scatter.5.cloned.1.call-start = ((), (), s32[]{:S(2)}) async-start(), calls=%async_computation.3 | async-start | bytes 2621440 | tf_op jit(solution)/shard_map/reduce_scatter | solution.py:174
  170.1 2.4 %copy-start.2 = (bf16[512,2048]{1,0:T(8,128)(2,1)S(1)}, bf16[512,2048]{1,0:T(8,128)(2,1)}, u32[]{:S(2)}) copy-start(bf16[512,2048]{1,0:T(8,128)(2,1)} %copy-done.1) | copy-start | bytes 6291460
  170.1 2.4 %copy-start.4 = (bf16[512,2048]{1,0:T(8,128)(2,1)S(1)}, bf16[512,2048]{1,0:T(8,128)(2,1)}, u32[]{:S(2)}) copy-start(bf16[512,2048]{1,0:T(8,128)(2,1)} %copy-done.3) | copy-start | bytes 6291460
  170.1 2.9 %copy-start.6 = (bf16[512,2048]{1,0:T(8,128)(2,1)S(1)}, bf16[512,2048]{1,0:T(8,128)(2,1)}, u32[]{:S(2)}) copy-start(bf16[512,2048]{1,0:T(8,128)(2,1)} %copy-done.5) | copy-start | bytes 6291460
  170.1 3.5 %copy-start.8 = (bf16[512,2048]{1,0:T(8,128)(2,1)S(1)}, bf16[512,2048]{1,0:T(8,128)(2,1)}, u32[]{:S(2)}) copy-start(bf16[512,2048]{1,0:T(8,128)(2,1)} %copy-done.7) | copy-start | bytes 6291460
  178.0 4.6 %copy-start.11 = (bf16[256,256]{1,0:T(8,128)(2,1)S(1)}, bf16[256,256]{1,0:T(8,128)(2,1)}, u32[]{:S(2)}) copy-start(bf16[256,256]{1,0:T(8,128)(2,1)} %get-tuple-element.13) | copy-start | bytes 393220
Sparse Core Ops, SparseCore 0:
  100.9 53.8 reduce-scatter.2
  157.1 43.7 reduce-scatter.4

commit v3 on v2

--- a/solution.py
+++ b/solution.py
@@ -15,11 +15,15 @@
     return lax.ppermute(value, axis, [(source, source + steps) for source in range(leading, last)])
 
 
-def swap_pairs(value, axis, from_side):
+def swap_pairs(value, axis, from_side, stride=2):
     count = lax.axis_size(axis)
     return lax.ppermute(
-        value, axis, [(source, source ^ 1) for source in range(from_side, count, 2)]
-    )
+        value, axis, [(source, source ^ 1) for source in range(from_side, count, stride)]
+    )
+
+
+def lag_rows_total(blocks):
+    return sum(block.shape[0] for block in blocks)
 
 
 def gather_later(block):
@@ -167,11 +171,19 @@
             )
         )
     row_count = lax.axis_size("row")
-    partial = jnp.concatenate(grad_rows, axis=0).astype(jnp.bfloat16)
-    share = partial.shape[0] // (row_count * 2)
-    staged = partial.reshape(row_count, 2, share, chan_width).transpose(1, 0, 2, 3)
-    by_side = lax.psum_scatter(staged, "side", scatter_dimension=0, tiled=True)
-    by_row = lax.psum_scatter(by_side, "row", scatter_dimension=1, tiled=True)
+    share = lag_rows_total(grad_rows) // (row_count * 2)
+    side_zero = lax.axis_index("side") == 0
+    parts = 2 if row_count % 2 == 0 else 1
+    reduced = []
+    for part in range(parts):
+        chosen = grad_rows[part * LAG_BLOCKS // parts : (part + 1) * LAG_BLOCKS // parts]
+        staged = jnp.concatenate(chosen, axis=0).reshape(-1, 2, share, chan_width)
+        mine = jnp.where(side_zero, staged[:, 0], staged[:, 1])
+        theirs = jnp.where(side_zero, staged[:, 1], staged[:, 0]).astype(jnp.bfloat16)
+        reduced.append(mine + swap_pairs(theirs, SEQ_AXES, 0, 1).astype(jnp.float32))
+    by_row = lax.psum_scatter(
+        jnp.concatenate(reduced, axis=0).astype(jnp.bfloat16), "row", scatter_dimension=0, tiled=True
+    )
     grad_filter = by_row.reshape(share, chan_width).astype(jnp.float32)
     return (grad_inputs, grad_filter)
 

time: 210 us -> 194 us (0.924)
  waiting for transfers between devices: 129 us -> 111 us
  other arithmetic: 22.3 us -> 25.9 us
    reduce_scatter x2 -> x1, waiting for transfers between devices: 70.6 us -> 17.4 us  [on_device(): lax.psum_scatter(jnp.concatenate(reduced, axis=0).astype(jnp.bfloat16), '...]
    ppermute x2 -> x4, waiting for transfers between devices: 16.5 us -> 54.5 us  [swap_pairs(): lax.ppermute(value, axis, [(source, source ^ 1) for source in range(from_...]
    ppermute x2, waiting for transfers between devices: 27.9 us -> 24.7 us  [from_behind(): lax.ppermute(value, axis, [(source, source + steps) for source in range(l...]
    convert_element_type x1 -> x0, local copies, waits for them, and re-layouts: 2.26 us -> none  [on_device(): partial = jnp.concatenate(grad_rows, axis=0).astype(jnp.bfloat16)]
    concatenate x1 -> x3, other arithmetic: 0.39 us -> 2.55 us  [the longest x1 1.57 us: on_device(): jnp.concatenate(reduced, axis=0).astype(jnp.bfloat16)]
    ppermute x2 -> x4, starting transfers between devices: 4.1 us -> 5.5 us  [swap_pairs(): lax.ppermute(value, axis, [(source, source ^ 1) for source in range(from_...]
    another operation x4 -> x6, other arithmetic: 6.59 us -> 7.71 us
  transfers between devices with their start and end apart: 7 -> 8, of which waited for: 6 -> 7; matrix products, arithmetic and copies ran while one was open for 21% -> 27% of each run, Pallas kernels for 0% -> 0%
where the time goes in v3:
time: 194 us; the launch traced here: 193 us
  waiting for transfers between devices  111 us (57%)
  matrix products  29.6 us (15%)
  other arithmetic  25.9 us (13%)
  between operations  14.5 us (7%)
  starting transfers between devices  9.93 us (5%)
  local copies, waits for them, and re-layouts  2.81 us (1%)
    ppermute x4, waiting for transfers between devices, swap_pairs(): lax.ppermute(value, axis, [(source, source ^ 1) for source in range(from_...  54.5 us
    ppermute x2, waiting for transfers between devices, from_behind(): lax.ppermute(value, axis, [(source, source + steps) for source in range(l...  24.7 us
    reduce_scatter x1, waiting for transfers between devices, on_device(): lax.psum_scatter(jnp.concatenate(reduced, axis=0).astype(jnp.bfloat16), '...  17.4 us
    ppermute x1, waiting for transfers between devices, gather_later(): lax.ppermute(two_on, SEQ_AXES, [(source, source ^ 1) for source in range(...  13.9 us
    dot_general x6, matrix products, slab_spectrum(): jnp.dot(jnp.concatenate([fwd_re, fwd_im], axis=0), slab_data, preferred_e...  9.29 us
    dot_general x1, matrix products, filter_taps(): jnp.dot(second_act, w_out, precision=lax.Precision.HIGHEST, preferred_ele...  8.74 us
    another operation x6, other arithmetic  7.71 us
    ppermute x4, starting transfers between devices, swap_pairs(): lax.ppermute(value, axis, [(source, source ^ 1) for source in range(from_...  5.5 us
  transfers between devices with their start and end apart: 8, of which 7 were waited for; matrix products, arithmetic and copies ran while one was open for 27% of the time, Pallas kernels for 0%

profile of v3, /device:TPU:0, one launch (start us, length us, event | category | flops | bytes accessed | tf_op | source)
XLA Modules:
  0.0 193.4 jit_solution(6851120948584368060)
XLA Ops:
  7.2 0.0 copy-start
  7.2 0.0 reduce-scatter.2.cloned.1.call-start
  7.2 1.4 collective-permute-start.1
  8.7 1.3 collective-permute-start
  10.0 1.8 multiply_convert_fusion.1
  11.8 23.9 %collective-permute-done.1 = bf16[256,2048]{1,0:T(8,128)(2,1)} collective-permute-done((bf16[256,2048]{1,0:T(8,128)(2,1)}, bf16[256,2048]{1,0:T(8,128)(2,1)}, u32[]{:S(2)}, u32[]{:S(2)}) %collective-permute-start.1) | collective-permute-done | bytes 1048608 | tf_op jit(solution)/shard_map/ppermute | solution.py:15
  35.8 1.7 collective-permute-start.2
  37.4 1.0 select_convert_fusion.2
  38.5 1.0 fusion.86
  39.5 2.0 %convolution_convert_fusion.5 = bf16[512,2048]{1,0:T(8,128)(2,1)S(1)} fusion(bf16[256,2048]{1,0:T(8,128)(2,1)} %param.9, bf16[256,256]{1,0:T(8,128)(2,1)S(1)} %select_convert_fusion.2, bf16[256,256]{1,0:T(8,128)(2,1)S(1)} %fusion.86), kind=kOutput, calls=%fused_computation.25 | convolution fusion | flops 538443776 | bytes 3407872 | tf_op jit(solution)/shard_map/dot_general | solution.py:98
  41.5 0.7 convolution_convert_fusion
  42.2 1.3 collective-permute-start.3
  43.5 2.0 %convolution_convert_fusion.3 = bf16[512,2048]{1,0:T(8,128)(2,1)S(1)} fusion(bf16[256,2048]{1,0:T(8,128)(2,1)} %collective-permute-done.1, bf16[256,256]{1,0:T(8,128)(2,1)S(1)} %select_convert_fusion.2, bf16[256,256]{1,0:T(8,128)(2,1)S(1)} %fusion.86), kind=kOutput, calls=%fused_computation.23 | convolution fusion | flops 538443776 | bytes 3407872 | tf_op jit(solution)/shard_map/dot_general | solution.py:98
  45.5 0.0 collective-permute-done
  45.5 0.0 copy-start.10
  45.5 1.0 copy-done.10
  46.5 13.9 %collective-permute-done.2 = bf16[256,2048]{1,0:T(8,128)(2,1)} collective-permute-done((bf16[256,2048]{1,0:T(8,128)(2,1)}, bf16[256,2048]{1,0:T(8,128)(2,1)}, u32[]{:S(2)}, u32[]{:S(2)}) %collective-permute-start.2) | collective-permute-done | bytes 1048608 | tf_op jit(solution)/shard_map/ppermute | solution.py:34
  60.4 2.0 %convolution_convert_fusion.4 = bf16[512,2048]{1,0:T(8,128)(2,1)S(1)} fusion(bf16[256,2048]{1,0:T(8,128)(2,1)} %copy-done.10, bf16[256,2048]{1,0:T(8,128)(2,1)} %collective-permute-done.2, pred[]{:T(512)S(6)} %eq.91, bf16[256,256]{1,0:T(8,128)(2,1)S(1)} %select_convert_fusion.2, bf16[256,256]{1,0:T(8,128)(2,1)S(1)} %fusion.86), kind=kOutput, calls=%fused_computation.24 | convolution fusion | flops 538968064 | bytes 4456449 | tf_op jit(solution)/shard_map/dot_general | solution.py:98
  62.4 0.0 copy-start.11
  62.4 1.7 fusion.28
  64.1 0.0 copy-done.11
  64.1 0.7 fusion.49
  64.9 1.7 fusion.23
  66.5 0.7 fusion.45
  67.3 0.8 collective-permute-done.3
  68.0 2.8 %collective-permute-start.4 = (bf16[256,2048]{1,0:T(8,128)(2,1)S(1)}, bf16[256,2048]{1,0:T(8,128)(2,1)S(1)}, u32[]{:S(2)}, u32[]{:S(2)}) collective-permute-start(bf16[256,2048]{1,0:T(8,128)(2,1)S(1)} %collective-permute-done.3), channel_id=1, source_target_pairs={{0,2},{4,6},{8,10},{12,14},{1,3},{5,7},{9,11},{13,15},{16,18},{20,... | collective-permute-start | bytes 3145736 | tf_op jit(solution)/shard_map/ppermute | solution.py:20
  70.9 0.5 pad_maximum_fusion
  71.4 0.2 fusion.66
  71.5 0.1 collective-permute-start.5
  71.6 0.7 convolution_convert_fusion.1
  72.3 0.0 copy-start.8
  72.4 21.8 %collective-permute-done.4 = bf16[256,2048]{1,0:T(8,128)(2,1)S(1)} collective-permute-done((bf16[256,2048]{1,0:T(8,128)(2,1)S(1)}, bf16[256,2048]{1,0:T(8,128)(2,1)S(1)}, u32[]{:S(2)}, u32[]{:S(2)}) %collective-permute-start.4) | collective-permute-done | bytes 1048608 | tf_op jit(solution)/shard_map/ppermute | solution.py:20
  94.2 2.0 %convolution_convert_fusion.2 = bf16[512,2048]{1,0:T(8,128)(2,1)S(1)} fusion(bf16[256,2048]{1,0:T(8,128)(2,1)} %collective-permute-done.2, bf16[256,2048]{1,0:T(8,128)(2,1)S(1)} %collective-permute-done.4, pred[]{:T(512)S(6)} %eq.91, bf16[256,256]{1,0:T(8,128)(2,1)S(1)} %select_convert_fusion.2, bf16[256,256]{1,0:T(8,128)(2,1)S(1)} %fusion.86), kind=kOutput, calls=%fused_computation.22 | convolution fusion | flops 538968064 | bytes 4456449 | tf_op jit(solution)/shard_map/dot_general | solution.py:98
  96.2 0.0 copy-done.4
  96.2 0.0 copy-start.2
  96.2 1.7 fusion.33
  97.9 1.6 fusion.38
  99.5 0.7 fusion.57
  100.3 0.7 fusion.53
  101.0 0.5 pad_maximum_fusion.1
  101.5 0.2 fusion.67
  101.7 1.3 collective-permute-start.6
  103.0 13.7 %collective-permute-done.5 = bf16[2,128,2048]{2,1,0:T(8,128)(2,1)S(1)} collective-permute-done((bf16[2,128,2048]{2,1,0:T(8,128)(2,1)S(1)}, bf16[2,128,2048]{2,1,0:T(8,128)(2,1)S(1)}, u32[]{:S(2)}, u32[]{:S(2)}) %collective-permute-start.5) | collective-permute-done | bytes 1048608 | tf_op jit(solution)/shard_map/ppermute | solution.py:20
  116.7 0.5 fusion.62
  117.2 19.0 %collective-permute-done.6 = bf16[2,128,2048]{2,1,0:T(8,128)(2,1)S(1)} collective-permute-done((bf16[2,128,2048]{2,1,0:T(8,128)(2,1)S(1)}, bf16[2,128,2048]{2,1,0:T(8,128)(2,1)S(1)}, u32[]{:S(2)}, u32[]{:S(2)}) %collective-permute-start.6) | collective-permute-done | bytes 1048608 | tf_op jit(solution)/shard_map/ppermute | solution.py:20
  136.2 0.5 fusion.61
  136.7 1.6 pad_maximum_fusion.2
  138.3 0.0 copy-start.13
  138.3 0.0 reduce-scatter.2.cloned.1.call-update
  138.4 0.6 copy-done.15
  139.0 0.3 fusion.94
  139.4 2.5 %fusion.65 = f32[1024,64]{1,0:T(8,128)S(1)} fusion(f32[33,64]{1,0:T(8,128)S(1)} %copy-done.14, f32[64]{0:T(128)S(1)} %copy-done.17, f32[64]{0:T(128)S(1)} %copy-done.16, f32[1024,16]{0,1:T(8,128)S(1)} %get-tuple-element.11, f32[1024,16]{0,1:T(8,128)S(1)} %get-tuple-element.10, f32[1024,1]{0,1:T(1,128)S(1)} %convert_multiply_fusion.38), kind=kOutput, calls=%fused_computation.131 | convolution fusion | flops 26150912 | bytes 406272 | tf_op jit(solution)/shard_map/dot_general | solution.py:71
  142.0 2.2 %fusion.63 = f32[1024,64]{1,0:T(8,128)S(1)} fusion(f32[1024,64]{1,0:T(8,128)S(1)} %fusion.65, f32[64,64]{1,0:T(8,128)S(1)} %copy-done.13, f32[64]{0:T(128)S(1)} %copy-done.16), kind=kOutput, calls=%fused_computation.129 | convolution fusion | flops 50397184 | bytes 540928 | tf_op jit(solution)/shard_map/dot_general | solution.py:79
  144.1 8.7 %multiply_convert_fusion = bf16[1024,2048]{1,0:T(8,128)(2,1)S(1)} fusion(f32[1024,64]{1,0:T(8,128)S(1)} %fusion.63, f32[64,2048]{1,0:T(8,128)} %param.14, f32[1024]{0:T(1024)S(1)} %iota_convert_fusion, f32[2048]{0:T(1024)S(1)} %neg.7), kind=kOutput, calls=%fused_computation.1 | convolution fusion | flops 1616904192 | bytes 4993024 | tf_op jit(solution)/shard_map/dot_general | solution.py:83
  152.9 2.4 %convert_bitcast_fusion = bf16[4,512,2048]{2,1,0:T(8,128)(2,1)S(1)} fusion(bf16[4,256,2048]{2,1,0:T(8,128)(2,1)S(1)} %bitcast.125, bf16[256,256]{1,0:T(8,128)(2,1)S(1)} %select_convert_fusion.2, bf16[256,256]{1,0:T(8,128)(2,1)S(1)} %fusion.86), kind=kOutput, calls=%fused_computation | convolution fusion | flops 2152202240 | bytes 12845056 | tf_op jit(solution)/shard_map/fs,jsc->jfc/dot_general | solution.py:106
  155.3 0.5 copy-done.7
  155.8 0.6 copy-done.9
  156.4 4.4 %fusion.6 = bf16[256,2048]{1,0:T(8,128)(2,1)S(1)} fusion(f32[256]{0:T(256)S(1)} %compare_select_fusion, pred[256]{0:T(512)(128)(4,1)S(1)} %iota_compare_fusion, bf16[4,512,2048]{2,1,0:T(8,128)(2,1)S(1)} %convert_bitcast_fusion, bf16[512,2048]{1,0:T(8,128)(2,1)S(1)} %copy-done.9, bf16[512,2048]{1,0:T(8,128)(2,1)S(1)} %copy-done.7, ...), kind=kLoop, calls=%fused_computation.61 | loop fusion | flops 28311552 | bytes 19924224 | tf_op jit(solution)/shard_map/convert_element_type | solution.py:150
  160.7 0.0 copy-start.12
  160.8 0.0 copy-start.1
  160.8 4.6 %fusion.12 = bf16[256,2048]{1,0:T(8,128)(2,1)S(1)} fusion(f32[256]{0:T(256)S(1)} %compare_select_fusion, pred[256]{0:T(512)(128)(4,1)S(1)} %iota_compare_fusion, bf16[4,512,2048]{2,1,0:T(8,128)(2,1)S(1)} %convert_bitcast_fusion, bf16[512,2048]{1,0:T(8,128)(2,1)S(1)} %copy-done.9, bf16[512,2048]{1,0:T(8,128)(2,1)S(1)} %copy-done.7, ...), kind=kLoop, calls=%fused_computation.67 | loop fusion | flops 30408704 | bytes 19924224 | tf_op jit(solution)/shard_map/convert_element_type | solution.py:151
  165.4 1.7 convolution_convert_fusion.6
  167.1 17.4 %reduce-scatter.2.cloned.1.call-done = bf16[1,128,2048]{2,1,0:T(8,128)(2,1)} async-done(((bf16[4,128,2048]{2,1,0:T(8,128)(2,1)}), bf16[1,128,2048]{2,1,0:T(8,128)(2,1)}) %reduce-scatter.2.cloned.1.call-update) | async-done | bytes 524304 | tf_op jit(solution)/shard_map/reduce_scatter | solution.py:184
  184.4 2.1 %bitcast_convert_fusion = f32[128,2048]{1,0:T(8,128)} fusion(bf16[1,128,2048]{2,1,0:T(8,128)(2,1)} %reduce-scatter.2.cloned.1.call-done), kind=kLoop, calls=%fused_computation.146 | loop fusion | flops 262144 | bytes 1572864 | tf_op jit(solution)/shard_map/convert_element_type | solution.py:187
  (29 shorter events, 0.1 us)
Async XLA Ops:
  7.2 34.3 %copy-start = (bf16[256,2048]{1,0:T(8,128)(2,1)S(1)}, bf16[256,2048]{1,0:T(8,128)(2,1)}, u32[]{:S(2)}) copy-start(bf16[256,2048]{1,0:T(8,128)(2,1)} %param.8) | copy-start | bytes 3145732
  7.2 177.3 %reduce-scatter.2.cloned.1.call-start = ((), (), s32[]{:S(2)}) async-start(), calls=%async_computation.1 | async-start | bytes 2621440 | tf_op jit(solution)/shard_map/reduce_scatter | solution.py:184
  7.2 28.5 %collective-permute-start.1 = (bf16[256,2048]{1,0:T(8,128)(2,1)}, bf16[256,2048]{1,0:T(8,128)(2,1)}, u32[]{:S(2)}, u32[]{:S(2)}) collective-permute-start(bf16[256,2048]{1,0:T(8,128)(2,1)} %param.9), channel_id=1, source_target_pairs={{4,0},{6,2},{8,4},{10,6},{12,8},{14,10},{5,1},{7,3},{9,5},{11,7},{... | collective-permute-start | bytes 3145736 | tf_op jit(solution)/shard_map/ppermute | solution.py:15
  8.7 36.8 %collective-permute-start = (bf16[256,2048]{1,0:T(8,128)(2,1)}, bf16[256,2048]{1,0:T(8,128)(2,1)S(1)}, u32[]{:S(2)}, u32[]{:S(2)}) collective-permute-start(bf16[256,2048]{1,0:T(8,128)(2,1)} %param.9), channel_id=1, source_target_pairs={{2,0},{6,4},{10,8},{14,12},{3,1},{7,5},{11,9},{15,13},{18,16},{22,... | collective-permute-start | bytes 3145736 | tf_op jit(solution)/shard_map/ppermute | solution.py:20
  35.8 24.7 %collective-permute-start.2 = (bf16[256,2048]{1,0:T(8,128)(2,1)}, bf16[256,2048]{1,0:T(8,128)(2,1)}, u32[]{:S(2)}, u32[]{:S(2)}) collective-permute-start(bf16[256,2048]{1,0:T(8,128)(2,1)} %collective-permute-done.1), channel_id=1, source_target_pairs={{0,2},{2,0},{4,6},{6,4},{8,10},{10,8},{12,14},{14,12},{1,3},{3,1},... | collective-permute-start | bytes 3145736 | tf_op jit(solution)/shard_map/ppermute | solution.py:34
  41.5 23.4 %copy-start.6 = (bf16[512,2048]{1,0:T(8,128)(2,1)}, bf16[512,2048]{1,0:T(8,128)(2,1)S(1)}, u32[]{:S(2)}) copy-start(bf16[512,2048]{1,0:T(8,128)(2,1)S(1)} %convolution_convert_fusion.5) | copy-start | bytes 6291460
  42.2 25.9 %collective-permute-start.3 = (bf16[256,2048]{1,0:T(8,128)(2,1)}, bf16[256,2048]{1,0:T(8,128)(2,1)S(1)}, u32[]{:S(2)}, u32[]{:S(2)}) collective-permute-start(bf16[256,2048]{1,0:T(8,128)(2,1)} %collective-permute-done.1), channel_id=1, source_target_pairs={{4,0},{6,2},{8,4},{10,6},{12,8},{14,10},{5,1},{7,3},{9,5},{11,7},{... | collective-permute-start | bytes 3145736 | tf_op jit(solution)/shard_map/ppermute | solution.py:15
  45.5 50.7 %copy-start.4 = (bf16[512,2048]{1,0:T(8,128)(2,1)}, bf16[512,2048]{1,0:T(8,128)(2,1)S(1)}, u32[]{:S(2)}) copy-start(bf16[512,2048]{1,0:T(8,128)(2,1)S(1)} %convolution_convert_fusion.3) | copy-start | bytes 6291460
  45.5 1.0 copy-start.10
  62.4 1.7 copy-start.11
  68.0 26.2 %collective-permute-start.4 = (bf16[256,2048]{1,0:T(8,128)(2,1)S(1)}, bf16[256,2048]{1,0:T(8,128)(2,1)S(1)}, u32[]{:S(2)}, u32[]{:S(2)}) collective-permute-start(bf16[256,2048]{1,0:T(8,128)(2,1)S(1)} %collective-permute-done.3), channel_id=1, source_target_pairs={{0,2},{4,6},{8,10},{12,14},{1,3},{5,7},{9,11},{13,15},{16,18},{20,... | collective-permute-start | bytes 3145736 | tf_op jit(solution)/shard_map/ppermute | solution.py:20
  71.5 45.1 %collective-permute-start.5 = (bf16[2,128,2048]{2,1,0:T(8,128)(2,1)S(1)}, bf16[2,128,2048]{2,1,0:T(8,128)(2,1)S(1)}, u32[]{:S(2)}, u32[]{:S(2)}) collective-permute-start(bf16[2,128,2048]{2,1,0:T(8,128)(2,1)S(1)} %fusion.66), channel_id=1, source_target_pairs={{0,2},{2,0},{4,6},{6,4},{8,10},{10,8},{12,14},{14,12},{1,3},{3,1},... | collective-permute-start | bytes 3145736 | tf_op jit(solution)/shard_map/ppermute | solution.py:20
  72.3 25.5 %copy-start.8 = (bf16[512,2048]{1,0:T(8,128)(2,1)}, bf16[512,2048]{1,0:T(8,128)(2,1)S(1)}, u32[]{:S(2)}) copy-start(bf16[512,2048]{1,0:T(8,128)(2,1)S(1)} %convolution_convert_fusion.1) | copy-start | bytes 6291460
  96.2 1.7 copy-start.2
  101.7 34.5 %collective-permute-start.6 = (bf16[2,128,2048]{2,1,0:T(8,128)(2,1)S(1)}, bf16[2,128,2048]{2,1,0:T(8,128)(2,1)S(1)}, u32[]{:S(2)}, u32[]{:S(2)}) collective-permute-start(bf16[2,128,2048]{2,1,0:T(8,128)(2,1)S(1)} %fusion.67), channel_id=1, source_target_pairs={{0,2},{2,0},{4,6},{6,4},{8,10},{10,8},{12,14},{14,12},{1,3},{3,1},... | collective-permute-start | bytes 3145736 | tf_op jit(solution)/shard_map/ppermute | solution.py:20
  138.3 0.7 copy-start.15
  138.3 1.1 copy-start.14
  138.3 1.1 copy-start.16
  138.3 1.1 copy-start.17
  138.3 3.6 %copy-start.13 = (f32[64,64]{1,0:T(8,128)S(1)}, f32[64,64]{1,0:T(8,128)}, u32[]{:S(2)}) copy-start(f32[64,64]{1,0:T(8,128)} %param.12) | copy-start | bytes 49156
  152.9 2.4 %copy-start.3 = (bf16[512,2048]{1,0:T(8,128)(2,1)S(1)}, bf16[512,2048]{1,0:T(8,128)(2,1)}, u32[]{:S(2)}) copy-start(bf16[512,2048]{1,0:T(8,128)(2,1)} %copy-done.2) | copy-start | bytes 6291460
  152.9 2.4 %copy-start.5 = (bf16[512,2048]{1,0:T(8,128)(2,1)S(1)}, bf16[512,2048]{1,0:T(8,128)(2,1)}, u32[]{:S(2)}) copy-start(bf16[512,2048]{1,0:T(8,128)(2,1)} %copy-done.4) | copy-start | bytes 6291460
  152.9 2.9 %copy-start.7 = (bf16[512,2048]{1,0:T(8,128)(2,1)S(1)}, bf16[512,2048]{1,0:T(8,128)(2,1)}, u32[]{:S(2)}) copy-start(bf16[512,2048]{1,0:T(8,128)(2,1)} %copy-done.6) | copy-start | bytes 6291460
  152.9 3.5 %copy-start.9 = (bf16[512,2048]{1,0:T(8,128)(2,1)S(1)}, bf16[512,2048]{1,0:T(8,128)(2,1)}, u32[]{:S(2)}) copy-start(bf16[512,2048]{1,0:T(8,128)(2,1)} %copy-done.8) | copy-start | bytes 6291460
  160.7 4.6 %copy-start.12 = (bf16[256,256]{1,0:T(8,128)(2,1)S(1)}, bf16[256,256]{1,0:T(8,128)(2,1)}, u32[]{:S(2)}) copy-start(bf16[256,256]{1,0:T(8,128)(2,1)} %get-tuple-element.13) | copy-start | bytes 393220
  160.8 25.8 %copy-start.1 = (bf16[256,2048]{1,0:T(8,128)(2,1)S(1)}, bf16[256,2048]{1,0:T(8,128)(2,1)}, u32[]{:S(2)}) copy-start(bf16[256,2048]{1,0:T(8,128)(2,1)} %param.8) | copy-start | bytes 3145732
Sparse Core Ops, SparseCore 0:
  138.5 45.9 reduce-scatter.1

commit v4 on v3

--- a/solution.py
+++ b/solution.py
@@ -34,7 +34,11 @@
     partner_two_on = lax.ppermute(
         two_on, SEQ_AXES, [(source, source ^ 1) for source in range(lax.axis_size(SEQ_AXES))]
     )
-    partner_four_on = swap_pairs(four_on, SEQ_AXES, 0)
+    partner_four_on = lax.ppermute(
+        partner_two_on,
+        SEQ_AXES,
+        [(source, source - 2) for source in range(3, lax.axis_size(SEQ_AXES), 2)],
+    )
     one_on = jnp.where(side_zero, partner_own, partner_two_on)
     three_on = jnp.where(side_zero, partner_two_on, partner_four_on)
     return [block, one_on, two_on, three_on, four_on]

time: 194 us -> 176 us (0.907)
  waiting for transfers between devices: 111 us -> 73.5 us
  starting transfers between devices: 9.93 us -> 28.2 us
    ppermute x4 -> x3, waiting for transfers between devices: 54.5 us -> 19.9 us  [swap_pairs(): lax.ppermute(value, axis, [(source, source ^ 1) for source in range(from_...]
    ppermute x4 -> x3, starting transfers between devices: 5.5 us -> 23 us  [swap_pairs(): lax.ppermute(value, axis, [(source, source ^ 1) for source in range(from_...]
  transfers between devices with their start and end apart: 8 -> 8, of which waited for: 7 -> 4; matrix products, arithmetic and copies ran while one was open for 27% -> 30% of each run, Pallas kernels for 0% -> 0%
where the time goes in v4:
time: 176 us
  waiting for transfers between devices  73.5 us (42%)
  matrix products  30.4 us (17%)
  starting transfers between devices  28.2 us (16%)
  other arithmetic  26.1 us (15%)
  between operations  14.5 us (8%)
  local copies, waits for them, and re-layouts  2.84 us (2%)
    ppermute x2, waiting for transfers between devices, from_behind(): lax.ppermute(value, axis, [(source, source + steps) for source in range(l...  23.9 us
    ppermute x3, starting transfers between devices, swap_pairs(): lax.ppermute(value, axis, [(source, source ^ 1) for source in range(from_...  23 us
    ppermute x3, waiting for transfers between devices, swap_pairs(): lax.ppermute(value, axis, [(source, source ^ 1) for source in range(from_...  19.9 us
    reduce_scatter x1, waiting for transfers between devices, on_device(): lax.psum_scatter(jnp.concatenate(reduced, axis=0).astype(jnp.bfloat16), '...  15.7 us
    ppermute x1, waiting for transfers between devices, gather_later(): lax.ppermute(two_on, SEQ_AXES, [(source, source ^ 1) for source in range(...  13.9 us
    dot_general x6, matrix products, slab_spectrum(): jnp.dot(jnp.concatenate([fwd_re, fwd_im], axis=0), slab_data, preferred_e...  10 us
    dot_general x1, matrix products, filter_taps(): jnp.dot(second_act, w_out, precision=lax.Precision.HIGHEST, preferred_ele...  8.79 us
    another operation x6, other arithmetic  7.91 us
  transfers between devices with their start and end apart: 8, of which 4 were waited for; matrix products, arithmetic and copies ran while one was open for 30% of the time, Pallas kernels for 0%

profile of v4, /device:TPU:0, one launch (start us, length us, event | category | flops | bytes accessed | tf_op | source)
XLA Modules:
  0.0 175.7 jit_solution(10404810012402386980)
XLA Ops:
  7.2 0.0 copy-start
  7.2 0.0 reduce-scatter.2.cloned.1.call-start
  7.2 1.4 collective-permute-start.1
  8.7 1.3 collective-permute-start
  10.0 1.8 %multiply_convert_fusion.1 = (bf16[256,256]{1,0:T(8,128)(2,1)S(1)}, bf16[256,256]{1,0:T(8,128)(2,1)}) fusion(f32[256]{0:T(256)S(1)} %compare_select_fusion, pred[256]{0:T(512)(128)(4,1)S(1)} %iota_compare_fusion, f32[256]{0:T(256)S(1)} %broadcast_select_fusion), kind=kLoop, calls=%fused_computation.157 | loop fusion | flops 1376256 | bytes 264448 | tf_op jit(solution)/shard_map/convert_element_type | solution.py:59
  11.8 23.9 %collective-permute-done.1 = bf16[256,2048]{1,0:T(8,128)(2,1)} collective-permute-done((bf16[256,2048]{1,0:T(8,128)(2,1)}, bf16[256,2048]{1,0:T(8,128)(2,1)}, u32[]{:S(2)}, u32[]{:S(2)}) %collective-permute-start.1) | collective-permute-done | bytes 1048608 | tf_op jit(solution)/shard_map/ppermute | solution.py:15
  35.8 1.7 collective-permute-start.2
  37.4 1.0 select_convert_fusion.2
  38.5 1.0 fusion.86
  39.5 2.0 %convolution_convert_fusion.5 = bf16[512,2048]{1,0:T(8,128)(2,1)S(1)} fusion(bf16[256,2048]{1,0:T(8,128)(2,1)} %param.9, bf16[256,256]{1,0:T(8,128)(2,1)S(1)} %select_convert_fusion.2, bf16[256,256]{1,0:T(8,128)(2,1)S(1)} %fusion.86), kind=kOutput, calls=%fused_computation.25 | convolution fusion | flops 538443776 | bytes 3407872 | tf_op jit(solution)/shard_map/dot_general | solution.py:102
  41.5 0.7 convolution_convert_fusion
  42.2 1.3 collective-permute-start.4
  43.5 2.0 %convolution_convert_fusion.3 = bf16[512,2048]{1,0:T(8,128)(2,1)S(1)} fusion(bf16[256,2048]{1,0:T(8,128)(2,1)} %collective-permute-done.1, bf16[256,256]{1,0:T(8,128)(2,1)S(1)} %select_convert_fusion.2, bf16[256,256]{1,0:T(8,128)(2,1)S(1)} %fusion.86), kind=kOutput, calls=%fused_computation.23 | convolution fusion | flops 538443776 | bytes 3407872 | tf_op jit(solution)/shard_map/dot_general | solution.py:102
  45.5 0.0 collective-permute-done
  45.5 0.0 copy-start.10
  45.5 1.0 copy-done.10
  46.5 13.9 %collective-permute-done.2 = bf16[256,2048]{1,0:T(8,128)(2,1)} collective-permute-done((bf16[256,2048]{1,0:T(8,128)(2,1)}, bf16[256,2048]{1,0:T(8,128)(2,1)}, u32[]{:S(2)}, u32[]{:S(2)}) %collective-permute-start.2) | collective-permute-done | bytes 1048608 | tf_op jit(solution)/shard_map/ppermute | solution.py:34
  60.4 2.0 %convolution_convert_fusion.4 = bf16[512,2048]{1,0:T(8,128)(2,1)S(1)} fusion(bf16[256,2048]{1,0:T(8,128)(2,1)} %copy-done.10, bf16[256,2048]{1,0:T(8,128)(2,1)} %collective-permute-done.2, pred[]{:T(512)S(6)} %eq.91, bf16[256,256]{1,0:T(8,128)(2,1)S(1)} %select_convert_fusion.2, bf16[256,256]{1,0:T(8,128)(2,1)S(1)} %fusion.86), kind=kOutput, calls=%fused_computation.24 | convolution fusion | flops 538968064 | bytes 4456449 | tf_op jit(solution)/shard_map/dot_general | solution.py:102
  62.4 1.7 fusion.28
  64.1 0.0 copy-done.6
  64.1 0.0 copy-start.11
  64.1 1.7 fusion.23
  65.8 0.7 fusion.49
  66.6 0.7 collective-permute-start.3
  67.3 0.7 fusion.45
  68.0 0.5 pad_maximum_fusion
  68.5 0.2 fusion.66
  68.7 2.0 %collective-permute-start.5 = (bf16[2,128,2048]{2,1,0:T(8,128)(2,1)S(1)}, bf16[2,128,2048]{2,1,0:T(8,128)(2,1)S(1)}, u32[]{:S(2)}, u32[]{:S(2)}) collective-permute-start(bf16[2,128,2048]{2,1,0:T(8,128)(2,1)S(1)} %fusion.66), channel_id=1, source_target_pairs={{0,2},{2,0},{4,6},{6,4},{8,10},{10,8},{12,14},{14,12},{1,3},{3,1},... | collective-permute-start | bytes 3145736 | tf_op jit(solution)/shard_map/ppermute | solution.py:20
  70.7 0.0 collective-permute-done.4
  70.7 0.7 convolution_convert_fusion.1
  71.4 0.0 collective-permute-done.3
  71.4 2.7 %convolution_convert_fusion.2 = bf16[512,2048]{1,0:T(8,128)(2,1)S(1)} fusion(bf16[256,2048]{1,0:T(8,128)(2,1)} %collective-permute-done.2, bf16[256,2048]{1,0:T(8,128)(2,1)S(1)} %collective-permute-done.3, pred[]{:T(512)S(6)} %eq.91, bf16[256,256]{1,0:T(8,128)(2,1)S(1)} %select_convert_fusion.2, bf16[256,256]{1,0:T(8,128)(2,1)S(1)} %fusion.86), kind=kOutput, calls=%fused_computation.22 | convolution fusion | flops 538968064 | bytes 4456449 | tf_op jit(solution)/shard_map/dot_general | solution.py:102
  74.2 1.8 %fusion.33 = (bf16[256,2048]{1,0:T(8,128)(2,1)S(1)}, bf16[256,2048]{1,0:T(8,128)(2,1)S(1)}) fusion(f32[256]{0:T(256)S(1)} %compare_select_fusion, pred[256]{0:T(512)(128)(4,1)S(1)} %iota_compare_fusion, bf16[512,2048]{1,0:T(8,128)(2,1)S(1)} %convolution_convert_fusion.2, bf16[512,2048]{1,0:T(8,128)(2,1)S(1)} %convolution_convert_fusion.3, ...), kind=kLoop, calls=%fused_computation.88 | loop fusion | flops 10485760 | bytes 8389888 | tf_op jit(solution)/shard_map/convert.13
  76.1 0.0 copy-done.8
  76.1 0.0 copy-done.2
  76.1 1.6 fusion.38
  77.7 0.7 fusion.57
  78.4 0.7 fusion.53
  79.2 0.5 pad_maximum_fusion.1
  79.7 0.2 fusion.67
  79.9 19.8 %collective-permute-start.6 = (bf16[2,128,2048]{2,1,0:T(8,128)(2,1)S(1)}, bf16[2,128,2048]{2,1,0:T(8,128)(2,1)S(1)}, u32[]{:S(2)}, u32[]{:S(2)}) collective-permute-start(bf16[2,128,2048]{2,1,0:T(8,128)(2,1)S(1)} %fusion.67), channel_id=1, source_target_pairs={{0,2},{2,0},{4,6},{6,4},{8,10},{10,8},{12,14},{14,12},{1,3},{3,1},... | collective-permute-start | bytes 3145736 | tf_op jit(solution)/shard_map/ppermute | solution.py:20
  99.6 0.0 collective-permute-done.5
  99.6 0.5 fusion.62
  100.1 19.9 %collective-permute-done.6 = bf16[2,128,2048]{2,1,0:T(8,128)(2,1)S(1)} collective-permute-done((bf16[2,128,2048]{2,1,0:T(8,128)(2,1)S(1)}, bf16[2,128,2048]{2,1,0:T(8,128)(2,1)S(1)}, u32[]{:S(2)}, u32[]{:S(2)}) %collective-permute-start.6) | collective-permute-done | bytes 1048608 | tf_op jit(solution)/shard_map/ppermute | solution.py:20
  120.1 0.5 fusion.61
  120.6 1.6 pad_maximum_fusion.2
  122.2 0.0 copy-start.13
  122.2 0.0 reduce-scatter.2.cloned.1.call-update
  122.2 0.6 copy-done.15
  122.9 0.3 fusion.94
  123.3 2.5 %fusion.65 = f32[1024,64]{1,0:T(8,128)S(1)} fusion(f32[33,64]{1,0:T(8,128)S(1)} %copy-done.14, f32[64]{0:T(128)S(1)} %copy-done.17, f32[64]{0:T(128)S(1)} %copy-done.16, f32[1024,16]{0,1:T(8,128)S(1)} %get-tuple-element.11, f32[1024,16]{0,1:T(8,128)S(1)} %get-tuple-element.10, f32[1024,1]{0,1:T(1,128)S(1)} %convert_multiply_fusion.38), kind=kOutput, calls=%fused_computation.131 | convolution fusion | flops 26150912 | bytes 406272 | tf_op jit(solution)/shard_map/dot_general | solution.py:75
  125.8 0.0 copy-done.13
  125.8 2.2 %fusion.63 = f32[1024,64]{1,0:T(8,128)S(1)} fusion(f32[1024,64]{1,0:T(8,128)S(1)} %fusion.65, f32[64,64]{1,0:T(8,128)S(1)} %copy-done.13, f32[64]{0:T(128)S(1)} %copy-done.16), kind=kOutput, calls=%fused_computation.129 | convolution fusion | flops 50397184 | bytes 540928 | tf_op jit(solution)/shard_map/dot_general | solution.py:83
  128.0 8.8 %multiply_convert_fusion = bf16[1024,2048]{1,0:T(8,128)(2,1)S(1)} fusion(f32[1024,64]{1,0:T(8,128)S(1)} %fusion.63, f32[64,2048]{1,0:T(8,128)} %param.14, f32[1024]{0:T(1024)S(1)} %iota_convert_fusion, f32[2048]{0:T(1024)S(1)} %neg.7), kind=kOutput, calls=%fused_computation.1 | convolution fusion | flops 1616904192 | bytes 4993024 | tf_op jit(solution)/shard_map/dot_general | solution.py:87
  136.8 2.4 %convert_bitcast_fusion = bf16[4,512,2048]{2,1,0:T(8,128)(2,1)S(1)} fusion(bf16[4,256,2048]{2,1,0:T(8,128)(2,1)S(1)} %bitcast.125, bf16[256,256]{1,0:T(8,128)(2,1)S(1)} %select_convert_fusion.2, bf16[256,256]{1,0:T(8,128)(2,1)S(1)} %fusion.86), kind=kOutput, calls=%fused_computation | convolution fusion | flops 2152202240 | bytes 12845056 | tf_op jit(solution)/shard_map/fs,jsc->jfc/dot_general | solution.py:110
  139.2 0.5 copy-done.7
  139.7 0.6 copy-done.9
  140.3 4.4 %fusion.6 = bf16[256,2048]{1,0:T(8,128)(2,1)S(1)} fusion(f32[256]{0:T(256)S(1)} %compare_select_fusion, pred[256]{0:T(512)(128)(4,1)S(1)} %iota_compare_fusion, bf16[4,512,2048]{2,1,0:T(8,128)(2,1)S(1)} %convert_bitcast_fusion, bf16[512,2048]{1,0:T(8,128)(2,1)S(1)} %copy-done.9, bf16[512,2048]{1,0:T(8,128)(2,1)S(1)} %copy-done.7, ...), kind=kLoop, calls=%fused_computation.61 | loop fusion | flops 28311552 | bytes 19924224 | tf_op jit(solution)/shard_map/convert_element_type | solution.py:154
  144.7 0.0 copy-start.12
  144.7 0.0 copy-start.1
  144.7 4.6 %fusion.12 = bf16[256,2048]{1,0:T(8,128)(2,1)S(1)} fusion(f32[256]{0:T(256)S(1)} %compare_select_fusion, pred[256]{0:T(512)(128)(4,1)S(1)} %iota_compare_fusion, bf16[4,512,2048]{2,1,0:T(8,128)(2,1)S(1)} %convert_bitcast_fusion, bf16[512,2048]{1,0:T(8,128)(2,1)S(1)} %copy-done.9, bf16[512,2048]{1,0:T(8,128)(2,1)S(1)} %copy-done.7, ...), kind=kLoop, calls=%fused_computation.67 | loop fusion | flops 30408704 | bytes 19924224 | tf_op jit(solution)/shard_map/convert_element_type | solution.py:155
  149.3 1.7 convolution_convert_fusion.6
  151.0 15.7 %reduce-scatter.2.cloned.1.call-done = bf16[1,128,2048]{2,1,0:T(8,128)(2,1)} async-done(((bf16[4,128,2048]{2,1,0:T(8,128)(2,1)}), bf16[1,128,2048]{2,1,0:T(8,128)(2,1)}) %reduce-scatter.2.cloned.1.call-update) | async-done | bytes 524304 | tf_op jit(solution)/shard_map/reduce_scatter | solution.py:188
  166.7 2.1 %bitcast_convert_fusion = f32[128,2048]{1,0:T(8,128)} fusion(bf16[1,128,2048]{2,1,0:T(8,128)(2,1)} %reduce-scatter.2.cloned.1.call-done), kind=kLoop, calls=%fused_computation.146 | loop fusion | flops 262144 | bytes 1572864 | tf_op jit(solution)/shard_map/convert_element_type | solution.py:191
  (29 shorter events, 0.1 us)
Async XLA Ops:
  7.2 34.3 %copy-start = (bf16[256,2048]{1,0:T(8,128)(2,1)S(1)}, bf16[256,2048]{1,0:T(8,128)(2,1)}, u32[]{:S(2)}) copy-start(bf16[256,2048]{1,0:T(8,128)(2,1)} %param.8) | copy-start | bytes 3145732
  7.2 159.5 %reduce-scatter.2.cloned.1.call-start = ((), (), s32[]{:S(2)}) async-start(), calls=%async_computation.1 | async-start | bytes 2621440 | tf_op jit(solution)/shard_map/reduce_scatter | solution.py:188
  7.2 28.5 %collective-permute-start.1 = (bf16[256,2048]{1,0:T(8,128)(2,1)}, bf16[256,2048]{1,0:T(8,128)(2,1)}, u32[]{:S(2)}, u32[]{:S(2)}) collective-permute-start(bf16[256,2048]{1,0:T(8,128)(2,1)} %param.9), channel_id=1, source_target_pairs={{4,0},{6,2},{8,4},{10,6},{12,8},{14,10},{5,1},{7,3},{9,5},{11,7},{... | collective-permute-start | bytes 3145736 | tf_op jit(solution)/shard_map/ppermute | solution.py:15
  8.7 36.8 %collective-permute-start = (bf16[256,2048]{1,0:T(8,128)(2,1)}, bf16[256,2048]{1,0:T(8,128)(2,1)S(1)}, u32[]{:S(2)}, u32[]{:S(2)}) collective-permute-start(bf16[256,2048]{1,0:T(8,128)(2,1)} %param.9), channel_id=1, source_target_pairs={{2,0},{6,4},{10,8},{14,12},{3,1},{7,5},{11,9},{15,13},{18,16},{22,... | collective-permute-start | bytes 3145736 | tf_op jit(solution)/shard_map/ppermute | solution.py:20
  35.8 24.7 %collective-permute-start.2 = (bf16[256,2048]{1,0:T(8,128)(2,1)}, bf16[256,2048]{1,0:T(8,128)(2,1)}, u32[]{:S(2)}, u32[]{:S(2)}) collective-permute-start(bf16[256,2048]{1,0:T(8,128)(2,1)} %collective-permute-done.1), channel_id=1, source_target_pairs={{0,2},{2,0},{4,6},{6,4},{8,10},{10,8},{12,14},{14,12},{1,3},{3,1},... | collective-permute-start | bytes 3145736 | tf_op jit(solution)/shard_map/ppermute | solution.py:34
  41.5 22.7 %copy-start.6 = (bf16[512,2048]{1,0:T(8,128)(2,1)}, bf16[512,2048]{1,0:T(8,128)(2,1)S(1)}, u32[]{:S(2)}) copy-start(bf16[512,2048]{1,0:T(8,128)(2,1)S(1)} %convolution_convert_fusion.5) | copy-start | bytes 6291460
  42.2 28.5 %collective-permute-start.4 = (bf16[256,2048]{1,0:T(8,128)(2,1)}, bf16[256,2048]{1,0:T(8,128)(2,1)S(1)}, u32[]{:S(2)}, u32[]{:S(2)}) collective-permute-start(bf16[256,2048]{1,0:T(8,128)(2,1)} %collective-permute-done.1), channel_id=1, source_target_pairs={{4,0},{6,2},{8,4},{10,6},{12,8},{14,10},{5,1},{7,3},{9,5},{11,7},{... | collective-permute-start | bytes 3145736 | tf_op jit(solution)/shard_map/ppermute | solution.py:15
  45.5 28.7 %copy-start.4 = (bf16[512,2048]{1,0:T(8,128)(2,1)}, bf16[512,2048]{1,0:T(8,128)(2,1)S(1)}, u32[]{:S(2)}) copy-start(bf16[512,2048]{1,0:T(8,128)(2,1)S(1)} %convolution_convert_fusion.3) | copy-start | bytes 6291460
  45.5 1.0 copy-start.10
  64.1 1.7 copy-start.11
  66.6 4.9 %collective-permute-start.3 = (bf16[256,2048]{1,0:T(8,128)(2,1)}, bf16[256,2048]{1,0:T(8,128)(2,1)S(1)}, u32[]{:S(2)}, u32[]{:S(2)}) collective-permute-start(bf16[256,2048]{1,0:T(8,128)(2,1)} %collective-permute-done.2), channel_id=1, source_target_pairs={{6,2},{10,6},{14,10},{7,3},{11,7},{15,11},{22,18},{26,22},{30,26},... | collective-permute-start | bytes 3145736 | tf_op jit(solution)/shard_map/ppermute | solution.py:37
  68.7 30.9 %collective-permute-start.5 = (bf16[2,128,2048]{2,1,0:T(8,128)(2,1)S(1)}, bf16[2,128,2048]{2,1,0:T(8,128)(2,1)S(1)}, u32[]{:S(2)}, u32[]{:S(2)}) collective-permute-start(bf16[2,128,2048]{2,1,0:T(8,128)(2,1)S(1)} %fusion.66), channel_id=1, source_target_pairs={{0,2},{2,0},{4,6},{6,4},{8,10},{10,8},{12,14},{14,12},{1,3},{3,1},... | collective-permute-start | bytes 3145736 | tf_op jit(solution)/shard_map/ppermute | solution.py:20
  71.4 4.6 %copy-start.8 = (bf16[512,2048]{1,0:T(8,128)(2,1)}, bf16[512,2048]{1,0:T(8,128)(2,1)S(1)}, u32[]{:S(2)}) copy-start(bf16[512,2048]{1,0:T(8,128)(2,1)S(1)} %convolution_convert_fusion.1) | copy-start | bytes 6291460
  74.2 1.9 %copy-start.2 = (bf16[512,2048]{1,0:T(8,128)(2,1)}, bf16[512,2048]{1,0:T(8,128)(2,1)S(1)}, u32[]{:S(2)}) copy-start(bf16[512,2048]{1,0:T(8,128)(2,1)S(1)} %convolution_convert_fusion.2) | copy-start | bytes 6291460
  79.9 40.2 %collective-permute-start.6 = (bf16[2,128,2048]{2,1,0:T(8,128)(2,1)S(1)}, bf16[2,128,2048]{2,1,0:T(8,128)(2,1)S(1)}, u32[]{:S(2)}, u32[]{:S(2)}) collective-permute-start(bf16[2,128,2048]{2,1,0:T(8,128)(2,1)S(1)} %fusion.67), channel_id=1, source_target_pairs={{0,2},{2,0},{4,6},{6,4},{8,10},{10,8},{12,14},{14,12},{1,3},{3,1},... | collective-permute-start | bytes 3145736 | tf_op jit(solution)/shard_map/ppermute | solution.py:20
  122.2 0.7 copy-start.15
  122.2 1.1 copy-start.14
  122.2 1.1 copy-start.16
  122.2 1.1 copy-start.17
  122.2 3.6 %copy-start.13 = (f32[64,64]{1,0:T(8,128)S(1)}, f32[64,64]{1,0:T(8,128)}, u32[]{:S(2)}) copy-start(f32[64,64]{1,0:T(8,128)} %param.12) | copy-start | bytes 49156
  136.8 2.4 %copy-start.3 = (bf16[512,2048]{1,0:T(8,128)(2,1)S(1)}, bf16[512,2048]{1,0:T(8,128)(2,1)}, u32[]{:S(2)}) copy-start(bf16[512,2048]{1,0:T(8,128)(2,1)} %copy-done.2) | copy-start | bytes 6291460
  136.8 2.4 %copy-start.5 = (bf16[512,2048]{1,0:T(8,128)(2,1)S(1)}, bf16[512,2048]{1,0:T(8,128)(2,1)}, u32[]{:S(2)}) copy-start(bf16[512,2048]{1,0:T(8,128)(2,1)} %copy-done.4) | copy-start | bytes 6291460
  136.8 2.9 %copy-start.7 = (bf16[512,2048]{1,0:T(8,128)(2,1)S(1)}, bf16[512,2048]{1,0:T(8,128)(2,1)}, u32[]{:S(2)}) copy-start(bf16[512,2048]{1,0:T(8,128)(2,1)} %copy-done.6) | copy-start | bytes 6291460
  136.8 3.5 %copy-start.9 = (bf16[512,2048]{1,0:T(8,128)(2,1)S(1)}, bf16[512,2048]{1,0:T(8,128)(2,1)}, u32[]{:S(2)}) copy-start(bf16[512,2048]{1,0:T(8,128)(2,1)} %copy-done.8) | copy-start | bytes 6291460
  144.7 4.6 %copy-start.12 = (bf16[256,256]{1,0:T(8,128)(2,1)S(1)}, bf16[256,256]{1,0:T(8,128)(2,1)}, u32[]{:S(2)}) copy-start(bf16[256,256]{1,0:T(8,128)(2,1)} %get-tuple-element.13) | copy-start | bytes 393220
  144.7 24.1 %copy-start.1 = (bf16[256,2048]{1,0:T(8,128)(2,1)S(1)}, bf16[256,2048]{1,0:T(8,128)(2,1)}, u32[]{:S(2)}) copy-start(bf16[256,2048]{1,0:T(8,128)(2,1)} %param.8) | copy-start | bytes 3145732
Sparse Core Ops, SparseCore 0:
  122.4 44.3 reduce-scatter.1

commit v5 on v4

--- a/solution.py
+++ b/solution.py
@@ -177,10 +177,10 @@
     row_count = lax.axis_size("row")
     share = lag_rows_total(grad_rows) // (row_count * 2)
     side_zero = lax.axis_index("side") == 0
-    parts = 2 if row_count % 2 == 0 else 1
+    bounds = [0, 1, 2, LAG_BLOCKS] if row_count % 4 == 0 else [0, LAG_BLOCKS]
     reduced = []
-    for part in range(parts):
-        chosen = grad_rows[part * LAG_BLOCKS // parts : (part + 1) * LAG_BLOCKS // parts]
+    for low, high in zip(bounds[:-1], bounds[1:]):
+        chosen = grad_rows[low:high]
         staged = jnp.concatenate(chosen, axis=0).reshape(-1, 2, share, chan_width)
         mine = jnp.where(side_zero, staged[:, 0], staged[:, 1])
         theirs = jnp.where(side_zero, staged[:, 1], staged[:, 0]).astype(jnp.bfloat16)

time: 176 us -> 188 us (1.068)
  waiting for transfers between devices: 73.5 us -> 86 us
    ppermute x3 -> x4, waiting for transfers between devices: 19.9 us -> 31.3 us  [swap_pairs(): lax.ppermute(value, axis, [(source, source ^ 1) for source in range(from_...]
    another operation x6 -> x7, other arithmetic: 7.91 us -> 7.5 us
    ppermute x3 -> x4, starting transfers between devices: 23 us -> 22.7 us  [swap_pairs(): lax.ppermute(value, axis, [(source, source ^ 1) for source in range(from_...]
  transfers between devices with their start and end apart: 8 -> 9, of which waited for: 4 -> 4; matrix products, arithmetic and copies ran while one was open for 30% -> 27% of each run, Pallas kernels for 0% -> 0%
where the time goes in v5:
time: 188 us; the launch traced here: 187 us
  waiting for transfers between devices  86 us (46%)
  matrix products  30.4 us (16%)
  starting transfers between devices  28.1 us (15%)
  other arithmetic  25.2 us (13%)
  between operations  14.6 us (8%)
  local copies, waits for them, and re-layouts  2.82 us (2%)
    ppermute x4, waiting for transfers between devices, swap_pairs(): lax.ppermute(value, axis, [(source, source ^ 1) for source in range(from_...  31.3 us
    ppermute x2, waiting for transfers between devices, from_behind(): lax.ppermute(value, axis, [(source, source + steps) for source in range(l...  23.9 us
    ppermute x4, starting transfers between devices, swap_pairs(): lax.ppermute(value, axis, [(source, source ^ 1) for source in range(from_...  22.7 us
    reduce_scatter x1, waiting for transfers between devices, on_device(): lax.psum_scatter(jnp.concatenate(reduced, axis=0).astype(jnp.bfloat16), '...  16.8 us
    ppermute x1, waiting for transfers between devices, gather_later(): lax.ppermute(two_on, SEQ_AXES, [(source, source ^ 1) for source in range(...  13.9 us
    dot_general x6, matrix products, slab_spectrum(): jnp.dot(jnp.concatenate([fwd_re, fwd_im], axis=0), slab_data, preferred_e...  10 us
    dot_general x1, matrix products, filter_taps(): jnp.dot(second_act, w_out, precision=lax.Precision.HIGHEST, preferred_ele...  8.74 us
    another operation x7, other arithmetic  7.5 us
  transfers between devices with their start and end apart: 9, of which 4 were waited for; matrix products, arithmetic and copies ran while one was open for 27% of the time, Pallas kernels for 0%

profile of v5, /device:TPU:0, one launch (start us, length us, event | category | flops | bytes accessed | tf_op | source)
XLA Modules:
  0.0 187.1 jit_solution(5623731745033331683)
XLA Ops:
  7.2 0.0 copy-start
  7.2 0.0 reduce-scatter.2.cloned.1.call-start
  7.2 1.4 collective-permute-start.1
  8.7 1.3 collective-permute-start
  10.0 1.8 multiply_convert_fusion.1
  11.8 23.9 %collective-permute-done.1 = bf16[256,2048]{1,0:T(8,128)(2,1)} collective-permute-done((bf16[256,2048]{1,0:T(8,128)(2,1)}, bf16[256,2048]{1,0:T(8,128)(2,1)}, u32[]{:S(2)}, u32[]{:S(2)}) %collective-permute-start.1) | collective-permute-done | bytes 1048608 | tf_op jit(solution)/shard_map/ppermute | solution.py:15
  35.8 1.7 collective-permute-start.2
  37.4 1.0 select_convert_fusion.3
  38.5 1.0 fusion.88
  39.5 2.0 %convolution_convert_fusion.5 = bf16[512,2048]{1,0:T(8,128)(2,1)S(1)} fusion(bf16[256,2048]{1,0:T(8,128)(2,1)} %param.9, bf16[256,256]{1,0:T(8,128)(2,1)S(1)} %select_convert_fusion.3, bf16[256,256]{1,0:T(8,128)(2,1)S(1)} %fusion.88), kind=kOutput, calls=%fused_computation.24 | convolution fusion | flops 538443776 | bytes 3407872 | tf_op jit(solution)/shard_map/dot_general | solution.py:102
  41.5 0.7 convolution_convert_fusion
  42.2 1.3 collective-permute-start.4
  43.5 2.0 %convolution_convert_fusion.3 = bf16[512,2048]{1,0:T(8,128)(2,1)S(1)} fusion(bf16[256,2048]{1,0:T(8,128)(2,1)} %collective-permute-done.1, bf16[256,256]{1,0:T(8,128)(2,1)S(1)} %select_convert_fusion.3, bf16[256,256]{1,0:T(8,128)(2,1)S(1)} %fusion.88), kind=kOutput, calls=%fused_computation.22 | convolution fusion | flops 538443776 | bytes 3407872 | tf_op jit(solution)/shard_map/dot_general | solution.py:102
  45.5 0.0 collective-permute-done
  45.5 0.0 copy-start.10
  45.5 1.0 copy-done.10
  46.5 13.9 %collective-permute-done.2 = bf16[256,2048]{1,0:T(8,128)(2,1)} collective-permute-done((bf16[256,2048]{1,0:T(8,128)(2,1)}, bf16[256,2048]{1,0:T(8,128)(2,1)}, u32[]{:S(2)}, u32[]{:S(2)}) %collective-permute-start.2) | collective-permute-done | bytes 1048608 | tf_op jit(solution)/shard_map/ppermute | solution.py:34
  60.4 2.0 %convolution_convert_fusion.4 = bf16[512,2048]{1,0:T(8,128)(2,1)S(1)} fusion(bf16[256,2048]{1,0:T(8,128)(2,1)} %copy-done.10, bf16[256,2048]{1,0:T(8,128)(2,1)} %collective-permute-done.2, pred[]{:T(512)S(6)} %eq.91, bf16[256,256]{1,0:T(8,128)(2,1)S(1)} %select_convert_fusion.3, bf16[256,256]{1,0:T(8,128)(2,1)S(1)} %fusion.88), kind=kOutput, calls=%fused_computation.23 | convolution fusion | flops 538968064 | bytes 4456449 | tf_op jit(solution)/shard_map/dot_general | solution.py:102
  62.4 0.0 copy-start.11
  62.4 1.7 fusion.28
  64.1 0.7 fusion.49
  64.8 0.1 fusion.73
  64.9 1.4 collective-permute-start.6
  66.3 0.9 collective-permute-start.3
  67.3 1.6 fusion.23
  68.9 0.7 fusion.45
  69.6 0.0 collective-permute-done.4
  69.6 0.7 convolution_convert_fusion.1
  70.4 0.0 collective-permute-done.3
  70.4 2.7 %convolution_convert_fusion.2 = bf16[512,2048]{1,0:T(8,128)(2,1)S(1)} fusion(bf16[256,2048]{1,0:T(8,128)(2,1)} %collective-permute-done.2, bf16[256,2048]{1,0:T(8,128)(2,1)S(1)} %collective-permute-done.3, pred[]{:T(512)S(6)} %eq.91, bf16[256,256]{1,0:T(8,128)(2,1)S(1)} %select_convert_fusion.3, bf16[256,256]{1,0:T(8,128)(2,1)S(1)} %fusion.88), kind=kOutput, calls=%fused_computation.21 | convolution fusion | flops 538968064 | bytes 4456449 | tf_op jit(solution)/shard_map/dot_general | solution.py:102
  73.1 0.0 copy-done.4
  73.1 1.6 fusion.33
  74.8 1.6 fusion.38
  76.5 0.7 fusion.57
  77.2 0.7 fusion.53
  77.9 0.5 pad_maximum_fusion
  78.4 0.2 fusion.65
  78.6 19.9 %collective-permute-start.7 = (bf16[2,128,2048]{2,1,0:T(8,128)(2,1)S(1)}, bf16[2,128,2048]{2,1,0:T(8,128)(2,1)S(1)}, u32[]{:S(2)}, u32[]{:S(2)}) collective-permute-start(bf16[2,128,2048]{2,1,0:T(8,128)(2,1)S(1)} %fusion.65), channel_id=1, source_target_pairs={{0,2},{2,0},{4,6},{6,4},{8,10},{10,8},{12,14},{14,12},{1,3},{3,1},... | collective-permute-start | bytes 3145736 | tf_op jit(solution)/shard_map/ppermute | solution.py:20
  98.5 0.1 fusion.72
  98.6 0.1 collective-permute-start.5
  98.7 0.0 collective-permute-done.6
  98.7 0.2 fusion.66
  98.9 31.3 %collective-permute-done.5 = bf16[1,128,2048]{2,1,0:T(8,128)(2,1)S(1)} collective-permute-done((bf16[1,128,2048]{2,1,0:T(8,128)(2,1)S(1)}, bf16[1,128,2048]{2,1,0:T(8,128)(2,1)S(1)}, u32[]{:S(2)}, u32[]{:S(2)}) %collective-permute-start.5) | collective-permute-done | bytes 524320 | tf_op jit(solution)/shard_map/ppermute | solution.py:20
  130.2 0.2 fusion.67
  130.4 0.0 collective-permute-done.7
  130.4 0.5 fusion.61
  131.0 1.6 pad_maximum_fusion.1
  132.6 0.0 copy-start.13
  132.6 0.0 reduce-scatter.2.cloned.1.call-update
  132.6 0.6 copy-done.15
  133.3 0.3 fusion.96
  133.7 2.5 %fusion.64 = f32[1024,64]{1,0:T(8,128)S(1)} fusion(f32[33,64]{1,0:T(8,128)S(1)} %copy-done.14, f32[64]{0:T(128)S(1)} %copy-done.17, f32[64]{0:T(128)S(1)} %copy-done.16, f32[1024,16]{0,1:T(8,128)S(1)} %get-tuple-element.11, f32[1024,16]{0,1:T(8,128)S(1)} %get-tuple-element.10, f32[1024,1]{0,1:T(1,128)S(1)} %convert_multiply_fusion.38), kind=kOutput, calls=%fused_computation.125 | convolution fusion | flops 26150912 | bytes 406272 | tf_op jit(solution)/shard_map/dot_general | solution.py:75
  136.2 2.2 %fusion.62 = f32[1024,64]{1,0:T(8,128)S(1)} fusion(f32[1024,64]{1,0:T(8,128)S(1)} %fusion.64, f32[64,64]{1,0:T(8,128)S(1)} %copy-done.13, f32[64]{0:T(128)S(1)} %copy-done.16), kind=kOutput, calls=%fused_computation.123 | convolution fusion | flops 50397184 | bytes 540928 | tf_op jit(solution)/shard_map/dot_general | solution.py:83
  138.4 8.7 %multiply_convert_fusion = bf16[1024,2048]{1,0:T(8,128)(2,1)S(1)} fusion(f32[1024,64]{1,0:T(8,128)S(1)} %fusion.62, f32[64,2048]{1,0:T(8,128)} %param.14, f32[1024]{0:T(1024)S(1)} %iota_convert_fusion, f32[2048]{0:T(1024)S(1)} %neg.7), kind=kOutput, calls=%fused_computation.1 | convolution fusion | flops 1616904192 | bytes 4993024 | tf_op jit(solution)/shard_map/dot_general | solution.py:87
  147.2 2.4 %convert_bitcast_fusion = bf16[4,512,2048]{2,1,0:T(8,128)(2,1)S(1)} fusion(bf16[4,256,2048]{2,1,0:T(8,128)(2,1)S(1)} %bitcast.114, bf16[256,256]{1,0:T(8,128)(2,1)S(1)} %select_convert_fusion.3, bf16[256,256]{1,0:T(8,128)(2,1)S(1)} %fusion.88), kind=kOutput, calls=%fused_computation | convolution fusion | flops 2152202240 | bytes 12845056 | tf_op jit(solution)/shard_map/fs,jsc->jfc/dot_general | solution.py:110
  149.6 0.4 copy-done.7
  150.0 0.6 copy-done.9
  150.7 4.4 %fusion.6 = bf16[256,2048]{1,0:T(8,128)(2,1)S(1)} fusion(f32[256]{0:T(256)S(1)} %compare_select_fusion, pred[256]{0:T(512)(128)(4,1)S(1)} %iota_compare_fusion, bf16[4,512,2048]{2,1,0:T(8,128)(2,1)S(1)} %convert_bitcast_fusion, bf16[512,2048]{1,0:T(8,128)(2,1)S(1)} %copy-done.9, bf16[512,2048]{1,0:T(8,128)(2,1)S(1)} %copy-done.7, ...), kind=kLoop, calls=%fused_computation.60 | loop fusion | flops 28311552 | bytes 19924224 | tf_op jit(solution)/shard_map/convert_element_type | solution.py:154
  155.0 0.0 copy-start.12
  155.0 0.0 copy-start.1
  155.1 4.6 %fusion.12 = bf16[256,2048]{1,0:T(8,128)(2,1)S(1)} fusion(f32[256]{0:T(256)S(1)} %compare_select_fusion, pred[256]{0:T(512)(128)(4,1)S(1)} %iota_compare_fusion, bf16[4,512,2048]{2,1,0:T(8,128)(2,1)S(1)} %convert_bitcast_fusion, bf16[512,2048]{1,0:T(8,128)(2,1)S(1)} %copy-done.9, bf16[512,2048]{1,0:T(8,128)(2,1)S(1)} %copy-done.7, ...), kind=kLoop, calls=%fused_computation.66 | loop fusion | flops 30408704 | bytes 19924224 | tf_op jit(solution)/shard_map/convert_element_type | solution.py:155
  159.7 1.7 convolution_convert_fusion.6
  161.4 16.8 %reduce-scatter.2.cloned.1.call-done = bf16[1,128,2048]{2,1,0:T(8,128)(2,1)} async-done(((bf16[4,128,2048]{2,1,0:T(8,128)(2,1)}), bf16[1,128,2048]{2,1,0:T(8,128)(2,1)}) %reduce-scatter.2.cloned.1.call-update) | async-done | bytes 524304 | tf_op jit(solution)/shard_map/reduce_scatter | solution.py:188
  178.1 2.1 %bitcast_convert_fusion = f32[128,2048]{1,0:T(8,128)} fusion(bf16[1,128,2048]{2,1,0:T(8,128)(2,1)} %reduce-scatter.2.cloned.1.call-done), kind=kLoop, calls=%fused_computation.147 | loop fusion | flops 262144 | bytes 1572864 | tf_op jit(solution)/shard_map/convert_element_type | solution.py:191
  (32 shorter events, 0.1 us)
Async XLA Ops:
  7.2 34.3 %copy-start = (bf16[256,2048]{1,0:T(8,128)(2,1)S(1)}, bf16[256,2048]{1,0:T(8,128)(2,1)}, u32[]{:S(2)}) copy-start(bf16[256,2048]{1,0:T(8,128)(2,1)} %param.8) | copy-start | bytes 3145732
  7.2 170.9 %reduce-scatter.2.cloned.1.call-start = ((), (), s32[]{:S(2)}) async-start(), calls=%async_computation.1 | async-start | bytes 2621440 | tf_op jit(solution)/shard_map/reduce_scatter | solution.py:188
  7.2 28.5 %collective-permute-start.1 = (bf16[256,2048]{1,0:T(8,128)(2,1)}, bf16[256,2048]{1,0:T(8,128)(2,1)}, u32[]{:S(2)}, u32[]{:S(2)}) collective-permute-start(bf16[256,2048]{1,0:T(8,128)(2,1)} %param.9), channel_id=1, source_target_pairs={{4,0},{6,2},{8,4},{10,6},{12,8},{14,10},{5,1},{7,3},{9,5},{11,7},{... | collective-permute-start | bytes 3145736 | tf_op jit(solution)/shard_map/ppermute | solution.py:15
  8.7 36.8 %collective-permute-start = (bf16[256,2048]{1,0:T(8,128)(2,1)}, bf16[256,2048]{1,0:T(8,128)(2,1)S(1)}, u32[]{:S(2)}, u32[]{:S(2)}) collective-permute-start(bf16[256,2048]{1,0:T(8,128)(2,1)} %param.9), channel_id=1, source_target_pairs={{2,0},{6,4},{10,8},{14,12},{3,1},{7,5},{11,9},{15,13},{18,16},{22,... | collective-permute-start | bytes 3145736 | tf_op jit(solution)/shard_map/ppermute | solution.py:20
  35.8 24.7 %collective-permute-start.2 = (bf16[256,2048]{1,0:T(8,128)(2,1)}, bf16[256,2048]{1,0:T(8,128)(2,1)}, u32[]{:S(2)}, u32[]{:S(2)}) collective-permute-start(bf16[256,2048]{1,0:T(8,128)(2,1)} %collective-permute-done.1), channel_id=1, source_target_pairs={{0,2},{2,0},{4,6},{6,4},{8,10},{10,8},{12,14},{14,12},{1,3},{3,1},... | collective-permute-start | bytes 3145736 | tf_op jit(solution)/shard_map/ppermute | solution.py:34
  41.5 25.8 %copy-start.6 = (bf16[512,2048]{1,0:T(8,128)(2,1)}, bf16[512,2048]{1,0:T(8,128)(2,1)S(1)}, u32[]{:S(2)}) copy-start(bf16[512,2048]{1,0:T(8,128)(2,1)S(1)} %convolution_convert_fusion.5) | copy-start | bytes 6291460
  42.2 27.4 %collective-permute-start.4 = (bf16[256,2048]{1,0:T(8,128)(2,1)}, bf16[256,2048]{1,0:T(8,128)(2,1)S(1)}, u32[]{:S(2)}, u32[]{:S(2)}) collective-permute-start(bf16[256,2048]{1,0:T(8,128)(2,1)} %collective-permute-done.1), channel_id=1, source_target_pairs={{4,0},{6,2},{8,4},{10,6},{12,8},{14,10},{5,1},{7,3},{9,5},{11,7},{... | collective-permute-start | bytes 3145736 | tf_op jit(solution)/shard_map/ppermute | solution.py:15
  45.5 27.7 %copy-start.4 = (bf16[512,2048]{1,0:T(8,128)(2,1)}, bf16[512,2048]{1,0:T(8,128)(2,1)S(1)}, u32[]{:S(2)}) copy-start(bf16[512,2048]{1,0:T(8,128)(2,1)S(1)} %convolution_convert_fusion.3) | copy-start | bytes 6291460
  45.5 1.0 copy-start.10
  62.4 1.7 copy-start.11
  64.9 33.8 %collective-permute-start.6 = (bf16[1,128,2048]{2,1,0:T(8,128)(2,1)S(1)}, bf16[1,128,2048]{2,1,0:T(8,128)(2,1)S(1)}, u32[]{:S(2)}, u32[]{:S(2)}) collective-permute-start(bf16[1,128,2048]{2,1,0:T(8,128)(2,1)S(1)} %fusion.73), channel_id=1, source_target_pairs={{0,2},{2,0},{4,6},{6,4},{8,10},{10,8},{12,14},{14,12},{1,3},{3,1},... | collective-permute-start | bytes 1572872 | tf_op jit(solution)/shard_map/ppermute | solution.py:20
  66.3 4.0 %collective-permute-start.3 = (bf16[256,2048]{1,0:T(8,128)(2,1)}, bf16[256,2048]{1,0:T(8,128)(2,1)S(1)}, u32[]{:S(2)}, u32[]{:S(2)}) collective-permute-start(bf16[256,2048]{1,0:T(8,128)(2,1)} %collective-permute-done.2), channel_id=1, source_target_pairs={{6,2},{10,6},{14,10},{7,3},{11,7},{15,11},{22,18},{26,22},{30,26},... | collective-permute-start | bytes 3145736 | tf_op jit(solution)/shard_map/ppermute | solution.py:37
  70.4 4.4 %copy-start.8 = (bf16[512,2048]{1,0:T(8,128)(2,1)}, bf16[512,2048]{1,0:T(8,128)(2,1)S(1)}, u32[]{:S(2)}) copy-start(bf16[512,2048]{1,0:T(8,128)(2,1)S(1)} %convolution_convert_fusion.1) | copy-start | bytes 6291460
  73.1 1.7 copy-start.2
  78.6 51.9 %collective-permute-start.7 = (bf16[2,128,2048]{2,1,0:T(8,128)(2,1)S(1)}, bf16[2,128,2048]{2,1,0:T(8,128)(2,1)S(1)}, u32[]{:S(2)}, u32[]{:S(2)}) collective-permute-start(bf16[2,128,2048]{2,1,0:T(8,128)(2,1)S(1)} %fusion.65), channel_id=1, source_target_pairs={{0,2},{2,0},{4,6},{6,4},{8,10},{10,8},{12,14},{14,12},{1,3},{3,1},... | collective-permute-start | bytes 3145736 | tf_op jit(solution)/shard_map/ppermute | solution.py:20
  98.6 31.6 %collective-permute-start.5 = (bf16[1,128,2048]{2,1,0:T(8,128)(2,1)S(1)}, bf16[1,128,2048]{2,1,0:T(8,128)(2,1)S(1)}, u32[]{:S(2)}, u32[]{:S(2)}) collective-permute-start(bf16[1,128,2048]{2,1,0:T(8,128)(2,1)S(1)} %fusion.72), channel_id=1, source_target_pairs={{0,2},{2,0},{4,6},{6,4},{8,10},{10,8},{12,14},{14,12},{1,3},{3,1},... | collective-permute-start | bytes 1572872 | tf_op jit(solution)/shard_map/ppermute | solution.py:20
  132.6 0.7 copy-start.15
  132.6 1.1 copy-start.14
  132.6 1.1 copy-start.16
  132.6 1.1 copy-start.17
  132.6 3.6 %copy-start.13 = (f32[64,64]{1,0:T(8,128)S(1)}, f32[64,64]{1,0:T(8,128)}, u32[]{:S(2)}) copy-start(f32[64,64]{1,0:T(8,128)} %param.12) | copy-start | bytes 49156
  147.1 2.4 %copy-start.3 = (bf16[512,2048]{1,0:T(8,128)(2,1)S(1)}, bf16[512,2048]{1,0:T(8,128)(2,1)}, u32[]{:S(2)}) copy-start(bf16[512,2048]{1,0:T(8,128)(2,1)} %copy-done.2) | copy-start | bytes 6291460
  147.2 2.4 %copy-start.5 = (bf16[512,2048]{1,0:T(8,128)(2,1)S(1)}, bf16[512,2048]{1,0:T(8,128)(2,1)}, u32[]{:S(2)}) copy-start(bf16[512,2048]{1,0:T(8,128)(2,1)} %copy-done.4) | copy-start | bytes 6291460
  147.2 2.8 %copy-start.7 = (bf16[512,2048]{1,0:T(8,128)(2,1)S(1)}, bf16[512,2048]{1,0:T(8,128)(2,1)}, u32[]{:S(2)}) copy-start(bf16[512,2048]{1,0:T(8,128)(2,1)} %copy-done.6) | copy-start | bytes 6291460
  147.2 3.5 %copy-start.9 = (bf16[512,2048]{1,0:T(8,128)(2,1)S(1)}, bf16[512,2048]{1,0:T(8,128)(2,1)}, u32[]{:S(2)}) copy-start(bf16[512,2048]{1,0:T(8,128)(2,1)} %copy-done.8) | copy-start | bytes 6291460
  155.0 4.6 %copy-start.12 = (bf16[256,256]{1,0:T(8,128)(2,1)S(1)}, bf16[256,256]{1,0:T(8,128)(2,1)}, u32[]{:S(2)}) copy-start(bf16[256,256]{1,0:T(8,128)(2,1)} %get-tuple-element.13) | copy-start | bytes 393220
  155.0 25.2 %copy-start.1 = (bf16[256,2048]{1,0:T(8,128)(2,1)S(1)}, bf16[256,2048]{1,0:T(8,128)(2,1)}, u32[]{:S(2)}) copy-start(bf16[256,2048]{1,0:T(8,128)(2,1)} %param.8) | copy-start | bytes 3145732
Sparse Core Ops, SparseCore 0:
  132.8 45.2 reduce-scatter.1

commit v6 on v4

--- a/solution.py
+++ b/solution.py
@@ -28,11 +28,16 @@
 
 def gather_later(block):
     side_zero = lax.axis_index(SEQ_AXES) % 2 == 0
-    two_on = from_behind(block, SEQ_AXES, -2)
+    width = block.shape[1]
+    split = width // 2 if width % 256 == 0 else width
+    first_two_on = from_behind(block[:, :split], SEQ_AXES, -2)
+    first_two_on, rest = lax.optimization_barrier((first_two_on, block[:, split:]))
+    two_on = jnp.concatenate([first_two_on, from_behind(rest, SEQ_AXES, -2)], axis=1)
     partner_own = swap_pairs(block, SEQ_AXES, 1)
     four_on = from_behind(two_on, SEQ_AXES, -2)
-    partner_two_on = lax.ppermute(
-        two_on, SEQ_AXES, [(source, source ^ 1) for source in range(lax.axis_size(SEQ_AXES))]
+    partner_two_on = jnp.concatenate(
+        [swap_pairs(first_two_on, SEQ_AXES, 0, 1), swap_pairs(two_on[:, split:], SEQ_AXES, 0, 1)],
+        axis=1,
     )
     partner_four_on = lax.ppermute(
         partner_two_on,

time: 176 us -> 174 us (0.989)
  starting transfers between devices: 28.2 us -> 34.7 us
  waiting for transfers between devices: 73.5 us -> 67.3 us
    ppermute x1 -> x0, waiting for transfers between devices: 13.9 us -> none  [gather_later(): lax.ppermute(two_on, SEQ_AXES, [(source, source ^ 1) for source in range(...]
    ppermute x3 -> x5, waiting for transfers between devices: 19.9 us -> 30.5 us  [swap_pairs(): lax.ppermute(value, axis, [(source, source ^ 1) for source in range(from_...]
    ppermute x3 -> x5, starting transfers between devices: 23 us -> 29.8 us  [swap_pairs(): lax.ppermute(value, axis, [(source, source ^ 1) for source in range(from_...]
    ppermute x2 -> x3, waiting for transfers between devices: 23.9 us -> 21.9 us  [from_behind(): lax.ppermute(value, axis, [(source, source + steps) for source in range(l...]
    ppermute x2 -> x3, starting transfers between devices: 2.72 us -> 3.86 us  [from_behind(): lax.ppermute(value, axis, [(source, source + steps) for source in range(l...]
  transfers between devices with their start and end apart: 8 -> 10, of which waited for: 4 -> 7; matrix products, arithmetic and copies ran while one was open for 30% -> 30% of each run, Pallas kernels for 0% -> 0%
where the time goes in v6:
time: 174 us
  waiting for transfers between devices  67.3 us (39%)
  starting transfers between devices  34.7 us (20%)
  matrix products  28.7 us (16%)
  other arithmetic  25.5 us (15%)
  between operations  14.6 us (8%)
  local copies, waits for them, and re-layouts  3.25 us (2%)
    ppermute x5, waiting for transfers between devices, swap_pairs(): lax.ppermute(value, axis, [(source, source ^ 1) for source in range(from_...  30.5 us
    ppermute x5, starting transfers between devices, swap_pairs(): lax.ppermute(value, axis, [(source, source ^ 1) for source in range(from_...  29.8 us
    ppermute x3, waiting for transfers between devices, from_behind(): lax.ppermute(value, axis, [(source, source + steps) for source in range(l...  21.9 us
    reduce_scatter x1, waiting for transfers between devices, on_device(): lax.psum_scatter(jnp.concatenate(reduced, axis=0).astype(jnp.bfloat16), '...  14.9 us
    dot_general x1, matrix products, filter_taps(): jnp.dot(second_act, w_out, precision=lax.Precision.HIGHEST, preferred_ele...  8.79 us
    dot_general x6, matrix products, slab_spectrum(): jnp.dot(jnp.concatenate([fwd_re, fwd_im], axis=0), slab_data, preferred_e...  8.31 us
    another operation x6, other arithmetic  7.93 us
    convert_element_type x1, other arithmetic, on_device(): mix_im = sum_im.astype(jnp.bfloat16)  4.59 us
  transfers between devices with their start and end apart: 10, of which 7 were waited for; matrix products, arithmetic and copies ran while one was open for 30% of the time, Pallas kernels for 0%

profile of v6, /device:TPU:0, one launch (start us, length us, event | category | flops | bytes accessed | tf_op | source)
XLA Modules:
  0.0 174.1 jit_solution(17374140053263131579)
XLA Ops:
  7.2 0.0 copy-start
  7.2 0.0 reduce-scatter.2.cloned.1.call-start
  7.2 1.4 collective-permute-start
  8.7 1.3 fusion.101
  9.9 1.3 collective-permute-start.1
  11.3 1.0 fusion.86
  12.2 1.0 select_convert_fusion.2
  13.3 0.0 copy-done.11
  13.3 2.1 %convolution_convert_fusion.5 = bf16[512,2048]{1,0:T(8,128)(2,1)} fusion(bf16[256,2048]{1,0:T(8,128)(2,1)S(1)} %copy-done.11, bf16[256,256]{1,0:T(8,128)(2,1)S(1)} %select_convert_fusion.2, bf16[256,256]{1,0:T(8,128)(2,1)S(1)} %fusion.86), kind=kOutput, calls=%fused_computation.25 | convolution fusion | flops 538443776 | bytes 3407872 | tf_op jit(solution)/shard_map/dot_general | solution.py:107
  15.4 11.4 %collective-permute-done.1 = bf16[256,1024]{1,0:T(8,128)(2,1)S(1)} collective-permute-done((bf16[256,1024]{1,0:T(8,128)(2,1)S(1)}, bf16[256,1024]{1,0:T(8,128)(2,1)S(1)}, u32[]{:S(2)}, u32[]{:S(2)}) %collective-permute-start.1) | collective-permute-done | bytes 524320 | tf_op jit(solution)/shard_map/ppermute | solution.py:15
  26.8 1.3 collective-permute-start.3
  28.1 2.1 %convolution_convert_fusion = bf16[512,2048]{1,0:T(8,128)(2,1)} fusion(bf16[256,2048]{1,0:T(8,128)(2,1)S(1)} %copy-done, bf16[256,256]{1,0:T(8,128)(2,1)S(1)} %select_convert_fusion.2, bf16[256,256]{1,0:T(8,128)(2,1)S(1)} %fusion.86), kind=kOutput, calls=%fused_computation.20 | convolution fusion | flops 538443776 | bytes 3407872 | tf_op jit(solution)/shard_map/dot_general | solution.py:107
  30.2 3.3 %collective-permute-start.2 = (bf16[256,1024]{1,0:T(8,128)(2,1)S(1)}, bf16[256,1024]{1,0:T(8,128)(2,1)S(1)}, u32[]{:S(2)}, u32[]{:S(2)}) collective-permute-start(bf16[256,1024]{1,0:T(8,128)(2,1)S(1)} %collective-permute-done.1), channel_id=1, source_target_pairs={{0,2},{2,0},{4,6},{6,4},{8,10},{10,8},{12,14},{14,12},{1,3},{3,1},... | collective-permute-start | bytes 1572872 | tf_op jit(solution)/shard_map/ppermute | solution.py:20
  33.5 1.2 multiply_convert_fusion.1
  34.7 0.0 copy-start.12
  34.7 7.1 %collective-permute-done.3 = bf16[256,1024]{1,0:T(8,128)(2,1)S(1)} collective-permute-done((bf16[256,1024]{1,0:T(8,128)(2,1)S(1)}, bf16[256,1024]{1,0:T(8,128)(2,1)S(1)}, u32[]{:S(2)}, u32[]{:S(2)}) %collective-permute-start.3) | collective-permute-done | bytes 524320 | tf_op jit(solution)/shard_map/ppermute | solution.py:15
  41.9 2.9 %collective-permute-start.4 = (bf16[256,1024]{1,0:T(8,128)(2,1)S(1)}, bf16[256,1024]{1,0:T(8,128)(2,1)S(1)}, u32[]{:S(2)}, u32[]{:S(2)}) collective-permute-start(bf16[256,1024]{1,0:T(8,128)(2,1)S(1)} %collective-permute-done.3), channel_id=1, source_target_pairs={{0,2},{2,0},{4,6},{6,4},{8,10},{10,8},{12,14},{14,12},{1,3},{3,1},... | collective-permute-start | bytes 1572872 | tf_op jit(solution)/shard_map/ppermute | solution.py:20
  44.8 1.3 collective-permute-start.6
  46.1 0.9 collective-permute-done.2
  47.1 0.7 convolution_convert_fusion.3
  47.8 9.6 %collective-permute-done.4 = bf16[256,1024]{1,0:T(8,128)(2,1)S(1)} collective-permute-done((bf16[256,1024]{1,0:T(8,128)(2,1)S(1)}, bf16[256,1024]{1,0:T(8,128)(2,1)S(1)}, u32[]{:S(2)}, u32[]{:S(2)}) %collective-permute-start.4) | collective-permute-done | bytes 524320 | tf_op jit(solution)/shard_map/ppermute | solution.py:20
  57.5 1.0 collective-permute-start.5
  58.6 0.0 collective-permute-done
  58.6 2.0 %convolution_convert_fusion.4 = bf16[512,2048]{1,0:T(8,128)(2,1)S(1)} fusion(bf16[256,2048]{1,0:T(8,128)(2,1)} %collective-permute-done, bf16[256,2048]{1,0:T(8,128)(2,1)S(1)} %constant_dynamic-update-slice_fusion, pred[]{:T(512)S(6)} %eq.91, bf16[256,256]{1,0:T(8,128)(2,1)S(1)} %select_convert_fusion.2, bf16[256,256]{1,0:T(8,128)(2,1)S(1)} %fusion.86), kind=kOutput, calls=%fused_computation.24 | convolution fusion | flops 538968064 | bytes 4456449 | tf_op jit(solution)/shard_map/dot_general | solution.py:107
  60.6 1.7 fusion.28
  62.3 1.7 fusion.23
  64.0 0.7 fusion.49
  64.7 0.7 fusion.45
  65.4 0.5 pad_maximum_fusion
  65.9 0.2 fusion.66
  66.1 0.1 collective-permute-start.7
  66.2 3.3 %collective-permute-done.6 = bf16[256,2048]{1,0:T(8,128)(2,1)S(1)} collective-permute-done((bf16[256,2048]{1,0:T(8,128)(2,1)S(1)}, bf16[256,2048]{1,0:T(8,128)(2,1)S(1)}, u32[]{:S(2)}, u32[]{:S(2)}) %collective-permute-start.6) | collective-permute-done | bytes 1048608 | tf_op jit(solution)/shard_map/ppermute | solution.py:15
  69.5 0.7 convolution_convert_fusion.1
  70.3 0.0 collective-permute-done.5
  70.3 0.7 convolution_convert_fusion.2
  71.1 1.7 fusion.33
  72.7 1.9 %fusion.38 = (bf16[256,2048]{1,0:T(8,128)(2,1)S(1)}, bf16[256,2048]{1,0:T(8,128)(2,1)S(1)}) fusion(f32[256]{0:T(256)S(1)} %compare_select_fusion, pred[256]{0:T(512)(128)(4,1)S(1)} %iota_compare_fusion, bf16[512,2048]{1,0:T(8,128)(2,1)S(1)} %convolution_convert_fusion.1, bf16[512,2048]{1,0:T(8,128)(2,1)S(1)} %convolution_convert_fusion.2, ...), kind=kLoop, calls=%fused_computation.93 | loop fusion | flops 10485760 | bytes 8389888 | tf_op jit(solution)/shard_map/convert.11
  74.6 0.7 fusion.57
  75.3 0.7 fusion.53
  76.1 0.5 pad_maximum_fusion.1
  76.6 0.2 fusion.67
  76.8 22.1 %collective-permute-start.8 = (bf16[2,128,2048]{2,1,0:T(8,128)(2,1)S(1)}, bf16[2,128,2048]{2,1,0:T(8,128)(2,1)S(1)}, u32[]{:S(2)}, u32[]{:S(2)}) collective-permute-start(bf16[2,128,2048]{2,1,0:T(8,128)(2,1)S(1)} %fusion.67), channel_id=1, source_target_pairs={{0,2},{2,0},{4,6},{6,4},{8,10},{10,8},{12,14},{14,12},{1,3},{3,1},... | collective-permute-start | bytes 3145736 | tf_op jit(solution)/shard_map/ppermute | solution.py:20
  98.8 0.0 collective-permute-done.7
  98.8 0.5 fusion.62
  99.3 19.9 %collective-permute-done.8 = bf16[2,128,2048]{2,1,0:T(8,128)(2,1)S(1)} collective-permute-done((bf16[2,128,2048]{2,1,0:T(8,128)(2,1)S(1)}, bf16[2,128,2048]{2,1,0:T(8,128)(2,1)S(1)}, u32[]{:S(2)}, u32[]{:S(2)}) %collective-permute-start.8) | collective-permute-done | bytes 1048608 | tf_op jit(solution)/shard_map/ppermute | solution.py:20
  119.3 0.5 fusion.61
  119.8 1.6 pad_maximum_fusion.2
  121.4 0.0 copy-start.14
  121.4 0.0 reduce-scatter.2.cloned.1.call-update
  121.4 0.6 copy-done.16
  122.1 0.3 fusion.94
  122.5 2.5 %fusion.65 = f32[1024,64]{1,0:T(8,128)S(1)} fusion(f32[33,64]{1,0:T(8,128)S(1)} %copy-done.15, f32[64]{0:T(128)S(1)} %copy-done.18, f32[64]{0:T(128)S(1)} %copy-done.17, f32[1024,16]{0,1:T(8,128)S(1)} %get-tuple-element.17, f32[1024,16]{0,1:T(8,128)S(1)} %get-tuple-element.16, f32[1024,1]{0,1:T(1,128)S(1)} %convert_multiply_fusion.38), kind=kOutput, calls=%fused_computation.131 | convolution fusion | flops 26150912 | bytes 406272 | tf_op jit(solution)/shard_map/dot_general | solution.py:80
  125.0 2.2 %fusion.63 = f32[1024,64]{1,0:T(8,128)S(1)} fusion(f32[1024,64]{1,0:T(8,128)S(1)} %fusion.65, f32[64,64]{1,0:T(8,128)S(1)} %copy-done.14, f32[64]{0:T(128)S(1)} %copy-done.17), kind=kOutput, calls=%fused_computation.129 | convolution fusion | flops 50397184 | bytes 540928 | tf_op jit(solution)/shard_map/dot_general | solution.py:88
  127.2 8.8 %multiply_convert_fusion = bf16[1024,2048]{1,0:T(8,128)(2,1)S(1)} fusion(f32[1024,64]{1,0:T(8,128)S(1)} %fusion.63, f32[64,2048]{1,0:T(8,128)} %param.14, f32[1024]{0:T(1024)S(1)} %iota_convert_fusion, f32[2048]{0:T(1024)S(1)} %neg.7), kind=kOutput, calls=%fused_computation.1 | convolution fusion | flops 1616904192 | bytes 4993024 | tf_op jit(solution)/shard_map/dot_general | solution.py:92
  136.0 2.4 %convert_bitcast_fusion = bf16[4,512,2048]{2,1,0:T(8,128)(2,1)S(1)} fusion(bf16[4,256,2048]{2,1,0:T(8,128)(2,1)S(1)} %bitcast.125, bf16[256,256]{1,0:T(8,128)(2,1)S(1)} %select_convert_fusion.2, bf16[256,256]{1,0:T(8,128)(2,1)S(1)} %fusion.86), kind=kOutput, calls=%fused_computation | convolution fusion | flops 2152202240 | bytes 12845056 | tf_op jit(solution)/shard_map/fs,jsc->jfc/dot_general | solution.py:115
  138.4 0.5 copy-done.8
  138.9 0.6 copy-done.10
  139.5 4.4 %fusion.6 = bf16[256,2048]{1,0:T(8,128)(2,1)S(1)} fusion(f32[256]{0:T(256)S(1)} %compare_select_fusion, pred[256]{0:T(512)(128)(4,1)S(1)} %iota_compare_fusion, bf16[4,512,2048]{2,1,0:T(8,128)(2,1)S(1)} %convert_bitcast_fusion, bf16[512,2048]{1,0:T(8,128)(2,1)S(1)} %copy-done.10, bf16[512,2048]{1,0:T(8,128)(2,1)S(1)} %copy-done.8, ...), kind=kLoop, calls=%fused_computation.61 | loop fusion | flops 28311552 | bytes 19924224 | tf_op jit(solution)/shard_map/convert_element_type | solution.py:159
  143.9 0.0 copy-start.13
  143.9 0.0 copy-start.1
  143.9 4.6 %fusion.12 = bf16[256,2048]{1,0:T(8,128)(2,1)S(1)} fusion(f32[256]{0:T(256)S(1)} %compare_select_fusion, pred[256]{0:T(512)(128)(4,1)S(1)} %iota_compare_fusion, bf16[4,512,2048]{2,1,0:T(8,128)(2,1)S(1)} %convert_bitcast_fusion, bf16[512,2048]{1,0:T(8,128)(2,1)S(1)} %copy-done.10, bf16[512,2048]{1,0:T(8,128)(2,1)S(1)} %copy-done.8, ...), kind=kLoop, calls=%fused_computation.67 | loop fusion | flops 30408704 | bytes 19924224 | tf_op jit(solution)/shard_map/convert_element_type | solution.py:160
  148.5 1.7 convolution_convert_fusion.6
  150.2 14.9 %reduce-scatter.2.cloned.1.call-done = bf16[1,128,2048]{2,1,0:T(8,128)(2,1)} async-done(((bf16[4,128,2048]{2,1,0:T(8,128)(2,1)}), bf16[1,128,2048]{2,1,0:T(8,128)(2,1)}) %reduce-scatter.2.cloned.1.call-update) | async-done | bytes 524304 | tf_op jit(solution)/shard_map/reduce_scatter | solution.py:193
  165.1 2.1 %bitcast_convert_fusion = f32[128,2048]{1,0:T(8,128)} fusion(bf16[1,128,2048]{2,1,0:T(8,128)(2,1)} %reduce-scatter.2.cloned.1.call-done), kind=kLoop, calls=%fused_computation.146 | loop fusion | flops 262144 | bytes 1572864 | tf_op jit(solution)/shard_map/convert_element_type | solution.py:196
  (40 shorter events, 0.2 us)
Async XLA Ops:
  7.2 20.9 %copy-start = (bf16[256,2048]{1,0:T(8,128)(2,1)S(1)}, bf16[256,2048]{1,0:T(8,128)(2,1)}, u32[]{:S(2)}) copy-start(bf16[256,2048]{1,0:T(8,128)(2,1)} %param.8) | copy-start | bytes 3145732
  7.2 6.1 %copy-start.11 = (bf16[256,2048]{1,0:T(8,128)(2,1)S(1)}, bf16[256,2048]{1,0:T(8,128)(2,1)}, u32[]{:S(2)}) copy-start(bf16[256,2048]{1,0:T(8,128)(2,1)} %param.9) | copy-start | bytes 3145732
  7.2 157.9 %reduce-scatter.2.cloned.1.call-start = ((), (), s32[]{:S(2)}) async-start(), calls=%async_computation.1 | async-start | bytes 2621440 | tf_op jit(solution)/shard_map/reduce_scatter | solution.py:193
  7.2 51.3 %collective-permute-start = (bf16[256,2048]{1,0:T(8,128)(2,1)}, bf16[256,2048]{1,0:T(8,128)(2,1)}, u32[]{:S(2)}, u32[]{:S(2)}) collective-permute-start(bf16[256,2048]{1,0:T(8,128)(2,1)} %param.9), channel_id=1, source_target_pairs={{2,0},{6,4},{10,8},{14,12},{3,1},{7,5},{11,9},{15,13},{18,16},{22,... | collective-permute-start | bytes 3145736 | tf_op jit(solution)/shard_map/ppermute | solution.py:20
  9.9 16.8 %collective-permute-start.1 = (bf16[256,1024]{1,0:T(8,128)(2,1)S(1)}, bf16[256,1024]{1,0:T(8,128)(2,1)S(1)}, u32[]{:S(2)}, u32[]{:S(2)}) collective-permute-start(bf16[256,1024]{1,0:T(8,128)(2,1)S(1)} %get-tuple-element.15), channel_id=1, source_target_pairs={{4,0},{6,2},{8,4},{10,6},{12,8},{14,10},{5,1},{7,3},{9,5},{11,7},{... | collective-permute-start | bytes 1572872 | tf_op jit(solution)/shard_map/ppermute | solution.py:15
  26.8 15.1 %collective-permute-start.3 = (bf16[256,1024]{1,0:T(8,128)(2,1)S(1)}, bf16[256,1024]{1,0:T(8,128)(2,1)S(1)}, u32[]{:S(2)}, u32[]{:S(2)}) collective-permute-start(bf16[256,1024]{1,0:T(8,128)(2,1)S(1)} %get-tuple-element.5), channel_id=1, source_target_pairs={{4,0},{6,2},{8,4},{10,6},{12,8},{14,10},{5,1},{7,3},{9,5},{11,7},{... | collective-permute-start | bytes 1572872 | tf_op jit(solution)/shard_map/ppermute | solution.py:15
  30.2 16.9 %collective-permute-start.2 = (bf16[256,1024]{1,0:T(8,128)(2,1)S(1)}, bf16[256,1024]{1,0:T(8,128)(2,1)S(1)}, u32[]{:S(2)}, u32[]{:S(2)}) collective-permute-start(bf16[256,1024]{1,0:T(8,128)(2,1)S(1)} %collective-permute-done.1), channel_id=1, source_target_pairs={{0,2},{2,0},{4,6},{6,4},{8,10},{10,8},{12,14},{14,12},{1,3},{3,1},... | collective-permute-start | bytes 1572872 | tf_op jit(solution)/shard_map/ppermute | solution.py:20
  34.7 40.6 %copy-start.12 = (bf16[256,256]{1,0:T(8,128)(2,1)}, bf16[256,256]{1,0:T(8,128)(2,1)S(1)}, u32[]{:S(2)}) copy-start(bf16[256,256]{1,0:T(8,128)(2,1)S(1)} %get-tuple-element.19) | copy-start | bytes 393220
  41.9 15.6 %collective-permute-start.4 = (bf16[256,1024]{1,0:T(8,128)(2,1)S(1)}, bf16[256,1024]{1,0:T(8,128)(2,1)S(1)}, u32[]{:S(2)}, u32[]{:S(2)}) collective-permute-start(bf16[256,1024]{1,0:T(8,128)(2,1)S(1)} %collective-permute-done.3), channel_id=1, source_target_pairs={{0,2},{2,0},{4,6},{6,4},{8,10},{10,8},{12,14},{14,12},{1,3},{3,1},... | collective-permute-start | bytes 1572872 | tf_op jit(solution)/shard_map/ppermute | solution.py:20
  44.8 24.7 %collective-permute-start.6 = (bf16[256,2048]{1,0:T(8,128)(2,1)S(1)}, bf16[256,2048]{1,0:T(8,128)(2,1)S(1)}, u32[]{:S(2)}, u32[]{:S(2)}) collective-permute-start(bf16[256,2048]{1,0:T(8,128)(2,1)S(1)} %constant_dynamic-update-slice_fusion.2), channel_id=1, source_target_pairs={{4,0},{6,2},{8,4},{10,6},{12,8},{14,10},{5,1},{7,3},{9,5},{11,7},{... | collective-permute-start | bytes 3145736 | tf_op jit(solution)/shard_map/ppermute | solution.py:15
  47.8 23.2 %copy-start.5 = (bf16[512,2048]{1,0:T(8,128)(2,1)}, bf16[512,2048]{1,0:T(8,128)(2,1)S(1)}, u32[]{:S(2)}) copy-start(bf16[512,2048]{1,0:T(8,128)(2,1)S(1)} %convolution_convert_fusion.3) | copy-start | bytes 6291460
  57.5 3.1 %copy-start.4 = (bf16[512,2048]{1,0:T(8,128)(2,1)S(1)}, bf16[512,2048]{1,0:T(8,128)(2,1)}, u32[]{:S(2)}) copy-start(bf16[512,2048]{1,0:T(8,128)(2,1)} %convolution_convert_fusion) | copy-start | bytes 6291460
  57.5 12.8 %collective-permute-start.5 = (bf16[256,2048]{1,0:T(8,128)(2,1)S(1)}, bf16[256,2048]{1,0:T(8,128)(2,1)S(1)}, u32[]{:S(2)}, u32[]{:S(2)}) collective-permute-start(bf16[256,2048]{1,0:T(8,128)(2,1)S(1)} %constant_dynamic-update-slice_fusion), channel_id=1, source_target_pairs={{6,2},{10,6},{14,10},{7,3},{11,7},{15,11},{22,18},{26,22},{30,26},... | collective-permute-start | bytes 3145736 | tf_op jit(solution)/shard_map/ppermute | solution.py:42
  60.6 1.7 copy-start.7
  66.1 32.7 %collective-permute-start.7 = (bf16[2,128,2048]{2,1,0:T(8,128)(2,1)S(1)}, bf16[2,128,2048]{2,1,0:T(8,128)(2,1)S(1)}, u32[]{:S(2)}, u32[]{:S(2)}) collective-permute-start(bf16[2,128,2048]{2,1,0:T(8,128)(2,1)S(1)} %fusion.66), channel_id=1, source_target_pairs={{0,2},{2,0},{4,6},{6,4},{8,10},{10,8},{12,14},{14,12},{1,3},{3,1},... | collective-permute-start | bytes 3145736 | tf_op jit(solution)/shard_map/ppermute | solution.py:20
  70.3 2.5 %copy-start.9 = (bf16[512,2048]{1,0:T(8,128)(2,1)}, bf16[512,2048]{1,0:T(8,128)(2,1)S(1)}, u32[]{:S(2)}) copy-start(bf16[512,2048]{1,0:T(8,128)(2,1)S(1)} %convolution_convert_fusion.1) | copy-start | bytes 6291460
  71.0 1.7 copy-start.2
  76.8 42.5 %collective-permute-start.8 = (bf16[2,128,2048]{2,1,0:T(8,128)(2,1)S(1)}, bf16[2,128,2048]{2,1,0:T(8,128)(2,1)S(1)}, u32[]{:S(2)}, u32[]{:S(2)}) collective-permute-start(bf16[2,128,2048]{2,1,0:T(8,128)(2,1)S(1)} %fusion.67), channel_id=1, source_target_pairs={{0,2},{2,0},{4,6},{6,4},{8,10},{10,8},{12,14},{14,12},{1,3},{3,1},... | collective-permute-start | bytes 3145736 | tf_op jit(solution)/shard_map/ppermute | solution.py:20
  121.4 0.7 copy-start.16
  121.4 1.1 copy-start.15
  121.4 1.1 copy-start.17
  121.4 1.1 copy-start.18
  121.4 3.6 %copy-start.14 = (f32[64,64]{1,0:T(8,128)S(1)}, f32[64,64]{1,0:T(8,128)}, u32[]{:S(2)}) copy-start(f32[64,64]{1,0:T(8,128)} %param.12) | copy-start | bytes 49156
  136.0 2.4 %copy-start.3 = (bf16[512,2048]{1,0:T(8,128)(2,1)S(1)}, bf16[512,2048]{1,0:T(8,128)(2,1)}, u32[]{:S(2)}) copy-start(bf16[512,2048]{1,0:T(8,128)(2,1)} %copy-done.2) | copy-start | bytes 6291460
  136.0 2.4 %copy-start.6 = (bf16[512,2048]{1,0:T(8,128)(2,1)S(1)}, bf16[512,2048]{1,0:T(8,128)(2,1)}, u32[]{:S(2)}) copy-start(bf16[512,2048]{1,0:T(8,128)(2,1)} %copy-done.5) | copy-start | bytes 6291460
  136.0 2.9 %copy-start.8 = (bf16[512,2048]{1,0:T(8,128)(2,1)S(1)}, bf16[512,2048]{1,0:T(8,128)(2,1)}, u32[]{:S(2)}) copy-start(bf16[512,2048]{1,0:T(8,128)(2,1)} %convolution_convert_fusion.5) | copy-start | bytes 6291460
  136.0 3.5 %copy-start.10 = (bf16[512,2048]{1,0:T(8,128)(2,1)S(1)}, bf16[512,2048]{1,0:T(8,128)(2,1)}, u32[]{:S(2)}) copy-start(bf16[512,2048]{1,0:T(8,128)(2,1)} %copy-done.9) | copy-start | bytes 6291460
  143.9 4.6 %copy-start.13 = (bf16[256,256]{1,0:T(8,128)(2,1)S(1)}, bf16[256,256]{1,0:T(8,128)(2,1)}, u32[]{:S(2)}) copy-start(bf16[256,256]{1,0:T(8,128)(2,1)} %copy-done.12) | copy-start | bytes 393220
  143.9 23.3 %copy-start.1 = (bf16[256,2048]{1,0:T(8,128)(2,1)S(1)}, bf16[256,2048]{1,0:T(8,128)(2,1)}, u32[]{:S(2)}) copy-start(bf16[256,2048]{1,0:T(8,128)(2,1)} %param.8) | copy-start | bytes 3145732
Sparse Core Ops, SparseCore 0:
  121.6 43.5 reduce-scatter.1

commit v7 on v6

--- a/solution.py
+++ b/solution.py
@@ -183,17 +183,34 @@
     share = lag_rows_total(grad_rows) // (row_count * 2)
     side_zero = lax.axis_index("side") == 0
     parts = 2 if row_count % 2 == 0 else 1
-    reduced = []
-    for part in range(parts):
-        chosen = grad_rows[part * LAG_BLOCKS // parts : (part + 1) * LAG_BLOCKS // parts]
-        staged = jnp.concatenate(chosen, axis=0).reshape(-1, 2, share, chan_width)
-        mine = jnp.where(side_zero, staged[:, 0], staged[:, 1])
-        theirs = jnp.where(side_zero, staged[:, 1], staged[:, 0]).astype(jnp.bfloat16)
-        reduced.append(mine + swap_pairs(theirs, SEQ_AXES, 0, 1).astype(jnp.float32))
-    by_row = lax.psum_scatter(
-        jnp.concatenate(reduced, axis=0).astype(jnp.bfloat16), "row", scatter_dimension=0, tiled=True
-    )
-    grad_filter = by_row.reshape(share, chan_width).astype(jnp.float32)
+    halves = 2 if chan_width % 256 == 0 else 1
+    span = chan_width // halves
+    outputs = []
+    gate = None
+    for lane in range(halves):
+        reduced = []
+        for part in range(parts):
+            chosen = [
+                rows[:, lane * span : (lane + 1) * span]
+                for rows in grad_rows[part * LAG_BLOCKS // parts : (part + 1) * LAG_BLOCKS // parts]
+            ]
+            staged = jnp.concatenate(chosen, axis=0).reshape(-1, 2, share, span)
+            mine = jnp.where(side_zero, staged[:, 0], staged[:, 1])
+            theirs = jnp.where(side_zero, staged[:, 1], staged[:, 0]).astype(jnp.bfloat16)
+            if gate is not None:
+                theirs, gate = lax.optimization_barrier((theirs, gate))
+            received = swap_pairs(theirs, SEQ_AXES, 0, 1)
+            gate = received
+            reduced.append(mine + received.astype(jnp.float32))
+        outputs.append(
+            lax.psum_scatter(
+                jnp.concatenate(reduced, axis=0).astype(jnp.bfloat16),
+                "row",
+                scatter_dimension=0,
+                tiled=True,
+            ).reshape(share, span)
+        )
+    grad_filter = jnp.concatenate(outputs, axis=1).astype(jnp.float32)
     return (grad_inputs, grad_filter)
 
 

time: 174 us -> 177 us (1.017)
  waiting for transfers between devices: 67.3 us -> 46.8 us
  other arithmetic: 25.5 us -> 37.9 us
  matrix products: 28.7 us -> 33.6 us
  starting transfers between devices: 34.7 us -> 39.2 us
    ppermute x5 -> x7, waiting for transfers between devices: 30.5 us -> 18.9 us  [swap_pairs(): lax.ppermute(value, axis, [(source, source ^ 1) for source in range(from_...]
    ppermute x3, waiting for transfers between devices: 21.9 us -> 15.1 us  [from_behind(): lax.ppermute(value, axis, [(source, source + steps) for source in range(l...]
    convert_element_type x1, other arithmetic: 4.36 us -> 9.52 us  [on_device(): mix_re = sum_re.astype(jnp.bfloat16)]
    ppermute x5 -> x7, starting transfers between devices: 29.8 us -> 33.9 us  [swap_pairs(): lax.ppermute(value, axis, [(source, source ^ 1) for source in range(from_...]
    dot_general x1, matrix products: 2.35 us -> 5.63 us  [batch_spectrum(): jnp.einsum('fs,jsc->jfc', jnp.concatenate([fwd_re, fwd_im], axis=0), slab...]
    convert_element_type x1, other arithmetic: 4.59 us -> 6.8 us  [on_device(): mix_im = sum_im.astype(jnp.bfloat16)]
    reduce_scatter x1 -> x2, waiting for transfers between devices: 14.9 us -> 12.7 us  [on_device(): lax.psum_scatter(jnp.concatenate(reduced, axis=0).astype(jnp.bfloat16), '...]
    another operation x6 -> x8, other arithmetic: 7.93 us -> 7.81 us
  transfers between devices with their start and end apart: 10 -> 13, of which waited for: 7 -> 9; matrix products, arithmetic and copies ran while one was open for 30% -> 41% of each run, Pallas kernels for 0% -> 0%
where the time goes in v7:
time: 177 us; the launch traced here: 176 us
  waiting for transfers between devices  46.8 us (26%)
  starting transfers between devices  39.2 us (22%)
  other arithmetic  37.9 us (21%)
  matrix products  33.6 us (19%)
  between operations  14.7 us (8%)
  local copies, waits for them, and re-layouts  4.03 us (2%)
    ppermute x7, starting transfers between devices, swap_pairs(): lax.ppermute(value, axis, [(source, source ^ 1) for source in range(from_...  33.9 us
    ppermute x7, waiting for transfers between devices, swap_pairs(): lax.ppermute(value, axis, [(source, source ^ 1) for source in range(from_...  18.9 us
    ppermute x3, waiting for transfers between devices, from_behind(): lax.ppermute(value, axis, [(source, source + steps) for source in range(l...  15.1 us
    reduce_scatter x2, waiting for transfers between devices, on_device(): lax.psum_scatter(jnp.concatenate(reduced, axis=0).astype(jnp.bfloat16), '...  12.7 us
    convert_element_type x1, other arithmetic, on_device(): mix_re = sum_re.astype(jnp.bfloat16)  9.52 us
    dot_general x1, matrix products, filter_taps(): jnp.dot(second_act, w_out, precision=lax.Precision.HIGHEST, preferred_ele...  8.76 us
    dot_general x6, matrix products, slab_spectrum(): jnp.dot(jnp.concatenate([fwd_re, fwd_im], axis=0), slab_data, preferred_e...  8.27 us
    another operation x8, other arithmetic  7.81 us
  transfers between devices with their start and end apart: 13, of which 9 were waited for; matrix products, arithmetic and copies ran while one was open for 41% of the time, Pallas kernels for 0%

profile of v7, /device:TPU:0, one launch (start us, length us, event | category | flops | bytes accessed | tf_op | source)
XLA Modules:
  0.0 176.1 jit_solution(3828888381017717769)
XLA Ops:
  7.2 1.4 collective-permute-start
  8.7 2.1 %fusion.109 = (bf16[256,1024]{1,0:T(8,128)(2,1)}, bf16[256,1024]{1,0:T(8,128)(2,1)S(1)}) fusion(bf16[256,2048]{1,0:T(8,128)(2,1)} %param.9), kind=kLoop, calls=%fused_computation.217 | loop fusion | bytes 2097152 | tf_op jit(solution)/shard_map/slice | solution.py:34
  10.7 1.4 collective-permute-start.1
  12.2 1.0 fusion.90
  13.2 0.3 fusion.98
  13.5 1.0 select_convert_fusion.4
  14.6 2.1 %convolution_convert_fusion.5 = bf16[512,2048]{1,0:T(8,128)(2,1)} fusion(bf16[256,2048]{1,0:T(8,128)(2,1)S(1)} %copy-done.12, bf16[256,256]{1,0:T(8,128)(2,1)S(1)} %select_convert_fusion.4, bf16[256,256]{1,0:T(8,128)(2,1)S(1)} %fusion.90), kind=kOutput, calls=%fused_computation.23 | convolution fusion | flops 538443776 | bytes 3407872 | tf_op jit(solution)/shard_map/dot_general | solution.py:107
  16.7 2.5 %fusion.63 = f32[1024,64]{1,0:T(8,128)S(1)} fusion(f32[33,64]{1,0:T(8,128)S(1)} %copy-done.16, f32[64]{0:T(128)S(1)} %copy-done.20, f32[64]{0:T(128)S(1)} %copy-done.19, f32[1024,16]{0,1:T(8,128)S(1)} %get-tuple-element.31, f32[1024,16]{0,1:T(8,128)S(1)} %get-tuple-element.30, f32[1024,1]{0,1:T(1,128)S(1)} %convert_multiply_fusion.38), kind=kOutput, calls=%fused_computation.122 | convolution fusion | flops 26150912 | bytes 406272 | tf_op jit(solution)/shard_map/dot_general | solution.py:80
  19.2 2.1 %convolution_convert_fusion = bf16[512,2048]{1,0:T(8,128)(2,1)} fusion(bf16[256,2048]{1,0:T(8,128)(2,1)S(1)} %copy-done, bf16[256,256]{1,0:T(8,128)(2,1)S(1)} %select_convert_fusion.4, bf16[256,256]{1,0:T(8,128)(2,1)S(1)} %fusion.90), kind=kOutput, calls=%fused_computation.18 | convolution fusion | flops 538443776 | bytes 3407872 | tf_op jit(solution)/shard_map/dot_general | solution.py:107
  21.3 6.4 %collective-permute-done.1 = bf16[256,1024]{1,0:T(8,128)(2,1)S(1)} collective-permute-done((bf16[256,1024]{1,0:T(8,128)(2,1)S(1)}, bf16[256,1024]{1,0:T(8,128)(2,1)S(1)}, u32[]{:S(2)}, u32[]{:S(2)}) %collective-permute-start.1) | collective-permute-done | bytes 524320 | tf_op jit(solution)/shard_map/ppermute | solution.py:15
  27.7 1.3 collective-permute-start.3
  29.0 3.4 %collective-permute-start.2 = (bf16[256,1024]{1,0:T(8,128)(2,1)S(1)}, bf16[256,1024]{1,0:T(8,128)(2,1)S(1)}, u32[]{:S(2)}, u32[]{:S(2)}) collective-permute-start(bf16[256,1024]{1,0:T(8,128)(2,1)S(1)} %collective-permute-done.1), channel_id=1, source_target_pairs={{0,2},{2,0},{4,6},{6,4},{8,10},{10,8},{12,14},{14,12},{1,3},{3,1},... | collective-permute-start | bytes 1572872 | tf_op jit(solution)/shard_map/ppermute | solution.py:20
  32.4 1.8 %multiply_convert_fusion.1 = (bf16[256,256]{1,0:T(8,128)(2,1)S(1)}, bf16[256,256]{1,0:T(8,128)(2,1)}) fusion(f32[256]{0:T(256)S(1)} %compare_select_fusion, pred[256]{0:T(512)(128)(4,1)S(1)} %iota_compare_fusion, f32[256]{0:T(256)S(1)} %broadcast_select_fusion), kind=kLoop, calls=%fused_computation.172 | loop fusion | flops 1376256 | bytes 264448 | tf_op jit(solution)/shard_map/convert_element_type | solution.py:64
  34.2 0.6 neg.7
  34.8 3.8 %fusion.61 = f32[1024,64]{1,0:T(8,128)} fusion(f32[1024,64]{1,0:T(8,128)S(1)} %fusion.63, f32[64,64]{1,0:T(8,128)} %param.12, f32[64]{0:T(128)} %param.13), kind=kOutput, calls=%fused_computation.120 | convolution fusion | flops 50397184 | bytes 540928 | tf_op jit(solution)/shard_map/dot_general | solution.py:88
  38.7 4.3 %collective-permute-done.3 = bf16[256,1024]{1,0:T(8,128)(2,1)S(1)} collective-permute-done((bf16[256,1024]{1,0:T(8,128)(2,1)}, bf16[256,1024]{1,0:T(8,128)(2,1)S(1)}, u32[]{:S(2)}, u32[]{:S(2)}) %collective-permute-start.3) | collective-permute-done | bytes 524320 | tf_op jit(solution)/shard_map/ppermute | solution.py:15
  43.0 2.9 %collective-permute-start.4 = (bf16[256,1024]{1,0:T(8,128)(2,1)S(1)}, bf16[256,1024]{1,0:T(8,128)(2,1)S(1)}, u32[]{:S(2)}, u32[]{:S(2)}) collective-permute-start(bf16[256,1024]{1,0:T(8,128)(2,1)S(1)} %collective-permute-done.3), channel_id=1, source_target_pairs={{0,2},{2,0},{4,6},{6,4},{8,10},{10,8},{12,14},{14,12},{1,3},{3,1},... | collective-permute-start | bytes 1572872 | tf_op jit(solution)/shard_map/ppermute | solution.py:20
  46.0 1.3 collective-permute-start.6
  47.3 0.7 convolution_convert_fusion.3
  48.1 9.4 %collective-permute-done.4 = bf16[256,1024]{1,0:T(8,128)(2,1)S(1)} collective-permute-done((bf16[256,1024]{1,0:T(8,128)(2,1)S(1)}, bf16[256,1024]{1,0:T(8,128)(2,1)S(1)}, u32[]{:S(2)}, u32[]{:S(2)}) %collective-permute-start.4) | collective-permute-done | bytes 524320 | tf_op jit(solution)/shard_map/ppermute | solution.py:20
  57.5 1.0 collective-permute-start.5
  58.6 2.0 %convolution_convert_fusion.4 = bf16[512,2048]{1,0:T(8,128)(2,1)S(1)} fusion(bf16[256,2048]{1,0:T(8,128)(2,1)} %collective-permute-done, bf16[256,2048]{1,0:T(8,128)(2,1)S(1)} %constant_dynamic-update-slice_fusion, pred[]{:T(512)S(6)} %eq.91, bf16[256,256]{1,0:T(8,128)(2,1)S(1)} %select_convert_fusion.4, bf16[256,256]{1,0:T(8,128)(2,1)S(1)} %fusion.90), kind=kOutput, calls=%fused_computation.22 | convolution fusion | flops 538968064 | bytes 4456449 | tf_op jit(solution)/shard_map/dot_general | solution.py:107
  60.5 1.7 fusion.28
  62.2 1.7 fusion.23
  63.9 0.7 fusion.49
  64.7 0.2 fusion.106
  64.9 0.7 fusion.45
  65.6 0.2 fusion.105
  65.9 0.2 pad_maximum_fusion
  66.3 4.4 %collective-permute-done.6 = bf16[256,2048]{1,0:T(8,128)(2,1)S(1)} collective-permute-done((bf16[256,2048]{1,0:T(8,128)(2,1)S(1)}, bf16[256,2048]{1,0:T(8,128)(2,1)S(1)}, u32[]{:S(2)}, u32[]{:S(2)}) %collective-permute-start.6) | collective-permute-done | bytes 1048608 | tf_op jit(solution)/shard_map/ppermute | solution.py:15
  70.7 0.7 convolution_convert_fusion.1
  71.4 0.7 convolution_convert_fusion.2
  72.2 1.7 fusion.33
  74.0 1.7 fusion.38
  75.7 0.7 fusion.57
  76.4 0.1 fusion.108
  76.6 0.7 fusion.53
  77.3 1.1 fusion.107
  78.4 0.2 pad_maximum_fusion.1
  78.7 0.2 collective-permute-done.7
  78.9 21.9 %collective-permute-start.8 = (bf16[2,128,1024]{2,1,0:T(8,128)(2,1)S(1)}, bf16[2,128,1024]{2,1,0:T(8,128)(2,1)S(1)}, u32[]{:S(2)}, u32[]{:S(2)}) collective-permute-start(bf16[2,128,1024]{2,1,0:T(8,128)(2,1)S(1)} %fusion.73), channel_id=1, source_target_pairs={{0,2},{2,0},{4,6},{6,4},{8,10},{10,8},{12,14},{14,12},{1,3},{3,1},... | collective-permute-start | bytes 1572872 | tf_op jit(solution)/shard_map/ppermute | solution.py:20
  100.8 0.6 iota_convert_fusion
  101.4 1.5 pad_maximum_fusion.2
  102.9 0.3 fusion.67
  103.2 6.8 %collective-permute-done.8 = bf16[2,128,1024]{2,1,0:T(8,128)(2,1)S(1)} collective-permute-done((bf16[2,128,1024]{2,1,0:T(8,128)(2,1)S(1)}, bf16[2,128,1024]{2,1,0:T(8,128)(2,1)S(1)}, u32[]{:S(2)}, u32[]{:S(2)}) %collective-permute-start.8) | collective-permute-done | bytes 524320 | tf_op jit(solution)/shard_map/ppermute | solution.py:20
  110.0 0.3 fusion.66
  110.3 1.1 pad_maximum_fusion.4
  111.4 0.3 reduce-scatter.5.cloned.1.call-start
  111.7 1.6 fusion.74
  113.4 1.8 %collective-permute-start.9 = (bf16[2,128,1024]{2,1,0:T(8,128)(2,1)S(1)}, bf16[2,128,1024]{2,1,0:T(8,128)(2,1)S(1)}, u32[]{:S(2)}, u32[]{:S(2)}) collective-permute-start(bf16[2,128,1024]{2,1,0:T(8,128)(2,1)S(1)} %fusion.74), channel_id=1, source_target_pairs={{0,2},{2,0},{4,6},{6,4},{8,10},{10,8},{12,14},{14,12},{1,3},{3,1},... | collective-permute-start | bytes 1572872 | tf_op jit(solution)/shard_map/ppermute | solution.py:20
  115.2 8.8 %multiply_convert_fusion = bf16[1024,2048]{1,0:T(8,128)(2,1)S(1)} fusion(f32[1024,64]{1,0:T(8,128)} %fusion.61, f32[64,2048]{1,0:T(8,128)} %param.14, f32[1024]{0:T(1024)} %iota_convert_fusion, f32[2048]{0:T(1024)S(1)} %copy-done.18), kind=kOutput, calls=%fused_computation.1 | convolution fusion | flops 1616904192 | bytes 4993024 | tf_op jit(solution)/shard_map/dot_general | solution.py:92
  124.0 0.2 pad_maximum_fusion.3
  124.2 0.3 collective-permute-done.9
  124.6 2.4 %collective-permute-start.10 = (bf16[2,128,1024]{2,1,0:T(8,128)(2,1)S(1)}, bf16[2,128,1024]{2,1,0:T(8,128)(2,1)S(1)}, u32[]{:S(2)}, u32[]{:S(2)}) collective-permute-start(bf16[2,128,1024]{2,1,0:T(8,128)(2,1)S(1)} %fusion.75), channel_id=1, source_target_pairs={{0,2},{2,0},{4,6},{6,4},{8,10},{10,8},{12,14},{14,12},{1,3},{3,1},... | collective-permute-start | bytes 1572872 | tf_op jit(solution)/shard_map/ppermute | solution.py:20
  126.9 5.6 %convert_bitcast_fusion = bf16[4,512,2048]{2,1,0:T(8,128)(2,1)} fusion(bf16[4,256,2048]{2,1,0:T(8,128)(2,1)S(1)} %bitcast.174, bf16[256,256]{1,0:T(8,128)(2,1)S(1)} %select_convert_fusion.4, bf16[256,256]{1,0:T(8,128)(2,1)S(1)} %fusion.90), kind=kOutput, calls=%fused_computation | convolution fusion | flops 2152202240 | bytes 12845056 | tf_op jit(solution)/shard_map/fs,jsc->jfc/dot_general | solution.py:115
  132.6 0.3 fusion.65
  132.8 2.1 %collective-permute-done.10 = bf16[2,128,1024]{2,1,0:T(8,128)(2,1)S(1)} collective-permute-done((bf16[2,128,1024]{2,1,0:T(8,128)(2,1)S(1)}, bf16[2,128,1024]{2,1,0:T(8,128)(2,1)S(1)}, u32[]{:S(2)}, u32[]{:S(2)}) %collective-permute-start.10) | collective-permute-done | bytes 524320 | tf_op jit(solution)/shard_map/ppermute | solution.py:20
  135.0 0.3 fusion.64
  135.2 1.1 pad_maximum_fusion.5
  136.4 9.5 %fusion.6 = bf16[256,2048]{1,0:T(8,128)(2,1)S(1)} fusion(f32[256]{0:T(256)S(1)} %compare_select_fusion, pred[256]{0:T(512)(128)(4,1)S(1)} %iota_compare_fusion, bf16[4,512,2048]{2,1,0:T(8,128)(2,1)} %convert_bitcast_fusion, bf16[512,2048]{1,0:T(8,128)(2,1)} %copy-done.9, bf16[512,2048]{1,0:T(8,128)(2,1)} %convolution_convert_fusion.5, ...), kind=kLoop, calls=%fused_computation.59 | loop fusion | flops 28311552 | bytes 19924224 | tf_op jit(solution)/shard_map/convert_element_type | solution.py:159
  146.0 6.8 %fusion.12 = bf16[256,2048]{1,0:T(8,128)(2,1)S(1)} fusion(f32[256]{0:T(256)S(1)} %compare_select_fusion, pred[256]{0:T(512)(128)(4,1)S(1)} %iota_compare_fusion, bf16[4,512,2048]{2,1,0:T(8,128)(2,1)} %convert_bitcast_fusion, bf16[512,2048]{1,0:T(8,128)(2,1)S(1)} %copy-done.10, bf16[512,2048]{1,0:T(8,128)(2,1)S(1)} %copy-done.8, ...), kind=kLoop, calls=%fused_computation.65 | loop fusion | flops 30408704 | bytes 19924224 | tf_op jit(solution)/shard_map/convert_element_type | solution.py:160
  152.8 1.7 convolution_convert_fusion.6
  154.5 12.7 %reduce-scatter.5.cloned.1.call-done = bf16[1,128,1024]{2,1,0:T(8,128)(2,1)} async-done(((bf16[4,128,1024]{2,1,0:T(8,128)(2,1)}), bf16[1,128,1024]{2,1,0:T(8,128)(2,1)}) %reduce-scatter.5.cloned.1.call-update) | async-done | bytes 262160 | tf_op jit(solution)/shard_map/reduce_scatter | solution.py:206
  167.2 2.1 %maximum_convert_fusion = f32[128,2048]{1,0:T(8,128)} fusion(bf16[128,1024]{1,0:T(8,128)(2,1)} %bitcast.176, bf16[128,1024]{1,0:T(8,128)(2,1)} %bitcast.175), kind=kLoop, calls=%fused_computation.161 | loop fusion | flops 1048576 | bytes 1572864 | tf_op jit(solution)/shard_map/convert_element_type | solution.py:213
  (62 shorter events, 0.7 us)
Async XLA Ops:
  7.2 12.1 %copy-start = (bf16[256,2048]{1,0:T(8,128)(2,1)S(1)}, bf16[256,2048]{1,0:T(8,128)(2,1)}, u32[]{:S(2)}) copy-start(bf16[256,2048]{1,0:T(8,128)(2,1)} %param.8) | copy-start | bytes 3145732
  7.2 7.4 %copy-start.12 = (bf16[256,2048]{1,0:T(8,128)(2,1)S(1)}, bf16[256,2048]{1,0:T(8,128)(2,1)}, u32[]{:S(2)}) copy-start(bf16[256,2048]{1,0:T(8,128)(2,1)} %param.9) | copy-start | bytes 3145732
  7.2 147.3 %reduce-scatter.3.cloned.1.call-start = ((), (), s32[]{:S(2)}) async-start(), calls=%async_computation.2 | async-start | bytes 1310720 | tf_op jit(solution)/shard_map/reduce_scatter | solution.py:206
  7.2 51.3 %collective-permute-start = (bf16[256,2048]{1,0:T(8,128)(2,1)}, bf16[256,2048]{1,0:T(8,128)(2,1)}, u32[]{:S(2)}, u32[]{:S(2)}) collective-permute-start(bf16[256,2048]{1,0:T(8,128)(2,1)} %param.9), channel_id=1, source_target_pairs={{2,0},{6,4},{10,8},{14,12},{3,1},{7,5},{11,9},{15,13},{18,16},{22,... | collective-permute-start | bytes 3145736 | tf_op jit(solution)/shard_map/ppermute | solution.py:20
  10.7 5.9 %copy-start.16 = (f32[33,64]{1,0:T(8,128)S(1)}, f32[33,64]{1,0:T(8,128)}, u32[]{:S(2)}) copy-start(f32[33,64]{1,0:T(8,128)} %param.10) | copy-start | bytes 25348
  10.7 5.9 %copy-start.19 = (f32[64]{0:T(128)S(1)}, f32[64]{0:T(128)}, u32[]{:S(2)}) copy-start(f32[64]{0:T(128)} %param.13) | copy-start | bytes 772
  10.7 5.9 %copy-start.20 = (f32[64]{0:T(128)S(1)}, f32[64]{0:T(128)}, u32[]{:S(2)}) copy-start(f32[64]{0:T(128)} %param.11) | copy-start | bytes 772
  10.7 17.0 %collective-permute-start.1 = (bf16[256,1024]{1,0:T(8,128)(2,1)S(1)}, bf16[256,1024]{1,0:T(8,128)(2,1)S(1)}, u32[]{:S(2)}, u32[]{:S(2)}) collective-permute-start(bf16[256,1024]{1,0:T(8,128)(2,1)S(1)} %get-tuple-element.29), channel_id=1, source_target_pairs={{4,0},{6,2},{8,4},{10,6},{12,8},{14,10},{5,1},{7,3},{9,5},{11,7},{... | collective-permute-start | bytes 1572872 | tf_op jit(solution)/shard_map/ppermute | solution.py:15
  16.7 17.5 %copy-start.17 = (f32[2048]{0:T(1024)S(1)}, f32[2048]{0:T(1024)}, u32[]{:S(2)}) copy-start(f32[2048]{0:T(1024)} %param.15) | copy-start | bytes 24580
  27.7 15.3 %collective-permute-start.3 = (bf16[256,1024]{1,0:T(8,128)(2,1)}, bf16[256,1024]{1,0:T(8,128)(2,1)S(1)}, u32[]{:S(2)}, u32[]{:S(2)}) collective-permute-start(bf16[256,1024]{1,0:T(8,128)(2,1)} %get-tuple-element.8), channel_id=1, source_target_pairs={{4,0},{6,2},{8,4},{10,6},{12,8},{14,10},{5,1},{7,3},{9,5},{11,7},{... | collective-permute-start | bytes 1572872 | tf_op jit(solution)/shard_map/ppermute | solution.py:15
  29.0 18.3 %collective-permute-start.2 = (bf16[256,1024]{1,0:T(8,128)(2,1)S(1)}, bf16[256,1024]{1,0:T(8,128)(2,1)S(1)}, u32[]{:S(2)}, u32[]{:S(2)}) collective-permute-start(bf16[256,1024]{1,0:T(8,128)(2,1)S(1)} %collective-permute-done.1), channel_id=1, source_target_pairs={{0,2},{2,0},{4,6},{6,4},{8,10},{10,8},{12,14},{14,12},{1,3},{3,1},... | collective-permute-start | bytes 1572872 | tf_op jit(solution)/shard_map/ppermute | solution.py:20
  43.0 14.4 %collective-permute-start.4 = (bf16[256,1024]{1,0:T(8,128)(2,1)S(1)}, bf16[256,1024]{1,0:T(8,128)(2,1)S(1)}, u32[]{:S(2)}, u32[]{:S(2)}) collective-permute-start(bf16[256,1024]{1,0:T(8,128)(2,1)S(1)} %collective-permute-done.3), channel_id=1, source_target_pairs={{0,2},{2,0},{4,6},{6,4},{8,10},{10,8},{12,14},{14,12},{1,3},{3,1},... | collective-permute-start | bytes 1572872 | tf_op jit(solution)/shard_map/ppermute | solution.py:20
  46.0 24.7 %collective-permute-start.6 = (bf16[256,2048]{1,0:T(8,128)(2,1)S(1)}, bf16[256,2048]{1,0:T(8,128)(2,1)S(1)}, u32[]{:S(2)}, u32[]{:S(2)}) collective-permute-start(bf16[256,2048]{1,0:T(8,128)(2,1)S(1)} %constant_dynamic-update-slice_fusion.2), channel_id=1, source_target_pairs={{4,0},{6,2},{8,4},{10,6},{12,8},{14,10},{5,1},{7,3},{9,5},{11,7},{... | collective-permute-start | bytes 3145736 | tf_op jit(solution)/shard_map/ppermute | solution.py:15
  48.1 24.1 %copy-start.4 = (bf16[512,2048]{1,0:T(8,128)(2,1)}, bf16[512,2048]{1,0:T(8,128)(2,1)S(1)}, u32[]{:S(2)}) copy-start(bf16[512,2048]{1,0:T(8,128)(2,1)S(1)} %convolution_convert_fusion.3) | copy-start | bytes 6291460
  57.5 3.0 %copy-start.6 = (bf16[512,2048]{1,0:T(8,128)(2,1)S(1)}, bf16[512,2048]{1,0:T(8,128)(2,1)}, u32[]{:S(2)}) copy-start(bf16[512,2048]{1,0:T(8,128)(2,1)} %convolution_convert_fusion) | copy-start | bytes 6291460
  57.5 13.9 %collective-permute-start.5 = (bf16[256,2048]{1,0:T(8,128)(2,1)S(1)}, bf16[256,2048]{1,0:T(8,128)(2,1)S(1)}, u32[]{:S(2)}, u32[]{:S(2)}) collective-permute-start(bf16[256,2048]{1,0:T(8,128)(2,1)S(1)} %constant_dynamic-update-slice_fusion), channel_id=1, source_target_pairs={{6,2},{10,6},{14,10},{7,3},{11,7},{15,11},{22,18},{26,22},{30,26},... | collective-permute-start | bytes 3145736 | tf_op jit(solution)/shard_map/ppermute | solution.py:42
  60.5 1.7 copy-start.7
  62.2 1.7 copy-start.14
  66.2 12.7 %collective-permute-start.7 = (bf16[2,128,1024]{2,1,0:T(8,128)(2,1)S(1)}, bf16[2,128,1024]{2,1,0:T(8,128)(2,1)S(1)}, u32[]{:S(2)}, u32[]{:S(2)}) collective-permute-start(bf16[2,128,1024]{2,1,0:T(8,128)(2,1)S(1)} %fusion.72), channel_id=1, source_target_pairs={{0,2},{2,0},{4,6},{6,4},{8,10},{10,8},{12,14},{14,12},{1,3},{3,1},... | collective-permute-start | bytes 1572872 | tf_op jit(solution)/shard_map/ppermute | solution.py:20
  71.4 2.5 %copy-start.9 = (bf16[512,2048]{1,0:T(8,128)(2,1)}, bf16[512,2048]{1,0:T(8,128)(2,1)S(1)}, u32[]{:S(2)}) copy-start(bf16[512,2048]{1,0:T(8,128)(2,1)S(1)} %convolution_convert_fusion.1) | copy-start | bytes 6291460
  72.2 1.8 copy-start.2
  78.9 31.1 %collective-permute-start.8 = (bf16[2,128,1024]{2,1,0:T(8,128)(2,1)S(1)}, bf16[2,128,1024]{2,1,0:T(8,128)(2,1)S(1)}, u32[]{:S(2)}, u32[]{:S(2)}) collective-permute-start(bf16[2,128,1024]{2,1,0:T(8,128)(2,1)S(1)} %fusion.73), channel_id=1, source_target_pairs={{0,2},{2,0},{4,6},{6,4},{8,10},{10,8},{12,14},{14,12},{1,3},{3,1},... | collective-permute-start | bytes 1572872 | tf_op jit(solution)/shard_map/ppermute | solution.py:20
  110.3 4.9 %copy-start.18 = (f32[2048]{0:T(1024)S(1)}, f32[2048]{0:T(1024)}, u32[]{:S(2)}) copy-start(f32[2048]{0:T(1024)} %neg.7) | copy-start | bytes 24580
  111.4 55.8 %reduce-scatter.5.cloned.1.call-start = ((), (), s32[]{:S(2)}) async-start(), calls=%async_computation.3 | async-start | bytes 1310720 | tf_op jit(solution)/shard_map/reduce_scatter | solution.py:206
  113.4 10.6 %copy-start.13 = (f32[256,1024]{1,0:T(8,128)S(1)}, f32[256,1024]{1,0:T(8,128)}, u32[]{:S(2)}) copy-start(f32[256,1024]{1,0:T(8,128)} %get-tuple-element.25) | copy-start | bytes 3145732
  113.4 11.2 %collective-permute-start.9 = (bf16[2,128,1024]{2,1,0:T(8,128)(2,1)S(1)}, bf16[2,128,1024]{2,1,0:T(8,128)(2,1)S(1)}, u32[]{:S(2)}, u32[]{:S(2)}) collective-permute-start(bf16[2,128,1024]{2,1,0:T(8,128)(2,1)S(1)} %fusion.74), channel_id=1, source_target_pairs={{0,2},{2,0},{4,6},{6,4},{8,10},{10,8},{12,14},{14,12},{1,3},{3,1},... | collective-permute-start | bytes 1572872 | tf_op jit(solution)/shard_map/ppermute | solution.py:20
  124.6 10.4 %collective-permute-start.10 = (bf16[2,128,1024]{2,1,0:T(8,128)(2,1)S(1)}, bf16[2,128,1024]{2,1,0:T(8,128)(2,1)S(1)}, u32[]{:S(2)}, u32[]{:S(2)}) collective-permute-start(bf16[2,128,1024]{2,1,0:T(8,128)(2,1)S(1)} %fusion.75), channel_id=1, source_target_pairs={{0,2},{2,0},{4,6},{6,4},{8,10},{10,8},{12,14},{14,12},{1,3},{3,1},... | collective-permute-start | bytes 1572872 | tf_op jit(solution)/shard_map/ppermute | solution.py:20
  126.9 5.6 %copy-start.11 = (f32[512,1024]{1,0:T(8,128)S(1)}, f32[512,1024]{1,0:T(8,128)}, u32[]{:S(2)}) copy-start(f32[512,1024]{1,0:T(8,128)} %pad_maximum_fusion.2) | copy-start | bytes 6291460
  136.3 9.6 %copy-start.3 = (bf16[512,2048]{1,0:T(8,128)(2,1)S(1)}, bf16[512,2048]{1,0:T(8,128)(2,1)}, u32[]{:S(2)}) copy-start(bf16[512,2048]{1,0:T(8,128)(2,1)} %copy-done.2) | copy-start | bytes 6291460
  136.3 9.6 %copy-start.5 = (bf16[512,2048]{1,0:T(8,128)(2,1)S(1)}, bf16[512,2048]{1,0:T(8,128)(2,1)}, u32[]{:S(2)}) copy-start(bf16[512,2048]{1,0:T(8,128)(2,1)} %copy-done.4) | copy-start | bytes 6291460
  136.3 9.6 %copy-start.8 = (bf16[512,2048]{1,0:T(8,128)(2,1)S(1)}, bf16[512,2048]{1,0:T(8,128)(2,1)}, u32[]{:S(2)}) copy-start(bf16[512,2048]{1,0:T(8,128)(2,1)} %convolution_convert_fusion.5) | copy-start | bytes 6291460
  136.4 9.6 %copy-start.10 = (bf16[512,2048]{1,0:T(8,128)(2,1)S(1)}, bf16[512,2048]{1,0:T(8,128)(2,1)}, u32[]{:S(2)}) copy-start(bf16[512,2048]{1,0:T(8,128)(2,1)} %copy-done.9) | copy-start | bytes 6291460
  145.9 6.8 %copy-start.15 = (bf16[256,256]{1,0:T(8,128)(2,1)S(1)}, bf16[256,256]{1,0:T(8,128)(2,1)}, u32[]{:S(2)}) copy-start(bf16[256,256]{1,0:T(8,128)(2,1)} %get-tuple-element.33) | copy-start | bytes 393220
  145.9 23.4 %copy-start.1 = (bf16[256,2048]{1,0:T(8,128)(2,1)S(1)}, bf16[256,2048]{1,0:T(8,128)(2,1)}, u32[]{:S(2)}) copy-start(bf16[256,2048]{1,0:T(8,128)(2,1)} %param.8) | copy-start | bytes 3145732
Sparse Core Ops, SparseCore 0:
  111.6 26.7 reduce-scatter.2
  141.4 25.7 reduce-scatter.4

commit v8 on v7

--- a/solution.py
+++ b/solution.py
@@ -197,10 +197,11 @@
             staged = jnp.concatenate(chosen, axis=0).reshape(-1, 2, share, span)
             mine = jnp.where(side_zero, staged[:, 0], staged[:, 1])
             theirs = jnp.where(side_zero, staged[:, 1], staged[:, 0]).astype(jnp.bfloat16)
-            if gate is not None:
+            if gate is not None and part == 0:
                 theirs, gate = lax.optimization_barrier((theirs, gate))
             received = swap_pairs(theirs, SEQ_AXES, 0, 1)
-            gate = received
+            if part == parts - 1:
+                gate = received
             reduced.append(mine + received.astype(jnp.float32))
         outputs.append(
             lax.psum_scatter(

time: 177 us -> 182 us (1.028)
  waiting for transfers between devices: 46.8 us -> 54.2 us
  local copies, waits for them, and re-layouts: 4.03 us -> 8.13 us
  other arithmetic: 37.9 us -> 34.4 us
  starting transfers between devices: 39.2 us -> 37.2 us
    ppermute x7, waiting for transfers between devices: 18.9 us -> 29.1 us  [swap_pairs(): lax.ppermute(value, axis, [(source, source ^ 1) for source in range(from_...]
    reduce_scatter x2, waiting for transfers between devices: 12.7 us -> 8.19 us  [on_device(): lax.psum_scatter(jnp.concatenate(reduced, axis=0).astype(jnp.bfloat16), '...]
    slice x4, local copies, waits for them, and re-layouts: 1.73 us -> 4.59 us  [on_device(): rows[:, lane * span:(lane + 1) * span]]
    ppermute x7, starting transfers between devices: 33.9 us -> 32 us  [swap_pairs(): lax.ppermute(value, axis, [(source, source ^ 1) for source in range(from_...]
    ppermute x3, waiting for transfers between devices: 15.1 us -> 17 us  [from_behind(): lax.ppermute(value, axis, [(source, source + steps) for source in range(l...]
  transfers between devices with their start and end apart: 13 -> 13, of which waited for: 9 -> 8; matrix products, arithmetic and copies ran while one was open for 41% -> 39% of each run, Pallas kernels for 0% -> 0%
where the time goes in v8:
time: 182 us
  waiting for transfers between devices  54.2 us (30%)
  starting transfers between devices  37.2 us (20%)
  other arithmetic  34.4 us (19%)
  matrix products  32.9 us (18%)
  between operations  14.7 us (8%)
  local copies, waits for them, and re-layouts  8.13 us (4%)
    ppermute x7, starting transfers between devices, swap_pairs(): lax.ppermute(value, axis, [(source, source ^ 1) for source in range(from_...  32 us
    ppermute x7, waiting for transfers between devices, swap_pairs(): lax.ppermute(value, axis, [(source, source ^ 1) for source in range(from_...  29.1 us
    ppermute x3, waiting for transfers between devices, from_behind(): lax.ppermute(value, axis, [(source, source + steps) for source in range(l...  17 us
    convert_element_type x1, other arithmetic, on_device(): mix_re = sum_re.astype(jnp.bfloat16)  9.52 us
    dot_general x1, matrix products, filter_taps(): jnp.dot(second_act, w_out, precision=lax.Precision.HIGHEST, preferred_ele...  8.87 us
    dot_general x6, matrix products, slab_spectrum(): jnp.dot(jnp.concatenate([fwd_re, fwd_im], axis=0), slab_data, preferred_e...  8.23 us
    reduce_scatter x2, waiting for transfers between devices, on_device(): lax.psum_scatter(jnp.concatenate(reduced, axis=0).astype(jnp.bfloat16), '...  8.19 us
    another operation x8, other arithmetic  7.82 us
  transfers between devices with their start and end apart: 13, of which 8 were waited for; matrix products, arithmetic and copies ran while one was open for 39% of the time, Pallas kernels for 0%

profile of v8, /device:TPU:0, one launch (start us, length us, event | category | flops | bytes accessed | tf_op | source)
XLA Modules:
  0.0 181.5 jit_solution(2157863704465162519)
XLA Ops:
  7.2 1.4 collective-permute-start
  8.7 2.1 %fusion.109 = (bf16[256,1024]{1,0:T(8,128)(2,1)}, bf16[256,1024]{1,0:T(8,128)(2,1)S(1)}) fusion(bf16[256,2048]{1,0:T(8,128)(2,1)} %param.9), kind=kLoop, calls=%fused_computation.217 | loop fusion | bytes 2097152 | tf_op jit(solution)/shard_map/slice | solution.py:34
  10.7 1.3 collective-permute-start.1
  12.1 1.0 fusion.90
  13.0 1.0 select_convert_fusion.4
  14.1 1.8 %multiply_convert_fusion.1 = (bf16[256,256]{1,0:T(8,128)(2,1)S(1)}, bf16[256,256]{1,0:T(8,128)(2,1)}) fusion(f32[256]{0:T(256)S(1)} %compare_select_fusion, pred[256]{0:T(512)(128)(4,1)S(1)} %iota_compare_fusion, f32[256]{0:T(256)S(1)} %broadcast_select_fusion), kind=kLoop, calls=%fused_computation.172 | loop fusion | flops 1376256 | bytes 264448 | tf_op jit(solution)/shard_map/convert_element_type | solution.py:64
  15.9 2.0 %convolution_convert_fusion.5 = bf16[512,2048]{1,0:T(8,128)(2,1)} fusion(bf16[256,2048]{1,0:T(8,128)(2,1)S(1)} %copy-done.11, bf16[256,256]{1,0:T(8,128)(2,1)S(1)} %select_convert_fusion.4, bf16[256,256]{1,0:T(8,128)(2,1)S(1)} %fusion.90), kind=kOutput, calls=%fused_computation.23 | convolution fusion | flops 538443776 | bytes 3407872 | tf_op jit(solution)/shard_map/dot_general | solution.py:107
  18.0 0.3 fusion.98
  18.3 2.1 %convolution_convert_fusion = bf16[512,2048]{1,0:T(8,128)(2,1)} fusion(bf16[256,2048]{1,0:T(8,128)(2,1)S(1)} %copy-done, bf16[256,256]{1,0:T(8,128)(2,1)S(1)} %select_convert_fusion.4, bf16[256,256]{1,0:T(8,128)(2,1)S(1)} %fusion.90), kind=kOutput, calls=%fused_computation.18 | convolution fusion | flops 538443776 | bytes 3407872 | tf_op jit(solution)/shard_map/dot_general | solution.py:107
  20.4 7.2 %collective-permute-done.1 = bf16[256,1024]{1,0:T(8,128)(2,1)S(1)} collective-permute-done((bf16[256,1024]{1,0:T(8,128)(2,1)S(1)}, bf16[256,1024]{1,0:T(8,128)(2,1)S(1)}, u32[]{:S(2)}, u32[]{:S(2)}) %collective-permute-start.1) | collective-permute-done | bytes 524320 | tf_op jit(solution)/shard_map/ppermute | solution.py:15
  27.6 1.3 collective-permute-start.3
  28.9 3.4 %collective-permute-start.2 = (bf16[256,1024]{1,0:T(8,128)(2,1)S(1)}, bf16[256,1024]{1,0:T(8,128)(2,1)S(1)}, u32[]{:S(2)}, u32[]{:S(2)}) collective-permute-start(bf16[256,1024]{1,0:T(8,128)(2,1)S(1)} %collective-permute-done.1), channel_id=1, source_target_pairs={{0,2},{2,0},{4,6},{6,4},{8,10},{10,8},{12,14},{14,12},{1,3},{3,1},... | collective-permute-start | bytes 1572872 | tf_op jit(solution)/shard_map/ppermute | solution.py:20
  32.3 0.6 iota_convert_fusion
  32.9 2.5 %fusion.63 = f32[1024,64]{1,0:T(8,128)S(1)} fusion(f32[33,64]{1,0:T(8,128)S(1)} %copy-done.19, f32[64]{0:T(128)S(1)} %copy-done.23, f32[64]{0:T(128)S(1)} %copy-done.21, f32[1024,16]{0,1:T(8,128)S(1)} %get-tuple-element.27, f32[1024,16]{0,1:T(8,128)S(1)} %get-tuple-element.26, f32[1024,1]{0,1:T(1,128)S(1)} %convert_multiply_fusion.38), kind=kOutput, calls=%fused_computation.122 | convolution fusion | flops 26150912 | bytes 406272 | tf_op jit(solution)/shard_map/dot_general | solution.py:80
  35.5 7.4 %collective-permute-done.3 = bf16[256,1024]{1,0:T(8,128)(2,1)S(1)} collective-permute-done((bf16[256,1024]{1,0:T(8,128)(2,1)}, bf16[256,1024]{1,0:T(8,128)(2,1)S(1)}, u32[]{:S(2)}, u32[]{:S(2)}) %collective-permute-start.3) | collective-permute-done | bytes 524320 | tf_op jit(solution)/shard_map/ppermute | solution.py:15
  42.9 2.9 %collective-permute-start.4 = (bf16[256,1024]{1,0:T(8,128)(2,1)S(1)}, bf16[256,1024]{1,0:T(8,128)(2,1)S(1)}, u32[]{:S(2)}, u32[]{:S(2)}) collective-permute-start(bf16[256,1024]{1,0:T(8,128)(2,1)S(1)} %collective-permute-done.3), channel_id=1, source_target_pairs={{0,2},{2,0},{4,6},{6,4},{8,10},{10,8},{12,14},{14,12},{1,3},{3,1},... | collective-permute-start | bytes 1572872 | tf_op jit(solution)/shard_map/ppermute | solution.py:20
  45.8 1.3 collective-permute-start.6
  47.2 0.7 convolution_convert_fusion.3
  47.9 9.6 %collective-permute-done.4 = bf16[256,1024]{1,0:T(8,128)(2,1)S(1)} collective-permute-done((bf16[256,1024]{1,0:T(8,128)(2,1)S(1)}, bf16[256,1024]{1,0:T(8,128)(2,1)S(1)}, u32[]{:S(2)}, u32[]{:S(2)}) %collective-permute-start.4) | collective-permute-done | bytes 524320 | tf_op jit(solution)/shard_map/ppermute | solution.py:20
  57.5 1.0 collective-permute-start.5
  58.6 2.0 %convolution_convert_fusion.4 = bf16[512,2048]{1,0:T(8,128)(2,1)S(1)} fusion(bf16[256,2048]{1,0:T(8,128)(2,1)} %collective-permute-done, bf16[256,2048]{1,0:T(8,128)(2,1)S(1)} %constant_dynamic-update-slice_fusion, pred[]{:T(512)S(6)} %eq.91, bf16[256,256]{1,0:T(8,128)(2,1)S(1)} %select_convert_fusion.4, bf16[256,256]{1,0:T(8,128)(2,1)S(1)} %fusion.90), kind=kOutput, calls=%fused_computation.22 | convolution fusion | flops 538968064 | bytes 4456449 | tf_op jit(solution)/shard_map/dot_general | solution.py:107
  60.5 1.7 fusion.28
  62.2 1.7 fusion.23
  63.9 0.7 fusion.49
  64.7 1.2 fusion.106
  65.9 0.7 fusion.45
  66.6 1.2 fusion.105
  67.7 0.2 pad_maximum_fusion
  68.0 0.1 fusion.72
  68.2 2.4 %collective-permute-done.6 = bf16[256,2048]{1,0:T(8,128)(2,1)S(1)} collective-permute-done((bf16[256,2048]{1,0:T(8,128)(2,1)S(1)}, bf16[256,2048]{1,0:T(8,128)(2,1)S(1)}, u32[]{:S(2)}, u32[]{:S(2)}) %collective-permute-start.6) | collective-permute-done | bytes 1048608 | tf_op jit(solution)/shard_map/ppermute | solution.py:15
  70.5 0.7 convolution_convert_fusion.1
  71.3 0.7 convolution_convert_fusion.2
  72.0 1.7 fusion.33
  73.8 1.7 fusion.38
  75.5 0.7 fusion.57
  76.3 1.1 fusion.108
  77.4 0.7 fusion.53
  78.1 1.1 fusion.107
  79.2 0.2 pad_maximum_fusion.1
  79.5 22.1 %collective-permute-start.8 = (bf16[2,128,1024]{2,1,0:T(8,128)(2,1)S(1)}, bf16[2,128,1024]{2,1,0:T(8,128)(2,1)S(1)}, u32[]{:S(2)}, u32[]{:S(2)}) collective-permute-start(bf16[2,128,1024]{2,1,0:T(8,128)(2,1)S(1)} %fusion.73), channel_id=1, source_target_pairs={{0,2},{2,0},{4,6},{6,4},{8,10},{10,8},{12,14},{14,12},{1,3},{3,1},... | collective-permute-start | bytes 1572872 | tf_op jit(solution)/shard_map/ppermute | solution.py:20
  101.6 3.1 %fusion.61 = f32[1024,64]{1,0:T(8,128)} fusion(f32[1024,64]{1,0:T(8,128)S(1)} %fusion.63, f32[64,64]{1,0:T(8,128)S(1)} %copy-done.18, f32[64]{0:T(128)S(1)} %copy-done.22), kind=kOutput, calls=%fused_computation.120 | convolution fusion | flops 50397184 | bytes 540928 | tf_op jit(solution)/shard_map/dot_general | solution.py:88
  104.6 0.3 fusion.67
  104.9 5.9 %collective-permute-done.8 = bf16[2,128,1024]{2,1,0:T(8,128)(2,1)S(1)} collective-permute-done((bf16[2,128,1024]{2,1,0:T(8,128)(2,1)S(1)}, bf16[2,128,1024]{2,1,0:T(8,128)(2,1)S(1)}, u32[]{:S(2)}, u32[]{:S(2)}) %collective-permute-start.8) | collective-permute-done | bytes 524320 | tf_op jit(solution)/shard_map/ppermute | solution.py:20
  110.8 0.3 fusion.66
  111.0 1.1 pad_maximum_fusion.4
  112.2 0.3 reduce-scatter.5.cloned.1.call-start
  112.5 8.9 %multiply_convert_fusion = bf16[1024,2048]{1,0:T(8,128)(2,1)S(1)} fusion(f32[1024,64]{1,0:T(8,128)} %fusion.61, f32[64,2048]{1,0:T(8,128)} %param.14, f32[1024]{0:T(1024)} %iota_convert_fusion, f32[2048]{0:T(1024)S(1)} %neg.7), kind=kOutput, calls=%fused_computation.1 | convolution fusion | flops 1616904192 | bytes 4993024 | tf_op jit(solution)/shard_map/dot_general | solution.py:92
  121.4 0.2 pad_maximum_fusion.2
  121.7 0.9 copy-done.14
  122.6 0.3 copy-done.15
  122.9 0.2 pad_maximum_fusion.3
  123.2 1.8 collective-permute-start.10
  125.0 0.3 collective-permute-start.9
  125.3 5.6 %convert_bitcast_fusion = bf16[4,512,2048]{2,1,0:T(8,128)(2,1)} fusion(bf16[4,256,2048]{2,1,0:T(8,128)(2,1)S(1)} %bitcast.174, bf16[256,256]{1,0:T(8,128)(2,1)S(1)} %select_convert_fusion.4, bf16[256,256]{1,0:T(8,128)(2,1)S(1)} %fusion.90), kind=kOutput, calls=%fused_computation | convolution fusion | flops 2152202240 | bytes 12845056 | tf_op jit(solution)/shard_map/fs,jsc->jfc/dot_general | solution.py:115
  131.0 7.2 %collective-permute-done.10 = bf16[2,128,1024]{2,1,0:T(8,128)(2,1)S(1)} collective-permute-done((bf16[2,128,1024]{2,1,0:T(8,128)(2,1)S(1)}, bf16[2,128,1024]{2,1,0:T(8,128)(2,1)S(1)}, u32[]{:S(2)}, u32[]{:S(2)}) %collective-permute-start.10) | collective-permute-done | bytes 524320 | tf_op jit(solution)/shard_map/ppermute | solution.py:20
  138.2 0.3 fusion.64
  138.4 6.4 %collective-permute-done.9 = bf16[2,128,1024]{2,1,0:T(8,128)(2,1)S(1)} collective-permute-done((bf16[2,128,1024]{2,1,0:T(8,128)(2,1)S(1)}, bf16[2,128,1024]{2,1,0:T(8,128)(2,1)S(1)}, u32[]{:S(2)}, u32[]{:S(2)}) %collective-permute-start.9) | collective-permute-done | bytes 524320 | tf_op jit(solution)/shard_map/ppermute | solution.py:20
  144.9 0.3 fusion.65
  145.1 1.1 pad_maximum_fusion.5
  146.3 9.5 %fusion.6 = bf16[256,2048]{1,0:T(8,128)(2,1)S(1)} fusion(f32[256]{0:T(256)S(1)} %compare_select_fusion, pred[256]{0:T(512)(128)(4,1)S(1)} %iota_compare_fusion, bf16[4,512,2048]{2,1,0:T(8,128)(2,1)} %convert_bitcast_fusion, bf16[512,2048]{1,0:T(8,128)(2,1)} %copy-done.9, bf16[512,2048]{1,0:T(8,128)(2,1)} %convolution_convert_fusion.5, ...), kind=kLoop, calls=%fused_computation.59 | loop fusion | flops 28311552 | bytes 19924224 | tf_op jit(solution)/shard_map/convert_element_type | solution.py:159
  155.9 6.8 %fusion.12 = bf16[256,2048]{1,0:T(8,128)(2,1)S(1)} fusion(f32[256]{0:T(256)S(1)} %compare_select_fusion, pred[256]{0:T(512)(128)(4,1)S(1)} %iota_compare_fusion, bf16[4,512,2048]{2,1,0:T(8,128)(2,1)} %convert_bitcast_fusion, bf16[512,2048]{1,0:T(8,128)(2,1)S(1)} %copy-done.10, bf16[512,2048]{1,0:T(8,128)(2,1)S(1)} %copy-done.8, ...), kind=kLoop, calls=%fused_computation.65 | loop fusion | flops 30408704 | bytes 19924224 | tf_op jit(solution)/shard_map/convert_element_type | solution.py:160
  162.7 1.7 convolution_convert_fusion.6
  164.4 8.2 %reduce-scatter.5.cloned.1.call-done = bf16[1,128,1024]{2,1,0:T(8,128)(2,1)} async-done(((bf16[4,128,1024]{2,1,0:T(8,128)(2,1)}), bf16[1,128,1024]{2,1,0:T(8,128)(2,1)}) %reduce-scatter.5.cloned.1.call-update) | async-done | bytes 262160 | tf_op jit(solution)/shard_map/reduce_scatter | solution.py:207
  172.6 2.1 %maximum_convert_fusion = f32[128,2048]{1,0:T(8,128)} fusion(bf16[128,1024]{1,0:T(8,128)(2,1)} %bitcast.176, bf16[128,1024]{1,0:T(8,128)(2,1)} %bitcast.175), kind=kLoop, calls=%fused_computation.161 | loop fusion | flops 1048576 | bytes 1572864 | tf_op jit(solution)/shard_map/convert_element_type | solution.py:214
  (68 shorter events, 0.7 us)
Async XLA Ops:
  7.2 11.1 %copy-start = (bf16[256,2048]{1,0:T(8,128)(2,1)S(1)}, bf16[256,2048]{1,0:T(8,128)(2,1)}, u32[]{:S(2)}) copy-start(bf16[256,2048]{1,0:T(8,128)(2,1)} %param.8) | copy-start | bytes 3145732
  7.2 8.7 %copy-start.11 = (bf16[256,2048]{1,0:T(8,128)(2,1)S(1)}, bf16[256,2048]{1,0:T(8,128)(2,1)}, u32[]{:S(2)}) copy-start(bf16[256,2048]{1,0:T(8,128)(2,1)} %param.9) | copy-start | bytes 3145732
  7.2 157.2 %reduce-scatter.3.cloned.1.call-start = ((), (), s32[]{:S(2)}) async-start(), calls=%async_computation.2 | async-start | bytes 1310720 | tf_op jit(solution)/shard_map/reduce_scatter | solution.py:207
  7.2 51.3 %collective-permute-start = (bf16[256,2048]{1,0:T(8,128)(2,1)}, bf16[256,2048]{1,0:T(8,128)(2,1)}, u32[]{:S(2)}, u32[]{:S(2)}) collective-permute-start(bf16[256,2048]{1,0:T(8,128)(2,1)} %param.9), channel_id=1, source_target_pairs={{2,0},{6,4},{10,8},{14,12},{3,1},{7,5},{11,9},{15,13},{18,16},{22,... | collective-permute-start | bytes 3145736 | tf_op jit(solution)/shard_map/ppermute | solution.py:20
  10.7 16.8 %collective-permute-start.1 = (bf16[256,1024]{1,0:T(8,128)(2,1)S(1)}, bf16[256,1024]{1,0:T(8,128)(2,1)S(1)}, u32[]{:S(2)}, u32[]{:S(2)}) collective-permute-start(bf16[256,1024]{1,0:T(8,128)(2,1)S(1)} %get-tuple-element.25), channel_id=1, source_target_pairs={{4,0},{6,2},{8,4},{10,6},{12,8},{14,10},{5,1},{7,3},{9,5},{11,7},{... | collective-permute-start | bytes 1572872 | tf_op jit(solution)/shard_map/ppermute | solution.py:15
  18.0 14.9 %copy-start.20 = (f32[2048]{0:T(1024)S(1)}, f32[2048]{0:T(1024)}, u32[]{:S(2)}) copy-start(f32[2048]{0:T(1024)} %param.15) | copy-start | bytes 24580
  18.0 14.9 %copy-start.19 = (f32[33,64]{1,0:T(8,128)S(1)}, f32[33,64]{1,0:T(8,128)}, u32[]{:S(2)}) copy-start(f32[33,64]{1,0:T(8,128)} %param.10) | copy-start | bytes 25348
  18.0 14.9 %copy-start.21 = (f32[64]{0:T(128)S(1)}, f32[64]{0:T(128)}, u32[]{:S(2)}) copy-start(f32[64]{0:T(128)} %param.13) | copy-start | bytes 772
  18.0 14.9 %copy-start.23 = (f32[64]{0:T(128)S(1)}, f32[64]{0:T(128)}, u32[]{:S(2)}) copy-start(f32[64]{0:T(128)} %param.11) | copy-start | bytes 772
  27.6 15.3 %collective-permute-start.3 = (bf16[256,1024]{1,0:T(8,128)(2,1)}, bf16[256,1024]{1,0:T(8,128)(2,1)S(1)}, u32[]{:S(2)}, u32[]{:S(2)}) collective-permute-start(bf16[256,1024]{1,0:T(8,128)(2,1)} %get-tuple-element.6), channel_id=1, source_target_pairs={{4,0},{6,2},{8,4},{10,6},{12,8},{14,10},{5,1},{7,3},{9,5},{11,7},{... | collective-permute-start | bytes 1572872 | tf_op jit(solution)/shard_map/ppermute | solution.py:15
  28.9 18.3 %collective-permute-start.2 = (bf16[256,1024]{1,0:T(8,128)(2,1)S(1)}, bf16[256,1024]{1,0:T(8,128)(2,1)S(1)}, u32[]{:S(2)}, u32[]{:S(2)}) collective-permute-start(bf16[256,1024]{1,0:T(8,128)(2,1)S(1)} %collective-permute-done.1), channel_id=1, source_target_pairs={{0,2},{2,0},{4,6},{6,4},{8,10},{10,8},{12,14},{14,12},{1,3},{3,1},... | collective-permute-start | bytes 1572872 | tf_op jit(solution)/shard_map/ppermute | solution.py:20
  42.9 14.6 %collective-permute-start.4 = (bf16[256,1024]{1,0:T(8,128)(2,1)S(1)}, bf16[256,1024]{1,0:T(8,128)(2,1)S(1)}, u32[]{:S(2)}, u32[]{:S(2)}) collective-permute-start(bf16[256,1024]{1,0:T(8,128)(2,1)S(1)} %collective-permute-done.3), channel_id=1, source_target_pairs={{0,2},{2,0},{4,6},{6,4},{8,10},{10,8},{12,14},{14,12},{1,3},{3,1},... | collective-permute-start | bytes 1572872 | tf_op jit(solution)/shard_map/ppermute | solution.py:20
  45.8 24.7 %collective-permute-start.6 = (bf16[256,2048]{1,0:T(8,128)(2,1)S(1)}, bf16[256,2048]{1,0:T(8,128)(2,1)S(1)}, u32[]{:S(2)}, u32[]{:S(2)}) collective-permute-start(bf16[256,2048]{1,0:T(8,128)(2,1)S(1)} %constant_dynamic-update-slice_fusion.2), channel_id=1, source_target_pairs={{4,0},{6,2},{8,4},{10,6},{12,8},{14,10},{5,1},{7,3},{9,5},{11,7},{... | collective-permute-start | bytes 3145736 | tf_op jit(solution)/shard_map/ppermute | solution.py:15
  47.9 24.1 %copy-start.4 = (bf16[512,2048]{1,0:T(8,128)(2,1)}, bf16[512,2048]{1,0:T(8,128)(2,1)S(1)}, u32[]{:S(2)}) copy-start(bf16[512,2048]{1,0:T(8,128)(2,1)S(1)} %convolution_convert_fusion.3) | copy-start | bytes 6291460
  57.5 3.0 %copy-start.6 = (bf16[512,2048]{1,0:T(8,128)(2,1)S(1)}, bf16[512,2048]{1,0:T(8,128)(2,1)}, u32[]{:S(2)}) copy-start(bf16[512,2048]{1,0:T(8,128)(2,1)} %convolution_convert_fusion) | copy-start | bytes 6291460
  57.5 13.8 %collective-permute-start.5 = (bf16[256,2048]{1,0:T(8,128)(2,1)S(1)}, bf16[256,2048]{1,0:T(8,128)(2,1)S(1)}, u32[]{:S(2)}, u32[]{:S(2)}) collective-permute-start(bf16[256,2048]{1,0:T(8,128)(2,1)S(1)} %constant_dynamic-update-slice_fusion), channel_id=1, source_target_pairs={{6,2},{10,6},{14,10},{7,3},{11,7},{15,11},{22,18},{26,22},{30,26},... | collective-permute-start | bytes 3145736 | tf_op jit(solution)/shard_map/ppermute | solution.py:42
  60.5 1.7 copy-start.7
  62.2 1.7 copy-start.16
  68.1 36.5 %collective-permute-start.7 = (bf16[2,128,1024]{2,1,0:T(8,128)(2,1)S(1)}, bf16[2,128,1024]{2,1,0:T(8,128)(2,1)S(1)}, u32[]{:S(2)}, u32[]{:S(2)}) collective-permute-start(bf16[2,128,1024]{2,1,0:T(8,128)(2,1)S(1)} %fusion.72), channel_id=1, source_target_pairs={{0,2},{2,0},{4,6},{6,4},{8,10},{10,8},{12,14},{14,12},{1,3},{3,1},... | collective-permute-start | bytes 1572872 | tf_op jit(solution)/shard_map/ppermute | solution.py:20
  71.3 2.5 %copy-start.9 = (bf16[512,2048]{1,0:T(8,128)(2,1)}, bf16[512,2048]{1,0:T(8,128)(2,1)S(1)}, u32[]{:S(2)}) copy-start(bf16[512,2048]{1,0:T(8,128)(2,1)S(1)} %convolution_convert_fusion.1) | copy-start | bytes 6291460
  72.0 1.8 copy-start.2
  79.2 22.4 %copy-start.18 = (f32[64,64]{1,0:T(8,128)S(1)}, f32[64,64]{1,0:T(8,128)}, u32[]{:S(2)}) copy-start(f32[64,64]{1,0:T(8,128)} %param.12) | copy-start | bytes 49156
  79.2 22.4 %copy-start.22 = (f32[64]{0:T(128)S(1)}, f32[64]{0:T(128)}, u32[]{:S(2)}) copy-start(f32[64]{0:T(128)} %param.13) | copy-start | bytes 772
  79.5 31.3 %collective-permute-start.8 = (bf16[2,128,1024]{2,1,0:T(8,128)(2,1)S(1)}, bf16[2,128,1024]{2,1,0:T(8,128)(2,1)S(1)}, u32[]{:S(2)}, u32[]{:S(2)}) collective-permute-start(bf16[2,128,1024]{2,1,0:T(8,128)(2,1)S(1)} %fusion.73), channel_id=1, source_target_pairs={{0,2},{2,0},{4,6},{6,4},{8,10},{10,8},{12,14},{14,12},{1,3},{3,1},... | collective-permute-start | bytes 1572872 | tf_op jit(solution)/shard_map/ppermute | solution.py:20
  112.2 9.2 %copy-start.12 = (f32[256,1024]{1,0:T(8,128)S(1)}, f32[256,1024]{1,0:T(8,128)}, u32[]{:S(2)}) copy-start(f32[256,1024]{1,0:T(8,128)} %get-tuple-element.19) | copy-start | bytes 3145732
  112.2 60.4 %reduce-scatter.5.cloned.1.call-start = ((), (), s32[]{:S(2)}) async-start(), calls=%async_computation.3 | async-start | bytes 1310720 | tf_op jit(solution)/shard_map/reduce_scatter | solution.py:207
  112.4 8.9 %copy-start.13 = (f32[256,1024]{1,0:T(8,128)S(1)}, f32[256,1024]{1,0:T(8,128)}, u32[]{:S(2)}) copy-start(f32[256,1024]{1,0:T(8,128)} %get-tuple-element.17) | copy-start | bytes 3145732
  121.3 1.2 copy-start.14
  121.4 1.5 copy-start.15
  123.2 14.9 %collective-permute-start.10 = (bf16[2,128,1024]{2,1,0:T(8,128)(2,1)S(1)}, bf16[2,128,1024]{2,1,0:T(8,128)(2,1)S(1)}, u32[]{:S(2)}, u32[]{:S(2)}) collective-permute-start(bf16[2,128,1024]{2,1,0:T(8,128)(2,1)S(1)} %fusion.75), channel_id=1, source_target_pairs={{0,2},{2,0},{4,6},{6,4},{8,10},{10,8},{12,14},{14,12},{1,3},{3,1},... | collective-permute-start | bytes 1572872 | tf_op jit(solution)/shard_map/ppermute | solution.py:20
  125.0 19.8 %collective-permute-start.9 = (bf16[2,128,1024]{2,1,0:T(8,128)(2,1)S(1)}, bf16[2,128,1024]{2,1,0:T(8,128)(2,1)S(1)}, u32[]{:S(2)}, u32[]{:S(2)}) collective-permute-start(bf16[2,128,1024]{2,1,0:T(8,128)(2,1)S(1)} %fusion.74), channel_id=1, source_target_pairs={{0,2},{2,0},{4,6},{6,4},{8,10},{10,8},{12,14},{14,12},{1,3},{3,1},... | collective-permute-start | bytes 1572872 | tf_op jit(solution)/shard_map/ppermute | solution.py:20
  146.2 9.6 %copy-start.3 = (bf16[512,2048]{1,0:T(8,128)(2,1)S(1)}, bf16[512,2048]{1,0:T(8,128)(2,1)}, u32[]{:S(2)}) copy-start(bf16[512,2048]{1,0:T(8,128)(2,1)} %copy-done.2) | copy-start | bytes 6291460
  146.2 9.6 %copy-start.5 = (bf16[512,2048]{1,0:T(8,128)(2,1)S(1)}, bf16[512,2048]{1,0:T(8,128)(2,1)}, u32[]{:S(2)}) copy-start(bf16[512,2048]{1,0:T(8,128)(2,1)} %copy-done.4) | copy-start | bytes 6291460
  146.3 9.6 %copy-start.8 = (bf16[512,2048]{1,0:T(8,128)(2,1)S(1)}, bf16[512,2048]{1,0:T(8,128)(2,1)}, u32[]{:S(2)}) copy-start(bf16[512,2048]{1,0:T(8,128)(2,1)} %convolution_convert_fusion.5) | copy-start | bytes 6291460
  146.3 9.6 %copy-start.10 = (bf16[512,2048]{1,0:T(8,128)(2,1)S(1)}, bf16[512,2048]{1,0:T(8,128)(2,1)}, u32[]{:S(2)}) copy-start(bf16[512,2048]{1,0:T(8,128)(2,1)} %copy-done.9) | copy-start | bytes 6291460
  155.8 6.8 %copy-start.17 = (bf16[256,256]{1,0:T(8,128)(2,1)S(1)}, bf16[256,256]{1,0:T(8,128)(2,1)}, u32[]{:S(2)}) copy-start(bf16[256,256]{1,0:T(8,128)(2,1)} %get-tuple-element.29) | copy-start | bytes 393220
  155.8 18.8 %copy-start.1 = (bf16[256,2048]{1,0:T(8,128)(2,1)S(1)}, bf16[256,2048]{1,0:T(8,128)(2,1)}, u32[]{:S(2)}) copy-start(bf16[256,2048]{1,0:T(8,128)(2,1)} %param.8) | copy-start | bytes 3145732
Sparse Core Ops, SparseCore 0:
  112.3 26.7 reduce-scatter.2
  146.4 26.1 reduce-scatter.4

commit v9 on v6

--- a/solution.py
+++ b/solution.py
@@ -35,14 +35,21 @@
     two_on = jnp.concatenate([first_two_on, from_behind(rest, SEQ_AXES, -2)], axis=1)
     partner_own = swap_pairs(block, SEQ_AXES, 1)
     four_on = from_behind(two_on, SEQ_AXES, -2)
-    partner_two_on = jnp.concatenate(
-        [swap_pairs(first_two_on, SEQ_AXES, 0, 1), swap_pairs(two_on[:, split:], SEQ_AXES, 0, 1)],
+    partner_halves = [
+        swap_pairs(first_two_on, SEQ_AXES, 0, 1),
+        swap_pairs(two_on[:, split:], SEQ_AXES, 0, 1),
+    ]
+    partner_two_on = jnp.concatenate(partner_halves, axis=1)
+    partner_four_on = jnp.concatenate(
+        [
+            lax.ppermute(
+                piece,
+                SEQ_AXES,
+                [(source, source - 2) for source in range(3, lax.axis_size(SEQ_AXES), 2)],
+            )
+            for piece in partner_halves
+        ],
         axis=1,
-    )
-    partner_four_on = lax.ppermute(
-        partner_two_on,
-        SEQ_AXES,
-        [(source, source - 2) for source in range(3, lax.axis_size(SEQ_AXES), 2)],
     )
     one_on = jnp.where(side_zero, partner_own, partner_two_on)
     three_on = jnp.where(side_zero, partner_two_on, partner_four_on)

time: 174 us -> 175 us (level)
  waiting for transfers between devices: 67.3 us -> 63.3 us
  starting transfers between devices: 34.7 us -> 38.5 us
    ppermute x5, starting transfers between devices: 29.8 us -> 33.1 us  [swap_pairs(): lax.ppermute(value, axis, [(source, source ^ 1) for source in range(from_...]
    ppermute x3, waiting for transfers between devices: 21.9 us -> 19.5 us  [from_behind(): lax.ppermute(value, axis, [(source, source + steps) for source in range(l...]
  transfers between devices with their start and end apart: 10 -> 11, of which waited for: 7 -> 7; matrix products, arithmetic and copies ran while one was open for 30% -> 30% of each run, Pallas kernels for 0% -> 0%
where the time goes in v9:
time: 175 us
  waiting for transfers between devices  63.3 us (36%)
  starting transfers between devices  38.5 us (22%)
  matrix products  28.8 us (16%)
  other arithmetic  25.3 us (14%)
  between operations  14.6 us (8%)
  local copies, waits for them, and re-layouts  4.3 us (2%)
    ppermute x5, starting transfers between devices, swap_pairs(): lax.ppermute(value, axis, [(source, source ^ 1) for source in range(from_...  33.1 us
    ppermute x5, waiting for transfers between devices, swap_pairs(): lax.ppermute(value, axis, [(source, source ^ 1) for source in range(from_...  28.9 us
    ppermute x3, waiting for transfers between devices, from_behind(): lax.ppermute(value, axis, [(source, source + steps) for source in range(l...  19.5 us
    reduce_scatter x1, waiting for transfers between devices, on_device(): lax.psum_scatter(jnp.concatenate(reduced, axis=0).astype(jnp.bfloat16), '...  14.9 us
    dot_general x1, matrix products, filter_taps(): jnp.dot(second_act, w_out, precision=lax.Precision.HIGHEST, preferred_ele...  8.74 us
    dot_general x6, matrix products, slab_spectrum(): jnp.dot(jnp.concatenate([fwd_re, fwd_im], axis=0), slab_data, preferred_e...  8.48 us
    another operation x6, other arithmetic  7.72 us
    convert_element_type x1, other arithmetic, on_device(): mix_im = sum_im.astype(jnp.bfloat16)  4.59 us
  transfers between devices with their start and end apart: 11, of which 7 were waited for; matrix products, arithmetic and copies ran while one was open for 30% of the time, Pallas kernels for 0%

profile of v9, /device:TPU:0, one launch (start us, length us, event | category | flops | bytes accessed | tf_op | source)
XLA Modules:
  0.0 174.9 jit_solution(4633759587612934181)
XLA Ops:
  7.2 0.0 copy-start
  7.2 0.0 reduce-scatter.2.cloned.1.call-start
  7.2 1.4 collective-permute-start
  8.7 1.3 fusion.103
  9.9 1.3 collective-permute-start.1
  11.3 1.0 fusion.87
  12.2 1.0 select_convert_fusion.2
  13.3 2.1 %convolution_convert_fusion.5 = bf16[512,2048]{1,0:T(8,128)(2,1)} fusion(bf16[256,2048]{1,0:T(8,128)(2,1)S(1)} %copy-done.11, bf16[256,256]{1,0:T(8,128)(2,1)S(1)} %select_convert_fusion.2, bf16[256,256]{1,0:T(8,128)(2,1)S(1)} %fusion.87), kind=kOutput, calls=%fused_computation.25 | convolution fusion | flops 538443776 | bytes 3407872 | tf_op jit(solution)/shard_map/dot_general | solution.py:114
  15.4 11.4 %collective-permute-done.1 = bf16[256,1024]{1,0:T(8,128)(2,1)S(1)} collective-permute-done((bf16[256,1024]{1,0:T(8,128)(2,1)S(1)}, bf16[256,1024]{1,0:T(8,128)(2,1)S(1)}, u32[]{:S(2)}, u32[]{:S(2)}) %collective-permute-start.1) | collective-permute-done | bytes 524320 | tf_op jit(solution)/shard_map/ppermute | solution.py:15
  26.8 1.3 collective-permute-start.3
  28.1 2.1 %convolution_convert_fusion = bf16[512,2048]{1,0:T(8,128)(2,1)} fusion(bf16[256,2048]{1,0:T(8,128)(2,1)S(1)} %copy-done, bf16[256,256]{1,0:T(8,128)(2,1)S(1)} %select_convert_fusion.2, bf16[256,256]{1,0:T(8,128)(2,1)S(1)} %fusion.87), kind=kOutput, calls=%fused_computation.20 | convolution fusion | flops 538443776 | bytes 3407872 | tf_op jit(solution)/shard_map/dot_general | solution.py:114
  30.2 3.3 %collective-permute-start.2 = (bf16[256,1024]{1,0:T(8,128)(2,1)S(1)}, bf16[256,1024]{1,0:T(8,128)(2,1)}, u32[]{:S(2)}, u32[]{:S(2)}) collective-permute-start(bf16[256,1024]{1,0:T(8,128)(2,1)S(1)} %collective-permute-done.1), channel_id=1, source_target_pairs={{0,2},{2,0},{4,6},{6,4},{8,10},{10,8},{12,14},{14,12},{1,3},{3,1},... | collective-permute-start | bytes 1572872 | tf_op jit(solution)/shard_map/ppermute | solution.py:20
  33.5 1.2 multiply_convert_fusion.1
  34.7 0.0 copy-start.12
  34.8 7.1 %collective-permute-done.3 = bf16[256,1024]{1,0:T(8,128)(2,1)S(1)} collective-permute-done((bf16[256,1024]{1,0:T(8,128)(2,1)S(1)}, bf16[256,1024]{1,0:T(8,128)(2,1)S(1)}, u32[]{:S(2)}, u32[]{:S(2)}) %collective-permute-start.3) | collective-permute-done | bytes 524320 | tf_op jit(solution)/shard_map/ppermute | solution.py:15
  41.9 2.9 %collective-permute-start.4 = (bf16[256,1024]{1,0:T(8,128)(2,1)S(1)}, bf16[256,1024]{1,0:T(8,128)(2,1)S(1)}, u32[]{:S(2)}, u32[]{:S(2)}) collective-permute-start(bf16[256,1024]{1,0:T(8,128)(2,1)S(1)} %collective-permute-done.3), channel_id=1, source_target_pairs={{0,2},{2,0},{4,6},{6,4},{8,10},{10,8},{12,14},{14,12},{1,3},{3,1},... | collective-permute-start | bytes 1572872 | tf_op jit(solution)/shard_map/ppermute | solution.py:20
  44.8 1.3 collective-permute-start.7
  46.1 1.0 collective-permute-done.2
  47.1 0.7 collective-permute-start.5
  47.8 1.1 constant_dynamic-update-slice_fusion.1
  48.9 0.7 convolution_convert_fusion.3
  49.7 7.8 %collective-permute-done.4 = bf16[256,1024]{1,0:T(8,128)(2,1)S(1)} collective-permute-done((bf16[256,1024]{1,0:T(8,128)(2,1)S(1)}, bf16[256,1024]{1,0:T(8,128)(2,1)S(1)}, u32[]{:S(2)}, u32[]{:S(2)}) %collective-permute-start.4) | collective-permute-done | bytes 524320 | tf_op jit(solution)/shard_map/ppermute | solution.py:20
  57.5 0.0 collective-permute-done
  57.5 2.1 %convolution_convert_fusion.4 = bf16[512,2048]{1,0:T(8,128)(2,1)S(1)} fusion(bf16[256,2048]{1,0:T(8,128)(2,1)} %collective-permute-done, bf16[256,2048]{1,0:T(8,128)(2,1)S(1)} %constant_dynamic-update-slice_fusion, pred[]{:T(512)S(6)} %eq.91, bf16[256,256]{1,0:T(8,128)(2,1)S(1)} %select_convert_fusion.2, bf16[256,256]{1,0:T(8,128)(2,1)S(1)} %fusion.87), kind=kOutput, calls=%fused_computation.24 | convolution fusion | flops 538968064 | bytes 4456449 | tf_op jit(solution)/shard_map/dot_general | solution.py:114
  59.7 1.7 fusion.28
  61.4 1.7 fusion.23
  63.1 0.7 fusion.49
  63.8 0.7 fusion.45
  64.5 0.5 pad_maximum_fusion
  65.0 0.9 collective-permute-start.6
  65.9 0.2 fusion.66
  66.1 0.1 collective-permute-start.8
  66.2 0.0 collective-permute-done.5
  66.2 0.8 convolution_convert_fusion.2
  67.0 1.7 fusion.33
  68.7 0.9 collective-permute-done.7
  69.6 0.7 convolution_convert_fusion.1
  70.4 1.6 fusion.38
  72.0 0.7 fusion.57
  72.8 0.7 fusion.53
  73.5 0.5 pad_maximum_fusion.1
  74.0 0.2 fusion.67
  74.2 25.3 %collective-permute-start.9 = (bf16[2,128,2048]{2,1,0:T(8,128)(2,1)S(1)}, bf16[2,128,2048]{2,1,0:T(8,128)(2,1)S(1)}, u32[]{:S(2)}, u32[]{:S(2)}) collective-permute-start(bf16[2,128,2048]{2,1,0:T(8,128)(2,1)S(1)} %fusion.67), channel_id=1, source_target_pairs={{0,2},{2,0},{4,6},{6,4},{8,10},{10,8},{12,14},{14,12},{1,3},{3,1},... | collective-permute-start | bytes 3145736 | tf_op jit(solution)/shard_map/ppermute | solution.py:20
  99.5 0.5 fusion.62
  100.0 20.0 %collective-permute-done.9 = bf16[2,128,2048]{2,1,0:T(8,128)(2,1)S(1)} collective-permute-done((bf16[2,128,2048]{2,1,0:T(8,128)(2,1)S(1)}, bf16[2,128,2048]{2,1,0:T(8,128)(2,1)S(1)}, u32[]{:S(2)}, u32[]{:S(2)}) %collective-permute-start.9) | collective-permute-done | bytes 1048608 | tf_op jit(solution)/shard_map/ppermute | solution.py:20
  120.0 0.5 fusion.61
  120.6 1.6 pad_maximum_fusion.2
  122.2 0.0 copy-start.14
  122.2 0.0 reduce-scatter.2.cloned.1.call-update
  122.2 0.6 copy-done.16
  122.9 0.3 fusion.95
  123.3 2.5 %fusion.65 = f32[1024,64]{1,0:T(8,128)S(1)} fusion(f32[33,64]{1,0:T(8,128)S(1)} %copy-done.15, f32[64]{0:T(128)S(1)} %copy-done.18, f32[64]{0:T(128)S(1)} %copy-done.17, f32[1024,16]{0,1:T(8,128)S(1)} %get-tuple-element.17, f32[1024,16]{0,1:T(8,128)S(1)} %get-tuple-element.16, f32[1024,1]{0,1:T(1,128)S(1)} %convert_multiply_fusion.38), kind=kOutput, calls=%fused_computation.131 | convolution fusion | flops 26150912 | bytes 406272 | tf_op jit(solution)/shard_map/dot_general | solution.py:87
  125.8 2.2 %fusion.63 = f32[1024,64]{1,0:T(8,128)S(1)} fusion(f32[1024,64]{1,0:T(8,128)S(1)} %fusion.65, f32[64,64]{1,0:T(8,128)S(1)} %copy-done.14, f32[64]{0:T(128)S(1)} %copy-done.17), kind=kOutput, calls=%fused_computation.129 | convolution fusion | flops 50397184 | bytes 540928 | tf_op jit(solution)/shard_map/dot_general | solution.py:95
  128.0 8.7 %multiply_convert_fusion = bf16[1024,2048]{1,0:T(8,128)(2,1)S(1)} fusion(f32[1024,64]{1,0:T(8,128)S(1)} %fusion.63, f32[64,2048]{1,0:T(8,128)} %param.14, f32[1024]{0:T(1024)S(1)} %iota_convert_fusion, f32[2048]{0:T(1024)S(1)} %neg.7), kind=kOutput, calls=%fused_computation.1 | convolution fusion | flops 1616904192 | bytes 4993024 | tf_op jit(solution)/shard_map/dot_general | solution.py:99
  136.8 2.4 %convert_bitcast_fusion = bf16[4,512,2048]{2,1,0:T(8,128)(2,1)S(1)} fusion(bf16[4,256,2048]{2,1,0:T(8,128)(2,1)S(1)} %bitcast.125, bf16[256,256]{1,0:T(8,128)(2,1)S(1)} %select_convert_fusion.2, bf16[256,256]{1,0:T(8,128)(2,1)S(1)} %fusion.87), kind=kOutput, calls=%fused_computation | convolution fusion | flops 2152202240 | bytes 12845056 | tf_op jit(solution)/shard_map/fs,jsc->jfc/dot_general | solution.py:122
  139.2 0.5 copy-done.8
  139.7 0.6 copy-done.10
  140.3 4.4 %fusion.6 = bf16[256,2048]{1,0:T(8,128)(2,1)S(1)} fusion(f32[256]{0:T(256)S(1)} %compare_select_fusion, pred[256]{0:T(512)(128)(4,1)S(1)} %iota_compare_fusion, bf16[4,512,2048]{2,1,0:T(8,128)(2,1)S(1)} %convert_bitcast_fusion, bf16[512,2048]{1,0:T(8,128)(2,1)S(1)} %copy-done.10, bf16[512,2048]{1,0:T(8,128)(2,1)S(1)} %copy-done.8, ...), kind=kLoop, calls=%fused_computation.61 | loop fusion | flops 28311552 | bytes 19924224 | tf_op jit(solution)/shard_map/convert_element_type | solution.py:166
  144.6 0.0 copy-start.13
  144.6 0.0 copy-start.1
  144.6 4.6 %fusion.12 = bf16[256,2048]{1,0:T(8,128)(2,1)S(1)} fusion(f32[256]{0:T(256)S(1)} %compare_select_fusion, pred[256]{0:T(512)(128)(4,1)S(1)} %iota_compare_fusion, bf16[4,512,2048]{2,1,0:T(8,128)(2,1)S(1)} %convert_bitcast_fusion, bf16[512,2048]{1,0:T(8,128)(2,1)S(1)} %copy-done.10, bf16[512,2048]{1,0:T(8,128)(2,1)S(1)} %copy-done.8, ...), kind=kLoop, calls=%fused_computation.67 | loop fusion | flops 30408704 | bytes 19924224 | tf_op jit(solution)/shard_map/convert_element_type | solution.py:167
  149.3 1.7 convolution_convert_fusion.6
  150.9 14.9 %reduce-scatter.2.cloned.1.call-done = bf16[1,128,2048]{2,1,0:T(8,128)(2,1)} async-done(((bf16[4,128,2048]{2,1,0:T(8,128)(2,1)}), bf16[1,128,2048]{2,1,0:T(8,128)(2,1)}) %reduce-scatter.2.cloned.1.call-update) | async-done | bytes 524304 | tf_op jit(solution)/shard_map/reduce_scatter | solution.py:200
  165.9 2.1 %bitcast_convert_fusion = f32[128,2048]{1,0:T(8,128)} fusion(bf16[1,128,2048]{2,1,0:T(8,128)(2,1)} %reduce-scatter.2.cloned.1.call-done), kind=kLoop, calls=%fused_computation.148 | loop fusion | flops 262144 | bytes 1572864 | tf_op jit(solution)/shard_map/convert_element_type | solution.py:203
  (42 shorter events, 0.2 us)
Async XLA Ops:
  7.2 20.9 %copy-start = (bf16[256,2048]{1,0:T(8,128)(2,1)S(1)}, bf16[256,2048]{1,0:T(8,128)(2,1)}, u32[]{:S(2)}) copy-start(bf16[256,2048]{1,0:T(8,128)(2,1)} %param.8) | copy-start | bytes 3145732
  7.2 6.1 %copy-start.11 = (bf16[256,2048]{1,0:T(8,128)(2,1)S(1)}, bf16[256,2048]{1,0:T(8,128)(2,1)}, u32[]{:S(2)}) copy-start(bf16[256,2048]{1,0:T(8,128)(2,1)} %param.9) | copy-start | bytes 3145732
  7.2 158.7 %reduce-scatter.2.cloned.1.call-start = ((), (), s32[]{:S(2)}) async-start(), calls=%async_computation.1 | async-start | bytes 2621440 | tf_op jit(solution)/shard_map/reduce_scatter | solution.py:200
  7.2 50.3 %collective-permute-start = (bf16[256,2048]{1,0:T(8,128)(2,1)}, bf16[256,2048]{1,0:T(8,128)(2,1)}, u32[]{:S(2)}, u32[]{:S(2)}) collective-permute-start(bf16[256,2048]{1,0:T(8,128)(2,1)} %param.9), channel_id=1, source_target_pairs={{2,0},{6,4},{10,8},{14,12},{3,1},{7,5},{11,9},{15,13},{18,16},{22,... | collective-permute-start | bytes 3145736 | tf_op jit(solution)/shard_map/ppermute | solution.py:20
  9.9 16.8 %collective-permute-start.1 = (bf16[256,1024]{1,0:T(8,128)(2,1)S(1)}, bf16[256,1024]{1,0:T(8,128)(2,1)S(1)}, u32[]{:S(2)}, u32[]{:S(2)}) collective-permute-start(bf16[256,1024]{1,0:T(8,128)(2,1)S(1)} %get-tuple-element.15), channel_id=1, source_target_pairs={{4,0},{6,2},{8,4},{10,6},{12,8},{14,10},{5,1},{7,3},{9,5},{11,7},{... | collective-permute-start | bytes 1572872 | tf_op jit(solution)/shard_map/ppermute | solution.py:15
  26.8 15.1 %collective-permute-start.3 = (bf16[256,1024]{1,0:T(8,128)(2,1)S(1)}, bf16[256,1024]{1,0:T(8,128)(2,1)S(1)}, u32[]{:S(2)}, u32[]{:S(2)}) collective-permute-start(bf16[256,1024]{1,0:T(8,128)(2,1)S(1)} %get-tuple-element.5), channel_id=1, source_target_pairs={{4,0},{6,2},{8,4},{10,6},{12,8},{14,10},{5,1},{7,3},{9,5},{11,7},{... | collective-permute-start | bytes 1572872 | tf_op jit(solution)/shard_map/ppermute | solution.py:15
  30.2 17.0 %collective-permute-start.2 = (bf16[256,1024]{1,0:T(8,128)(2,1)S(1)}, bf16[256,1024]{1,0:T(8,128)(2,1)}, u32[]{:S(2)}, u32[]{:S(2)}) collective-permute-start(bf16[256,1024]{1,0:T(8,128)(2,1)S(1)} %collective-permute-done.1), channel_id=1, source_target_pairs={{0,2},{2,0},{4,6},{6,4},{8,10},{10,8},{12,14},{14,12},{1,3},{3,1},... | collective-permute-start | bytes 1572872 | tf_op jit(solution)/shard_map/ppermute | solution.py:20
  34.7 38.1 %copy-start.12 = (bf16[256,256]{1,0:T(8,128)(2,1)}, bf16[256,256]{1,0:T(8,128)(2,1)S(1)}, u32[]{:S(2)}) copy-start(bf16[256,256]{1,0:T(8,128)(2,1)S(1)} %get-tuple-element.19) | copy-start | bytes 393220
  41.9 15.6 %collective-permute-start.4 = (bf16[256,1024]{1,0:T(8,128)(2,1)S(1)}, bf16[256,1024]{1,0:T(8,128)(2,1)S(1)}, u32[]{:S(2)}, u32[]{:S(2)}) collective-permute-start(bf16[256,1024]{1,0:T(8,128)(2,1)S(1)} %collective-permute-done.3), channel_id=1, source_target_pairs={{0,2},{2,0},{4,6},{6,4},{8,10},{10,8},{12,14},{14,12},{1,3},{3,1},... | collective-permute-start | bytes 1572872 | tf_op jit(solution)/shard_map/ppermute | solution.py:20
  44.8 24.8 %collective-permute-start.7 = (bf16[256,2048]{1,0:T(8,128)(2,1)S(1)}, bf16[256,2048]{1,0:T(8,128)(2,1)S(1)}, u32[]{:S(2)}, u32[]{:S(2)}) collective-permute-start(bf16[256,2048]{1,0:T(8,128)(2,1)S(1)} %constant_dynamic-update-slice_fusion.2), channel_id=1, source_target_pairs={{4,0},{6,2},{8,4},{10,6},{12,8},{14,10},{5,1},{7,3},{9,5},{11,7},{... | collective-permute-start | bytes 3145736 | tf_op jit(solution)/shard_map/ppermute | solution.py:15
  47.1 19.1 %collective-permute-start.5 = (bf16[256,1024]{1,0:T(8,128)(2,1)}, bf16[256,1024]{1,0:T(8,128)(2,1)S(1)}, u32[]{:S(2)}, u32[]{:S(2)}) collective-permute-start(bf16[256,1024]{1,0:T(8,128)(2,1)} %collective-permute-done.2), channel_id=1, source_target_pairs={{6,2},{10,6},{14,10},{7,3},{11,7},{15,11},{22,18},{26,22},{30,26},... | collective-permute-start | bytes 1572872 | tf_op jit(solution)/shard_map/ppermute | solution.py:45
  49.6 17.4 %copy-start.3 = (bf16[512,2048]{1,0:T(8,128)(2,1)}, bf16[512,2048]{1,0:T(8,128)(2,1)S(1)}, u32[]{:S(2)}) copy-start(bf16[512,2048]{1,0:T(8,128)(2,1)S(1)} %convolution_convert_fusion.3) | copy-start | bytes 6291460
  57.5 2.2 %copy-start.2 = (bf16[512,2048]{1,0:T(8,128)(2,1)S(1)}, bf16[512,2048]{1,0:T(8,128)(2,1)}, u32[]{:S(2)}) copy-start(bf16[512,2048]{1,0:T(8,128)(2,1)} %convolution_convert_fusion) | copy-start | bytes 6291460
  59.7 1.7 copy-start.7
  65.0 1.2 collective-permute-start.6
  66.1 33.4 %collective-permute-start.8 = (bf16[2,128,2048]{2,1,0:T(8,128)(2,1)S(1)}, bf16[2,128,2048]{2,1,0:T(8,128)(2,1)S(1)}, u32[]{:S(2)}, u32[]{:S(2)}) collective-permute-start(bf16[2,128,2048]{2,1,0:T(8,128)(2,1)S(1)} %fusion.66), channel_id=1, source_target_pairs={{0,2},{2,0},{4,6},{6,4},{8,10},{10,8},{12,14},{14,12},{1,3},{3,1},... | collective-permute-start | bytes 3145736 | tf_op jit(solution)/shard_map/ppermute | solution.py:20
  67.0 3.4 %copy-start.5 = (bf16[512,2048]{1,0:T(8,128)(2,1)}, bf16[512,2048]{1,0:T(8,128)(2,1)S(1)}, u32[]{:S(2)}) copy-start(bf16[512,2048]{1,0:T(8,128)(2,1)S(1)} %convolution_convert_fusion.2) | copy-start | bytes 6291460
  70.4 1.7 copy-start.9
  74.2 45.8 %collective-permute-start.9 = (bf16[2,128,2048]{2,1,0:T(8,128)(2,1)S(1)}, bf16[2,128,2048]{2,1,0:T(8,128)(2,1)S(1)}, u32[]{:S(2)}, u32[]{:S(2)}) collective-permute-start(bf16[2,128,2048]{2,1,0:T(8,128)(2,1)S(1)} %fusion.67), channel_id=1, source_target_pairs={{0,2},{2,0},{4,6},{6,4},{8,10},{10,8},{12,14},{14,12},{1,3},{3,1},... | collective-permute-start | bytes 3145736 | tf_op jit(solution)/shard_map/ppermute | solution.py:20
  122.2 0.7 copy-start.16
  122.2 1.1 copy-start.15
  122.2 1.1 copy-start.17
  122.2 1.1 copy-start.18
  122.2 3.6 %copy-start.14 = (f32[64,64]{1,0:T(8,128)S(1)}, f32[64,64]{1,0:T(8,128)}, u32[]{:S(2)}) copy-start(f32[64,64]{1,0:T(8,128)} %param.12) | copy-start | bytes 49156
  136.7 2.4 %copy-start.4 = (bf16[512,2048]{1,0:T(8,128)(2,1)S(1)}, bf16[512,2048]{1,0:T(8,128)(2,1)}, u32[]{:S(2)}) copy-start(bf16[512,2048]{1,0:T(8,128)(2,1)} %copy-done.3) | copy-start | bytes 6291460
  136.7 2.4 %copy-start.6 = (bf16[512,2048]{1,0:T(8,128)(2,1)S(1)}, bf16[512,2048]{1,0:T(8,128)(2,1)}, u32[]{:S(2)}) copy-start(bf16[512,2048]{1,0:T(8,128)(2,1)} %copy-done.5) | copy-start | bytes 6291460
  136.7 2.9 %copy-start.8 = (bf16[512,2048]{1,0:T(8,128)(2,1)S(1)}, bf16[512,2048]{1,0:T(8,128)(2,1)}, u32[]{:S(2)}) copy-start(bf16[512,2048]{1,0:T(8,128)(2,1)} %convolution_convert_fusion.5) | copy-start | bytes 6291460
  136.8 3.5 %copy-start.10 = (bf16[512,2048]{1,0:T(8,128)(2,1)S(1)}, bf16[512,2048]{1,0:T(8,128)(2,1)}, u32[]{:S(2)}) copy-start(bf16[512,2048]{1,0:T(8,128)(2,1)} %copy-done.9) | copy-start | bytes 6291460
  144.6 4.6 %copy-start.13 = (bf16[256,256]{1,0:T(8,128)(2,1)S(1)}, bf16[256,256]{1,0:T(8,128)(2,1)}, u32[]{:S(2)}) copy-start(bf16[256,256]{1,0:T(8,128)(2,1)} %copy-done.12) | copy-start | bytes 393220
  144.6 23.4 %copy-start.1 = (bf16[256,2048]{1,0:T(8,128)(2,1)S(1)}, bf16[256,2048]{1,0:T(8,128)(2,1)}, u32[]{:S(2)}) copy-start(bf16[256,2048]{1,0:T(8,128)(2,1)} %param.8) | copy-start | bytes 3145732
Sparse Core Ops, SparseCore 0:
  122.3 43.5 reduce-scatter.1

commit v10 on v6

--- a/solution.py
+++ b/solution.py
@@ -39,10 +39,16 @@
         [swap_pairs(first_two_on, SEQ_AXES, 0, 1), swap_pairs(two_on[:, split:], SEQ_AXES, 0, 1)],
         axis=1,
     )
-    partner_four_on = lax.ppermute(
-        partner_two_on,
-        SEQ_AXES,
-        [(source, source - 2) for source in range(3, lax.axis_size(SEQ_AXES), 2)],
+    partner_four_on = jnp.concatenate(
+        [
+            lax.ppermute(
+                partner_two_on[:, :split],
+                SEQ_AXES,
+                [(source, source - 2) for source in range(3, lax.axis_size(SEQ_AXES), 2)],
+            ),
+            swap_pairs(four_on[:, split:], SEQ_AXES, 0),
+        ],
+        axis=1,
     )
     one_on = jnp.where(side_zero, partner_own, partner_two_on)
     three_on = jnp.where(side_zero, partner_two_on, partner_four_on)

time: 174 us -> 181 us (1.040)
  waiting for transfers between devices: 67.3 us -> 87 us
  starting transfers between devices: 34.7 us -> 20.1 us
  local copies, waits for them, and re-layouts: 3.25 us -> 5.19 us
    ppermute x5 -> x6, waiting for transfers between devices: 30.5 us -> 48.9 us  [swap_pairs(): lax.ppermute(value, axis, [(source, source ^ 1) for source in range(from_...]
    ppermute x5 -> x6, starting transfers between devices: 29.8 us -> 15.5 us  [swap_pairs(): lax.ppermute(value, axis, [(source, source ^ 1) for source in range(from_...]
    unnamed x40, local copies, waits for them, and re-layouts: 1.91 us -> 3.81 us
  transfers between devices with their start and end apart: 10 -> 11, of which waited for: 7 -> 9; matrix products, arithmetic and copies ran while one was open for 30% -> 29% of each run, Pallas kernels for 0% -> 0%
where the time goes in v10:
time: 181 us
  waiting for transfers between devices  87 us (48%)
  matrix products  28.8 us (16%)
  other arithmetic  25.3 us (14%)
  starting transfers between devices  20.1 us (11%)
  between operations  14.6 us (8%)
  local copies, waits for them, and re-layouts  5.19 us (3%)
    ppermute x6, waiting for transfers between devices, swap_pairs(): lax.ppermute(value, axis, [(source, source ^ 1) for source in range(from_...  48.9 us
    ppermute x3, waiting for transfers between devices, from_behind(): lax.ppermute(value, axis, [(source, source + steps) for source in range(l...  22.4 us
    reduce_scatter x1, waiting for transfers between devices, on_device(): lax.psum_scatter(jnp.concatenate(reduced, axis=0).astype(jnp.bfloat16), '...  15.6 us
    ppermute x6, starting transfers between devices, swap_pairs(): lax.ppermute(value, axis, [(source, source ^ 1) for source in range(from_...  15.5 us
    dot_general x1, matrix products, filter_taps(): jnp.dot(second_act, w_out, precision=lax.Precision.HIGHEST, preferred_ele...  8.79 us
    dot_general x6, matrix products, slab_spectrum(): jnp.dot(jnp.concatenate([fwd_re, fwd_im], axis=0), slab_data, preferred_e...  8.43 us
    another operation x6, other arithmetic  7.7 us
    convert_element_type x1, other arithmetic, on_device(): mix_im = sum_im.astype(jnp.bfloat16)  4.59 us
  transfers between devices with their start and end apart: 11, of which 9 were waited for; matrix products, arithmetic and copies ran while one was open for 29% of the time, Pallas kernels for 0%

profile of v10, /device:TPU:0, one launch (start us, length us, event | category | flops | bytes accessed | tf_op | source)
XLA Modules:
  0.0 181.0 jit_solution(17094697807712559619)
XLA Ops:
  7.2 0.0 copy-start
  7.2 0.0 reduce-scatter.2.cloned.1.call-start
  7.2 1.4 collective-permute-start
  8.7 1.3 fusion.103
  9.9 1.3 collective-permute-start.1
  11.3 1.0 fusion.87
  12.2 1.0 select_convert_fusion.2
  13.3 2.1 %convolution_convert_fusion.5 = bf16[512,2048]{1,0:T(8,128)(2,1)} fusion(bf16[256,2048]{1,0:T(8,128)(2,1)S(1)} %copy-done.11, bf16[256,256]{1,0:T(8,128)(2,1)S(1)} %select_convert_fusion.2, bf16[256,256]{1,0:T(8,128)(2,1)S(1)} %fusion.87), kind=kOutput, calls=%fused_computation.25 | convolution fusion | flops 538443776 | bytes 3407872 | tf_op jit(solution)/shard_map/dot_general | solution.py:113
  15.4 11.4 %collective-permute-done.1 = bf16[256,1024]{1,0:T(8,128)(2,1)S(1)} collective-permute-done((bf16[256,1024]{1,0:T(8,128)(2,1)S(1)}, bf16[256,1024]{1,0:T(8,128)(2,1)S(1)}, u32[]{:S(2)}, u32[]{:S(2)}) %collective-permute-start.1) | collective-permute-done | bytes 524320 | tf_op jit(solution)/shard_map/ppermute | solution.py:15
  26.8 1.3 collective-permute-start.3
  28.1 2.0 %convolution_convert_fusion = bf16[512,2048]{1,0:T(8,128)(2,1)} fusion(bf16[256,2048]{1,0:T(8,128)(2,1)S(1)} %copy-done, bf16[256,256]{1,0:T(8,128)(2,1)S(1)} %select_convert_fusion.2, bf16[256,256]{1,0:T(8,128)(2,1)S(1)} %fusion.87), kind=kOutput, calls=%fused_computation.20 | convolution fusion | flops 538443776 | bytes 3407872 | tf_op jit(solution)/shard_map/dot_general | solution.py:113
  30.1 3.3 %collective-permute-start.2 = (bf16[256,1024]{1,0:T(8,128)(2,1)S(1)}, bf16[256,1024]{1,0:T(8,128)(2,1)}, u32[]{:S(2)}, u32[]{:S(2)}) collective-permute-start(bf16[256,1024]{1,0:T(8,128)(2,1)S(1)} %collective-permute-done.1), channel_id=1, source_target_pairs={{0,2},{2,0},{4,6},{6,4},{8,10},{10,8},{12,14},{14,12},{1,3},{3,1},... | collective-permute-start | bytes 1572872 | tf_op jit(solution)/shard_map/ppermute | solution.py:20
  33.5 1.2 multiply_convert_fusion.1
  34.6 0.0 copy-start.12
  34.7 7.2 %collective-permute-done.3 = bf16[256,1024]{1,0:T(8,128)(2,1)S(1)} collective-permute-done((bf16[256,1024]{1,0:T(8,128)(2,1)S(1)}, bf16[256,1024]{1,0:T(8,128)(2,1)S(1)}, u32[]{:S(2)}, u32[]{:S(2)}) %collective-permute-start.3) | collective-permute-done | bytes 524320 | tf_op jit(solution)/shard_map/ppermute | solution.py:15
  41.9 2.9 %collective-permute-start.4 = (bf16[256,1024]{1,0:T(8,128)(2,1)S(1)}, bf16[256,1024]{1,0:T(8,128)(2,1)S(1)}, u32[]{:S(2)}, u32[]{:S(2)}) collective-permute-start(bf16[256,1024]{1,0:T(8,128)(2,1)S(1)} %collective-permute-done.3), channel_id=1, source_target_pairs={{0,2},{2,0},{4,6},{6,4},{8,10},{10,8},{12,14},{14,12},{1,3},{3,1},... | collective-permute-start | bytes 1572872 | tf_op jit(solution)/shard_map/ppermute | solution.py:20
  44.8 1.3 collective-permute-start.6
  46.1 1.0 collective-permute-done.2
  47.1 0.7 collective-permute-start.5
  47.8 1.1 constant_dynamic-update-slice_fusion.1
  48.9 0.7 convolution_convert_fusion.3
  49.7 7.8 %collective-permute-done.4 = bf16[256,1024]{1,0:T(8,128)(2,1)S(1)} collective-permute-done((bf16[256,1024]{1,0:T(8,128)(2,1)S(1)}, bf16[256,1024]{1,0:T(8,128)(2,1)S(1)}, u32[]{:S(2)}, u32[]{:S(2)}) %collective-permute-start.4) | collective-permute-done | bytes 524320 | tf_op jit(solution)/shard_map/ppermute | solution.py:20
  57.5 2.1 %convolution_convert_fusion.4 = bf16[512,2048]{1,0:T(8,128)(2,1)S(1)} fusion(bf16[256,2048]{1,0:T(8,128)(2,1)} %collective-permute-done, bf16[256,2048]{1,0:T(8,128)(2,1)S(1)} %constant_dynamic-update-slice_fusion, pred[]{:T(512)S(6)} %eq.91, bf16[256,256]{1,0:T(8,128)(2,1)S(1)} %select_convert_fusion.2, bf16[256,256]{1,0:T(8,128)(2,1)S(1)} %fusion.87), kind=kOutput, calls=%fused_computation.24 | convolution fusion | flops 538968064 | bytes 4456449 | tf_op jit(solution)/shard_map/dot_general | solution.py:113
  59.7 1.7 fusion.28
  61.4 0.7 fusion.49
  62.1 0.9 copy-done.7
  63.0 1.7 fusion.23
  64.6 0.7 fusion.45
  65.4 0.5 pad_maximum_fusion
  65.9 3.8 %collective-permute-done.6 = bf16[256,2048]{1,0:T(8,128)(2,1)S(1)} collective-permute-done((bf16[256,2048]{1,0:T(8,128)(2,1)S(1)}, bf16[256,2048]{1,0:T(8,128)(2,1)S(1)}, u32[]{:S(2)}, u32[]{:S(2)}) %collective-permute-start.6) | collective-permute-done | bytes 1048608 | tf_op jit(solution)/shard_map/ppermute | solution.py:15
  69.7 5.3 %collective-permute-start.7 = (bf16[256,1024]{1,0:T(8,128)(2,1)S(1)}, bf16[256,1024]{1,0:T(8,128)(2,1)S(1)}, u32[]{:S(2)}, u32[]{:S(2)}) collective-permute-start(bf16[256,1024]{1,0:T(8,128)(2,1)S(1)} %slice.133), channel_id=1, source_target_pairs={{0,2},{4,6},{8,10},{12,14},{1,3},{5,7},{9,11},{13,15},{16,18},{20,... | collective-permute-start | bytes 1572872 | tf_op jit(solution)/shard_map/ppermute | solution.py:20
  75.0 0.2 fusion.66
  75.2 0.1 collective-permute-start.8
  75.3 0.7 convolution_convert_fusion.1
  76.0 11.1 %collective-permute-done.7 = bf16[256,1024]{1,0:T(8,128)(2,1)S(1)} collective-permute-done((bf16[256,1024]{1,0:T(8,128)(2,1)S(1)}, bf16[256,1024]{1,0:T(8,128)(2,1)S(1)}, u32[]{:S(2)}, u32[]{:S(2)}) %collective-permute-start.7) | collective-permute-done | bytes 524320 | tf_op jit(solution)/shard_map/ppermute | solution.py:20
  87.1 0.8 convolution_convert_fusion.2
  87.9 1.7 fusion.33
  89.6 1.6 fusion.38
  91.3 0.7 fusion.57
  92.0 0.7 fusion.53
  92.7 0.5 pad_maximum_fusion.1
  93.2 0.2 fusion.67
  93.4 2.5 %collective-permute-start.9 = (bf16[2,128,2048]{2,1,0:T(8,128)(2,1)S(1)}, bf16[2,128,2048]{2,1,0:T(8,128)(2,1)S(1)}, u32[]{:S(2)}, u32[]{:S(2)}) collective-permute-start(bf16[2,128,2048]{2,1,0:T(8,128)(2,1)S(1)} %fusion.67), channel_id=1, source_target_pairs={{0,2},{2,0},{4,6},{6,4},{8,10},{10,8},{12,14},{14,12},{1,3},{3,1},... | collective-permute-start | bytes 3145736 | tf_op jit(solution)/shard_map/ppermute | solution.py:20
  96.0 13.6 %collective-permute-done.8 = bf16[2,128,2048]{2,1,0:T(8,128)(2,1)S(1)} collective-permute-done((bf16[2,128,2048]{2,1,0:T(8,128)(2,1)S(1)}, bf16[2,128,2048]{2,1,0:T(8,128)(2,1)S(1)}, u32[]{:S(2)}, u32[]{:S(2)}) %collective-permute-start.8) | collective-permute-done | bytes 1048608 | tf_op jit(solution)/shard_map/ppermute | solution.py:20
  109.6 0.5 fusion.62
  110.1 15.3 %collective-permute-done.9 = bf16[2,128,2048]{2,1,0:T(8,128)(2,1)S(1)} collective-permute-done((bf16[2,128,2048]{2,1,0:T(8,128)(2,1)S(1)}, bf16[2,128,2048]{2,1,0:T(8,128)(2,1)S(1)}, u32[]{:S(2)}, u32[]{:S(2)}) %collective-permute-start.9) | collective-permute-done | bytes 1048608 | tf_op jit(solution)/shard_map/ppermute | solution.py:20
  125.4 0.5 fusion.61
  125.9 1.6 pad_maximum_fusion.2
  127.5 0.0 copy-start.14
  127.5 0.0 reduce-scatter.2.cloned.1.call-update
  127.6 0.6 copy-done.16
  128.2 0.3 fusion.95
  128.6 2.5 %fusion.65 = f32[1024,64]{1,0:T(8,128)S(1)} fusion(f32[33,64]{1,0:T(8,128)S(1)} %copy-done.15, f32[64]{0:T(128)S(1)} %copy-done.18, f32[64]{0:T(128)S(1)} %copy-done.17, f32[1024,16]{0,1:T(8,128)S(1)} %get-tuple-element.17, f32[1024,16]{0,1:T(8,128)S(1)} %get-tuple-element.16, f32[1024,1]{0,1:T(1,128)S(1)} %convert_multiply_fusion.38), kind=kOutput, calls=%fused_computation.131 | convolution fusion | flops 26150912 | bytes 406272 | tf_op jit(solution)/shard_map/dot_general | solution.py:86
  131.2 2.2 %fusion.63 = f32[1024,64]{1,0:T(8,128)S(1)} fusion(f32[1024,64]{1,0:T(8,128)S(1)} %fusion.65, f32[64,64]{1,0:T(8,128)S(1)} %copy-done.14, f32[64]{0:T(128)S(1)} %copy-done.17), kind=kOutput, calls=%fused_computation.129 | convolution fusion | flops 50397184 | bytes 540928 | tf_op jit(solution)/shard_map/dot_general | solution.py:94
  133.3 8.8 %multiply_convert_fusion = bf16[1024,2048]{1,0:T(8,128)(2,1)S(1)} fusion(f32[1024,64]{1,0:T(8,128)S(1)} %fusion.63, f32[64,2048]{1,0:T(8,128)} %param.14, f32[1024]{0:T(1024)S(1)} %iota_convert_fusion, f32[2048]{0:T(1024)S(1)} %neg.7), kind=kOutput, calls=%fused_computation.1 | convolution fusion | flops 1616904192 | bytes 4993024 | tf_op jit(solution)/shard_map/dot_general | solution.py:98
  142.2 2.4 %convert_bitcast_fusion = bf16[4,512,2048]{2,1,0:T(8,128)(2,1)S(1)} fusion(bf16[4,256,2048]{2,1,0:T(8,128)(2,1)S(1)} %bitcast.125, bf16[256,256]{1,0:T(8,128)(2,1)S(1)} %select_convert_fusion.2, bf16[256,256]{1,0:T(8,128)(2,1)S(1)} %fusion.87), kind=kOutput, calls=%fused_computation | convolution fusion | flops 2152202240 | bytes 12845056 | tf_op jit(solution)/shard_map/fs,jsc->jfc/dot_general | solution.py:121
  144.6 0.5 copy-done.8
  145.1 0.6 copy-done.10
  145.7 4.4 %fusion.6 = bf16[256,2048]{1,0:T(8,128)(2,1)S(1)} fusion(f32[256]{0:T(256)S(1)} %compare_select_fusion, pred[256]{0:T(512)(128)(4,1)S(1)} %iota_compare_fusion, bf16[4,512,2048]{2,1,0:T(8,128)(2,1)S(1)} %convert_bitcast_fusion, bf16[512,2048]{1,0:T(8,128)(2,1)S(1)} %copy-done.10, bf16[512,2048]{1,0:T(8,128)(2,1)S(1)} %copy-done.8, ...), kind=kLoop, calls=%fused_computation.61 | loop fusion | flops 28311552 | bytes 19924224 | tf_op jit(solution)/shard_map/convert_element_type | solution.py:165
  150.0 0.0 copy-start.1
  150.0 4.6 %fusion.12 = bf16[256,2048]{1,0:T(8,128)(2,1)S(1)} fusion(f32[256]{0:T(256)S(1)} %compare_select_fusion, pred[256]{0:T(512)(128)(4,1)S(1)} %iota_compare_fusion, bf16[4,512,2048]{2,1,0:T(8,128)(2,1)S(1)} %convert_bitcast_fusion, bf16[512,2048]{1,0:T(8,128)(2,1)S(1)} %copy-done.10, bf16[512,2048]{1,0:T(8,128)(2,1)S(1)} %copy-done.8, ...), kind=kLoop, calls=%fused_computation.67 | loop fusion | flops 30408704 | bytes 19924224 | tf_op jit(solution)/shard_map/convert_element_type | solution.py:166
  154.7 1.7 convolution_convert_fusion.6
  156.3 15.6 %reduce-scatter.2.cloned.1.call-done = bf16[1,128,2048]{2,1,0:T(8,128)(2,1)} async-done(((bf16[4,128,2048]{2,1,0:T(8,128)(2,1)}), bf16[1,128,2048]{2,1,0:T(8,128)(2,1)}) %reduce-scatter.2.cloned.1.call-update) | async-done | bytes 524304 | tf_op jit(solution)/shard_map/reduce_scatter | solution.py:199
  172.0 2.1 %bitcast_convert_fusion = f32[128,2048]{1,0:T(8,128)} fusion(bf16[1,128,2048]{2,1,0:T(8,128)(2,1)} %reduce-scatter.2.cloned.1.call-done), kind=kLoop, calls=%fused_computation.148 | loop fusion | flops 262144 | bytes 1572864 | tf_op jit(solution)/shard_map/convert_element_type | solution.py:202
  (43 shorter events, 0.2 us)
Async XLA Ops:
  7.2 20.9 %copy-start = (bf16[256,2048]{1,0:T(8,128)(2,1)S(1)}, bf16[256,2048]{1,0:T(8,128)(2,1)}, u32[]{:S(2)}) copy-start(bf16[256,2048]{1,0:T(8,128)(2,1)} %param.8) | copy-start | bytes 3145732
  7.2 6.1 %copy-start.11 = (bf16[256,2048]{1,0:T(8,128)(2,1)S(1)}, bf16[256,2048]{1,0:T(8,128)(2,1)}, u32[]{:S(2)}) copy-start(bf16[256,2048]{1,0:T(8,128)(2,1)} %param.9) | copy-start | bytes 3145732
  7.2 164.8 %reduce-scatter.2.cloned.1.call-start = ((), (), s32[]{:S(2)}) async-start(), calls=%async_computation.1 | async-start | bytes 2621440 | tf_op jit(solution)/shard_map/reduce_scatter | solution.py:199
  7.2 50.3 %collective-permute-start = (bf16[256,2048]{1,0:T(8,128)(2,1)}, bf16[256,2048]{1,0:T(8,128)(2,1)}, u32[]{:S(2)}, u32[]{:S(2)}) collective-permute-start(bf16[256,2048]{1,0:T(8,128)(2,1)} %param.9), channel_id=1, source_target_pairs={{2,0},{6,4},{10,8},{14,12},{3,1},{7,5},{11,9},{15,13},{18,16},{22,... | collective-permute-start | bytes 3145736 | tf_op jit(solution)/shard_map/ppermute | solution.py:20
  9.9 16.8 %collective-permute-start.1 = (bf16[256,1024]{1,0:T(8,128)(2,1)S(1)}, bf16[256,1024]{1,0:T(8,128)(2,1)S(1)}, u32[]{:S(2)}, u32[]{:S(2)}) collective-permute-start(bf16[256,1024]{1,0:T(8,128)(2,1)S(1)} %get-tuple-element.15), channel_id=1, source_target_pairs={{4,0},{6,2},{8,4},{10,6},{12,8},{14,10},{5,1},{7,3},{9,5},{11,7},{... | collective-permute-start | bytes 1572872 | tf_op jit(solution)/shard_map/ppermute | solution.py:15
  26.8 15.1 %collective-permute-start.3 = (bf16[256,1024]{1,0:T(8,128)(2,1)S(1)}, bf16[256,1024]{1,0:T(8,128)(2,1)S(1)}, u32[]{:S(2)}, u32[]{:S(2)}) collective-permute-start(bf16[256,1024]{1,0:T(8,128)(2,1)S(1)} %get-tuple-element.5), channel_id=1, source_target_pairs={{4,0},{6,2},{8,4},{10,6},{12,8},{14,10},{5,1},{7,3},{9,5},{11,7},{... | collective-permute-start | bytes 1572872 | tf_op jit(solution)/shard_map/ppermute | solution.py:15
  30.1 17.0 %collective-permute-start.2 = (bf16[256,1024]{1,0:T(8,128)(2,1)S(1)}, bf16[256,1024]{1,0:T(8,128)(2,1)}, u32[]{:S(2)}, u32[]{:S(2)}) collective-permute-start(bf16[256,1024]{1,0:T(8,128)(2,1)S(1)} %collective-permute-done.1), channel_id=1, source_target_pairs={{0,2},{2,0},{4,6},{6,4},{8,10},{10,8},{12,14},{14,12},{1,3},{3,1},... | collective-permute-start | bytes 1572872 | tf_op jit(solution)/shard_map/ppermute | solution.py:20
  34.6 57.4 %copy-start.12 = (bf16[256,256]{1,0:T(8,128)(2,1)}, bf16[256,256]{1,0:T(8,128)(2,1)S(1)}, u32[]{:S(2)}) copy-start(bf16[256,256]{1,0:T(8,128)(2,1)S(1)} %get-tuple-element.19) | copy-start | bytes 393220
  41.9 15.6 %collective-permute-start.4 = (bf16[256,1024]{1,0:T(8,128)(2,1)S(1)}, bf16[256,1024]{1,0:T(8,128)(2,1)S(1)}, u32[]{:S(2)}, u32[]{:S(2)}) collective-permute-start(bf16[256,1024]{1,0:T(8,128)(2,1)S(1)} %collective-permute-done.3), channel_id=1, source_target_pairs={{0,2},{2,0},{4,6},{6,4},{8,10},{10,8},{12,14},{14,12},{1,3},{3,1},... | collective-permute-start | bytes 1572872 | tf_op jit(solution)/shard_map/ppermute | solution.py:20
  44.8 24.8 %collective-permute-start.6 = (bf16[256,2048]{1,0:T(8,128)(2,1)S(1)}, bf16[256,2048]{1,0:T(8,128)(2,1)S(1)}, u32[]{:S(2)}, u32[]{:S(2)}) collective-permute-start(bf16[256,2048]{1,0:T(8,128)(2,1)S(1)} %constant_dynamic-update-slice_fusion.2), channel_id=1, source_target_pairs={{4,0},{6,2},{8,4},{10,6},{12,8},{14,10},{5,1},{7,3},{9,5},{11,7},{... | collective-permute-start | bytes 3145736 | tf_op jit(solution)/shard_map/ppermute | solution.py:15
  47.1 28.8 %collective-permute-start.5 = (bf16[256,1024]{1,0:T(8,128)(2,1)}, bf16[256,1024]{1,0:T(8,128)(2,1)S(1)}, u32[]{:S(2)}, u32[]{:S(2)}) collective-permute-start(bf16[256,1024]{1,0:T(8,128)(2,1)} %collective-permute-done.2), channel_id=1, source_target_pairs={{6,2},{10,6},{14,10},{7,3},{11,7},{15,11},{22,18},{26,22},{30,26},... | collective-permute-start | bytes 1572872 | tf_op jit(solution)/shard_map/ppermute | solution.py:44
  49.6 38.3 %copy-start.3 = (bf16[512,2048]{1,0:T(8,128)(2,1)}, bf16[512,2048]{1,0:T(8,128)(2,1)S(1)}, u32[]{:S(2)}) copy-start(bf16[512,2048]{1,0:T(8,128)(2,1)S(1)} %convolution_convert_fusion.3) | copy-start | bytes 6291460
  57.5 2.2 %copy-start.2 = (bf16[512,2048]{1,0:T(8,128)(2,1)S(1)}, bf16[512,2048]{1,0:T(8,128)(2,1)}, u32[]{:S(2)}) copy-start(bf16[512,2048]{1,0:T(8,128)(2,1)} %convolution_convert_fusion) | copy-start | bytes 6291460
  61.4 1.6 copy-start.7
  69.7 17.4 %collective-permute-start.7 = (bf16[256,1024]{1,0:T(8,128)(2,1)S(1)}, bf16[256,1024]{1,0:T(8,128)(2,1)S(1)}, u32[]{:S(2)}, u32[]{:S(2)}) collective-permute-start(bf16[256,1024]{1,0:T(8,128)(2,1)S(1)} %slice.133), channel_id=1, source_target_pairs={{0,2},{4,6},{8,10},{12,14},{1,3},{5,7},{9,11},{13,15},{16,18},{20,... | collective-permute-start | bytes 1572872 | tf_op jit(solution)/shard_map/ppermute | solution.py:20
  75.2 34.4 %collective-permute-start.8 = (bf16[2,128,2048]{2,1,0:T(8,128)(2,1)S(1)}, bf16[2,128,2048]{2,1,0:T(8,128)(2,1)S(1)}, u32[]{:S(2)}, u32[]{:S(2)}) collective-permute-start(bf16[2,128,2048]{2,1,0:T(8,128)(2,1)S(1)} %fusion.66), channel_id=1, source_target_pairs={{0,2},{2,0},{4,6},{6,4},{8,10},{10,8},{12,14},{14,12},{1,3},{3,1},... | collective-permute-start | bytes 3145736 | tf_op jit(solution)/shard_map/ppermute | solution.py:20
  76.0 13.6 %copy-start.9 = (bf16[512,2048]{1,0:T(8,128)(2,1)}, bf16[512,2048]{1,0:T(8,128)(2,1)S(1)}, u32[]{:S(2)}) copy-start(bf16[512,2048]{1,0:T(8,128)(2,1)S(1)} %convolution_convert_fusion.1) | copy-start | bytes 6291460
  87.9 1.7 copy-start.5
  93.4 32.0 %collective-permute-start.9 = (bf16[2,128,2048]{2,1,0:T(8,128)(2,1)S(1)}, bf16[2,128,2048]{2,1,0:T(8,128)(2,1)S(1)}, u32[]{:S(2)}, u32[]{:S(2)}) collective-permute-start(bf16[2,128,2048]{2,1,0:T(8,128)(2,1)S(1)} %fusion.67), channel_id=1, source_target_pairs={{0,2},{2,0},{4,6},{6,4},{8,10},{10,8},{12,14},{14,12},{1,3},{3,1},... | collective-permute-start | bytes 3145736 | tf_op jit(solution)/shard_map/ppermute | solution.py:20
  127.5 0.7 copy-start.16
  127.5 1.1 copy-start.15
  127.5 1.1 copy-start.17
  127.5 1.1 copy-start.18
  127.5 3.6 %copy-start.14 = (f32[64,64]{1,0:T(8,128)S(1)}, f32[64,64]{1,0:T(8,128)}, u32[]{:S(2)}) copy-start(f32[64,64]{1,0:T(8,128)} %param.12) | copy-start | bytes 49156
  142.1 2.4 %copy-start.4 = (bf16[512,2048]{1,0:T(8,128)(2,1)S(1)}, bf16[512,2048]{1,0:T(8,128)(2,1)}, u32[]{:S(2)}) copy-start(bf16[512,2048]{1,0:T(8,128)(2,1)} %copy-done.3) | copy-start | bytes 6291460
  142.1 2.4 %copy-start.6 = (bf16[512,2048]{1,0:T(8,128)(2,1)S(1)}, bf16[512,2048]{1,0:T(8,128)(2,1)}, u32[]{:S(2)}) copy-start(bf16[512,2048]{1,0:T(8,128)(2,1)} %copy-done.5) | copy-start | bytes 6291460
  142.1 2.9 %copy-start.8 = (bf16[512,2048]{1,0:T(8,128)(2,1)S(1)}, bf16[512,2048]{1,0:T(8,128)(2,1)}, u32[]{:S(2)}) copy-start(bf16[512,2048]{1,0:T(8,128)(2,1)} %convolution_convert_fusion.5) | copy-start | bytes 6291460
  142.2 3.5 %copy-start.10 = (bf16[512,2048]{1,0:T(8,128)(2,1)S(1)}, bf16[512,2048]{1,0:T(8,128)(2,1)}, u32[]{:S(2)}) copy-start(bf16[512,2048]{1,0:T(8,128)(2,1)} %copy-done.9) | copy-start | bytes 6291460
  150.0 4.6 %copy-start.13 = (bf16[256,256]{1,0:T(8,128)(2,1)S(1)}, bf16[256,256]{1,0:T(8,128)(2,1)}, u32[]{:S(2)}) copy-start(bf16[256,256]{1,0:T(8,128)(2,1)} %copy-done.12) | copy-start | bytes 393220
  150.0 24.1 %copy-start.1 = (bf16[256,2048]{1,0:T(8,128)(2,1)S(1)}, bf16[256,2048]{1,0:T(8,128)(2,1)}, u32[]{:S(2)}) copy-start(bf16[256,2048]{1,0:T(8,128)(2,1)} %param.8) | copy-start | bytes 3145732
Sparse Core Ops, SparseCore 0:
  127.7 44.2 reduce-scatter.1

commit v11 on v6

--- a/solution.py
+++ b/solution.py
@@ -163,7 +163,16 @@
         inv_both, jnp.concatenate([mix_re, mix_im], axis=0), preferred_element_type=jnp.float32
     ).astype(jnp.bfloat16)
     input_re, input_im = slab_spectrum(fwd_re, fwd_im, inputs)
-    grad_rows = []
+    row_count = lax.axis_size("row")
+    share = LAG_BLOCKS * tok_rows // (row_count * 2)
+    side_zero = lax.axis_index("side") == 0
+    inv_sides = inv_both.reshape(-1, 2, share, inv_both.shape[1])
+    inv_mine = jnp.where(side_zero, inv_sides[:, 0], inv_sides[:, 1]).reshape(-1, inv_both.shape[1])
+    inv_theirs = jnp.where(side_zero, inv_sides[:, 1], inv_sides[:, 0]).reshape(
+        -1, inv_both.shape[1]
+    )
+    mine_rows = []
+    theirs_rows = []
     for lag_block in range(LAG_BLOCKS):
         term_re, term_im = conj_product(
             input_re.astype(jnp.float32),
@@ -172,23 +181,17 @@
             pair_list[lag_block][1],
             dc_row,
         )
-        grad_rows.append(
-            jnp.dot(
-                inv_both,
-                jnp.concatenate([term_re, term_im], axis=0).astype(jnp.bfloat16),
-                preferred_element_type=jnp.float32,
-            )
-        )
-    row_count = lax.axis_size("row")
-    share = lag_rows_total(grad_rows) // (row_count * 2)
-    side_zero = lax.axis_index("side") == 0
+        stacked = jnp.concatenate([term_re, term_im], axis=0).astype(jnp.bfloat16)
+        theirs_rows.append(
+            jnp.dot(inv_theirs, stacked, preferred_element_type=jnp.float32).astype(jnp.bfloat16)
+        )
+        mine_rows.append(jnp.dot(inv_mine, stacked, preferred_element_type=jnp.float32))
     parts = 2 if row_count % 2 == 0 else 1
     reduced = []
     for part in range(parts):
-        chosen = grad_rows[part * LAG_BLOCKS // parts : (part + 1) * LAG_BLOCKS // parts]
-        staged = jnp.concatenate(chosen, axis=0).reshape(-1, 2, share, chan_width)
-        mine = jnp.where(side_zero, staged[:, 0], staged[:, 1])
-        theirs = jnp.where(side_zero, staged[:, 1], staged[:, 0]).astype(jnp.bfloat16)
+        low, high = part * LAG_BLOCKS // parts, (part + 1) * LAG_BLOCKS // parts
+        mine = jnp.concatenate(mine_rows[low:high], axis=0).reshape(-1, share, chan_width)
+        theirs = jnp.concatenate(theirs_rows[low:high], axis=0).reshape(-1, share, chan_width)
         reduced.append(mine + swap_pairs(theirs, SEQ_AXES, 0, 1).astype(jnp.float32))
     by_row = lax.psum_scatter(
         jnp.concatenate(reduced, axis=0).astype(jnp.bfloat16), "row", scatter_dimension=0, tiled=True

time: 174 us -> 173 us (level)
  matrix products: 28.7 us -> 24.2 us
  waiting for transfers between devices: 67.3 us -> 70.8 us
    ppermute x3, waiting for transfers between devices: 21.9 us -> 26 us  [from_behind(): lax.ppermute(value, axis, [(source, source + steps) for source in range(l...]
    dot_general x6, matrix products: 8.31 us -> 4.34 us  [slab_spectrum(): jnp.dot(jnp.concatenate([fwd_re, fwd_im], axis=0), slab_data, preferred_e...]
    dot_general x4 -> x8, matrix products: 2.88 us -> 3.55 us  [the longest x4 1.78 us: on_device(): jnp.dot(inv_theirs, stacked, preferred_element_type=jnp.float32)]
  transfers between devices with their start and end apart: 10 -> 10, of which waited for: 7 -> 7; matrix products, arithmetic and copies ran while one was open for 30% -> 29% of each run, Pallas kernels for 0% -> 0%
where the time goes in v11:
time: 173 us
  waiting for transfers between devices  70.8 us (41%)
  starting transfers between devices  33.1 us (19%)
  other arithmetic  25.7 us (15%)
  matrix products  24.2 us (14%)
  between operations  14.7 us (8%)
  local copies, waits for them, and re-layouts  4.61 us (3%)
    ppermute x5, waiting for transfers between devices, swap_pairs(): lax.ppermute(value, axis, [(source, source ^ 1) for source in range(from_...  29.2 us
    ppermute x5, starting transfers between devices, swap_pairs(): lax.ppermute(value, axis, [(source, source ^ 1) for source in range(from_...  28.3 us
    ppermute x3, waiting for transfers between devices, from_behind(): lax.ppermute(value, axis, [(source, source + steps) for source in range(l...  26 us
    reduce_scatter x1, waiting for transfers between devices, on_device(): lax.psum_scatter(jnp.concatenate(reduced, axis=0).astype(jnp.bfloat16), '...  15.5 us
    dot_general x1, matrix products, filter_taps(): jnp.dot(second_act, w_out, precision=lax.Precision.HIGHEST, preferred_ele...  7.54 us
    another operation x6, other arithmetic  7.37 us
    convert_element_type x1, other arithmetic, on_device(): mix_im = sum_im.astype(jnp.bfloat16)  4.54 us
    dot_general x6, matrix products, slab_spectrum(): jnp.dot(jnp.concatenate([fwd_re, fwd_im], axis=0), slab_data, preferred_e...  4.34 us
  transfers between devices with their start and end apart: 10, of which 7 were waited for; matrix products, arithmetic and copies ran while one was open for 29% of the time, Pallas kernels for 0%

profile of v11, /device:TPU:0, one launch (start us, length us, event | category | flops | bytes accessed | tf_op | source)
XLA Modules:
  0.0 173.0 jit_solution(4370355423401826293)
XLA Ops:
  7.2 0.0 copy-start
  7.2 0.0 reduce-scatter.2.cloned.1.call-start
  7.2 1.4 collective-permute-start
  8.7 2.2 %fusion.107 = (bf16[256,1024]{1,0:T(8,128)(2,1)}, bf16[256,1024]{1,0:T(8,128)(2,1)}) fusion(bf16[256,2048]{1,0:T(8,128)(2,1)} %param.9), kind=kLoop, calls=%fused_computation.220 | loop fusion | bytes 2097152 | tf_op jit(solution)/shard_map/slice | solution.py:34
  10.9 1.3 collective-permute-start.1
  12.2 1.0 fusion.88
  13.3 1.3 multiply_convert_fusion.2
  14.6 0.0 copy-start.11
  14.6 0.1 broadcast_select_fusion
  14.7 1.0 select_convert_fusion
  15.7 0.7 convolution_convert_fusion.5
  16.5 11.6 %collective-permute-done.1 = bf16[256,1024]{1,0:T(8,128)(2,1)} collective-permute-done((bf16[256,1024]{1,0:T(8,128)(2,1)}, bf16[256,1024]{1,0:T(8,128)(2,1)}, u32[]{:S(2)}, u32[]{:S(2)}) %collective-permute-start.1) | collective-permute-done | bytes 524320 | tf_op jit(solution)/shard_map/ppermute | solution.py:15
  28.1 1.3 collective-permute-start.3
  29.4 2.5 %collective-permute-start.2 = (bf16[256,1024]{1,0:T(8,128)(2,1)}, bf16[256,1024]{1,0:T(8,128)(2,1)S(1)}, u32[]{:S(2)}, u32[]{:S(2)}) collective-permute-start(bf16[256,1024]{1,0:T(8,128)(2,1)} %collective-permute-done.1), channel_id=1, source_target_pairs={{0,2},{2,0},{4,6},{6,4},{8,10},{10,8},{12,14},{14,12},{1,3},{3,1},... | collective-permute-start | bytes 1572872 | tf_op jit(solution)/shard_map/ppermute | solution.py:20
  31.9 0.7 convolution_convert_fusion
  32.6 1.1 constant_dynamic-update-slice_fusion.3
  33.7 9.4 %collective-permute-done.3 = bf16[256,1024]{1,0:T(8,128)(2,1)S(1)} collective-permute-done((bf16[256,1024]{1,0:T(8,128)(2,1)S(1)}, bf16[256,1024]{1,0:T(8,128)(2,1)S(1)}, u32[]{:S(2)}, u32[]{:S(2)}) %collective-permute-start.3) | collective-permute-done | bytes 524320 | tf_op jit(solution)/shard_map/ppermute | solution.py:15
  43.1 2.1 %collective-permute-start.4 = (bf16[256,1024]{1,0:T(8,128)(2,1)S(1)}, bf16[256,1024]{1,0:T(8,128)(2,1)S(1)}, u32[]{:S(2)}, u32[]{:S(2)}) collective-permute-start(bf16[256,1024]{1,0:T(8,128)(2,1)S(1)} %collective-permute-done.3), channel_id=1, source_target_pairs={{0,2},{2,0},{4,6},{6,4},{8,10},{10,8},{12,14},{14,12},{1,3},{3,1},... | collective-permute-start | bytes 1572872 | tf_op jit(solution)/shard_map/ppermute | solution.py:20
  45.2 1.3 collective-permute-start.6
  46.5 0.5 collective-permute-done.2
  47.1 0.7 convolution_convert_fusion.3
  47.8 9.6 %collective-permute-done.4 = bf16[256,1024]{1,0:T(8,128)(2,1)S(1)} collective-permute-done((bf16[256,1024]{1,0:T(8,128)(2,1)S(1)}, bf16[256,1024]{1,0:T(8,128)(2,1)S(1)}, u32[]{:S(2)}, u32[]{:S(2)}) %collective-permute-start.4) | collective-permute-done | bytes 524320 | tf_op jit(solution)/shard_map/ppermute | solution.py:20
  57.5 0.9 collective-permute-start.5
  58.4 0.7 convolution_convert_fusion.4
  59.2 1.7 fusion.28
  60.9 1.7 fusion.23
  62.5 0.4 convolution_convert_fusion.9
  63.0 0.4 convolution_convert_fusion.10
  63.5 0.1 pad_maximum_fusion.15
  63.6 0.2 collective-permute-start.7
  63.8 0.4 fusion.47
  64.2 0.4 fusion.48
  64.7 0.2 pad_maximum_fusion.2
  64.9 5.0 %collective-permute-done.6 = bf16[256,2048]{1,0:T(8,128)(2,1)S(1)} collective-permute-done((bf16[256,2048]{1,0:T(8,128)(2,1)S(1)}, bf16[256,2048]{1,0:T(8,128)(2,1)S(1)}, u32[]{:S(2)}, u32[]{:S(2)}) %collective-permute-start.6) | collective-permute-done | bytes 1048608 | tf_op jit(solution)/shard_map/ppermute | solution.py:15
  69.9 0.7 convolution_convert_fusion.1
  70.7 0.7 convolution_convert_fusion.2
  71.4 1.7 fusion.33
  73.2 1.7 fusion.38
  74.9 0.4 convolution_convert_fusion.7
  75.4 0.4 convolution_convert_fusion.8
  75.8 0.1 pad_maximum_fusion.16
  75.9 22.1 %collective-permute-start.8 = (bf16[2,128,2048]{2,1,0:T(8,128)(2,1)S(1)}, bf16[2,128,2048]{2,1,0:T(8,128)(2,1)S(1)}, u32[]{:S(2)}, u32[]{:S(2)}) collective-permute-start(bf16[2,128,2048]{2,1,0:T(8,128)(2,1)S(1)} %bitcast.101), channel_id=1, source_target_pairs={{0,2},{2,0},{4,6},{6,4},{8,10},{10,8},{12,14},{14,12},{1,3},{3,1},... | collective-permute-start | bytes 3145736 | tf_op jit(solution)/shard_map/ppermute | solution.py:20
  98.0 0.4 fusion.45
  98.5 0.4 fusion.46
  98.9 0.2 pad_maximum_fusion.5
  99.1 0.3 add_convert_fusion.1
  99.4 19.0 %collective-permute-done.8 = bf16[2,128,2048]{2,1,0:T(8,128)(2,1)S(1)} collective-permute-done((bf16[2,128,2048]{2,1,0:T(8,128)(2,1)S(1)}, bf16[2,128,2048]{2,1,0:T(8,128)(2,1)S(1)}, u32[]{:S(2)}, u32[]{:S(2)}) %collective-permute-start.8) | collective-permute-done | bytes 1048608 | tf_op jit(solution)/shard_map/ppermute | solution.py:20
  118.5 0.3 add_convert_fusion
  118.8 1.6 pad_maximum_fusion.6
  120.4 0.0 copy-start.17
  120.4 0.0 reduce-scatter.2.cloned.1.call-update
  120.4 0.3 fusion.96
  120.8 1.4 multiply_convert_fusion.3
  122.2 2.5 %fusion.51 = f32[1024,64]{1,0:T(8,128)S(1)} fusion(f32[33,64]{1,0:T(8,128)S(1)} %copy-done.13, f32[64]{0:T(128)S(1)} %copy-done.16, f32[64]{0:T(128)S(1)} %copy-done.15, f32[1024,16]{0,1:T(8,128)S(1)} %get-tuple-element.21, f32[1024,16]{0,1:T(8,128)S(1)} %get-tuple-element.20, f32[1024,1]{0,1:T(1,128)S(1)} %convert_multiply_fusion.38), kind=kOutput, calls=%fused_computation.119 | convolution fusion | flops 26150912 | bytes 406272 | tf_op jit(solution)/shard_map/dot_general | solution.py:80
  124.7 2.2 %fusion.49 = f32[1024,64]{1,0:T(8,128)S(1)} fusion(f32[1024,64]{1,0:T(8,128)S(1)} %fusion.51, f32[64,64]{1,0:T(8,128)S(1)} %copy-done.12, f32[64]{0:T(128)S(1)} %copy-done.15), kind=kOutput, calls=%fused_computation.117 | convolution fusion | flops 50397184 | bytes 540928 | tf_op jit(solution)/shard_map/dot_general | solution.py:88
  126.9 7.5 %multiply_convert_fusion = bf16[1024,2048]{1,0:T(8,128)(2,1)S(1)} fusion(f32[1024,64]{1,0:T(8,128)S(1)} %fusion.49, f32[64,2048]{1,0:T(8,128)S(1)} %copy-done.17, f32[1024]{0:T(1024)S(1)} %iota_convert_fusion, f32[2048]{0:T(1024)S(1)} %neg.7), kind=kOutput, calls=%fused_computation.1 | convolution fusion | flops 1616904192 | bytes 4993024 | tf_op jit(solution)/shard_map/dot_general | solution.py:92
  134.5 2.4 %convert_bitcast_fusion = bf16[4,512,2048]{2,1,0:T(8,128)(2,1)S(1)} fusion(bf16[4,256,2048]{2,1,0:T(8,128)(2,1)S(1)} %bitcast.97, bf16[256,256]{1,0:T(8,128)(2,1)S(1)} %select_convert_fusion, bf16[256,256]{1,0:T(8,128)(2,1)S(1)} %fusion.88), kind=kOutput, calls=%fused_computation | convolution fusion | flops 2152202240 | bytes 12845056 | tf_op jit(solution)/shard_map/fs,jsc->jfc/dot_general | solution.py:115
  136.9 0.5 copy-done.7
  137.4 0.6 copy-done.9
  138.0 4.3 %fusion.6 = bf16[256,2048]{1,0:T(8,128)(2,1)S(1)} fusion(f32[256]{0:T(256)S(1)} %compare_select_fusion.1, pred[256]{0:T(512)(128)(4,1)S(1)} %iota_compare_fusion, bf16[4,512,2048]{2,1,0:T(8,128)(2,1)S(1)} %convert_bitcast_fusion, bf16[512,2048]{1,0:T(8,128)(2,1)S(1)} %copy-done.9, bf16[512,2048]{1,0:T(8,128)(2,1)S(1)} %copy-done.7, ...), kind=kLoop, calls=%fused_computation.63 | loop fusion | flops 28311552 | bytes 19924224 | tf_op jit(solution)/shard_map/convert_element_type | solution.py:159
  142.3 4.5 %fusion.12 = bf16[256,2048]{1,0:T(8,128)(2,1)S(1)} fusion(f32[256]{0:T(256)S(1)} %compare_select_fusion.1, pred[256]{0:T(512)(128)(4,1)S(1)} %iota_compare_fusion, bf16[4,512,2048]{2,1,0:T(8,128)(2,1)S(1)} %convert_bitcast_fusion, bf16[512,2048]{1,0:T(8,128)(2,1)S(1)} %copy-done.9, bf16[512,2048]{1,0:T(8,128)(2,1)S(1)} %copy-done.7, ...), kind=kLoop, calls=%fused_computation.69 | loop fusion | flops 30408704 | bytes 19924224 | tf_op jit(solution)/shard_map/convert_element_type | solution.py:160
  146.9 1.7 convolution_convert_fusion.6
  148.6 15.5 %reduce-scatter.2.cloned.1.call-done = bf16[1,128,2048]{2,1,0:T(8,128)(2,1)} async-done(((bf16[4,128,2048]{2,1,0:T(8,128)(2,1)}), bf16[1,128,2048]{2,1,0:T(8,128)(2,1)}) %reduce-scatter.2.cloned.1.call-update) | async-done | bytes 524304 | tf_op jit(solution)/shard_map/reduce_scatter | solution.py:196
  164.1 2.1 %bitcast_convert_fusion = f32[128,2048]{1,0:T(8,128)} fusion(bf16[1,128,2048]{2,1,0:T(8,128)(2,1)} %reduce-scatter.2.cloned.1.call-done), kind=kLoop, calls=%fused_computation.134 | loop fusion | flops 262144 | bytes 1572864 | tf_op jit(solution)/shard_map/convert_element_type | solution.py:199
  (46 shorter events, 0.2 us)
Async XLA Ops:
  7.2 24.7 %copy-start = (bf16[256,2048]{1,0:T(8,128)(2,1)S(1)}, bf16[256,2048]{1,0:T(8,128)(2,1)}, u32[]{:S(2)}) copy-start(bf16[256,2048]{1,0:T(8,128)(2,1)} %param.8) | copy-start | bytes 3145732
  7.2 8.5 %copy-start.10 = (bf16[256,2048]{1,0:T(8,128)(2,1)S(1)}, bf16[256,2048]{1,0:T(8,128)(2,1)}, u32[]{:S(2)}) copy-start(bf16[256,2048]{1,0:T(8,128)(2,1)} %param.9) | copy-start | bytes 3145732
  7.2 6.1 %copy-start.14 = (f32[2048]{0:T(1024)S(1)}, f32[2048]{0:T(1024)}, u32[]{:S(2)}) copy-start(f32[2048]{0:T(1024)} %param.15) | copy-start | bytes 24580
  7.2 156.9 %reduce-scatter.2.cloned.1.call-start = ((), (), s32[]{:S(2)}) async-start(), calls=%async_computation.1 | async-start | bytes 2621440 | tf_op jit(solution)/shard_map/reduce_scatter | solution.py:196
  7.2 51.2 %collective-permute-start = (bf16[256,2048]{1,0:T(8,128)(2,1)}, bf16[256,2048]{1,0:T(8,128)(2,1)S(1)}, u32[]{:S(2)}, u32[]{:S(2)}) collective-permute-start(bf16[256,2048]{1,0:T(8,128)(2,1)} %param.9), channel_id=1, source_target_pairs={{2,0},{6,4},{10,8},{14,12},{3,1},{7,5},{11,9},{15,13},{18,16},{22,... | collective-permute-start | bytes 3145736 | tf_op jit(solution)/shard_map/ppermute | solution.py:20
  10.9 17.2 %collective-permute-start.1 = (bf16[256,1024]{1,0:T(8,128)(2,1)}, bf16[256,1024]{1,0:T(8,128)(2,1)}, u32[]{:S(2)}, u32[]{:S(2)}) collective-permute-start(bf16[256,1024]{1,0:T(8,128)(2,1)} %get-tuple-element.15), channel_id=1, source_target_pairs={{4,0},{6,2},{8,4},{10,6},{12,8},{14,10},{5,1},{7,3},{9,5},{11,7},{... | collective-permute-start | bytes 1572872 | tf_op jit(solution)/shard_map/ppermute | solution.py:15
  14.6 13.5 %copy-start.11 = (bf16[256,1024]{1,0:T(8,128)(2,1)S(1)}, bf16[256,1024]{1,0:T(8,128)(2,1)}, u32[]{:S(2)}) copy-start(bf16[256,1024]{1,0:T(8,128)(2,1)} %get-tuple-element.5) | copy-start | bytes 1572868
  16.5 44.4 %copy-start.6 = (bf16[512,2048]{1,0:T(8,128)(2,1)}, bf16[512,2048]{1,0:T(8,128)(2,1)S(1)}, u32[]{:S(2)}) copy-start(bf16[512,2048]{1,0:T(8,128)(2,1)S(1)} %convolution_convert_fusion.5) | copy-start | bytes 6291460
  28.1 15.0 %collective-permute-start.3 = (bf16[256,1024]{1,0:T(8,128)(2,1)S(1)}, bf16[256,1024]{1,0:T(8,128)(2,1)S(1)}, u32[]{:S(2)}, u32[]{:S(2)}) collective-permute-start(bf16[256,1024]{1,0:T(8,128)(2,1)S(1)} %copy-done.11), channel_id=1, source_target_pairs={{4,0},{6,2},{8,4},{10,6},{12,8},{14,10},{5,1},{7,3},{9,5},{11,7},{... | collective-permute-start | bytes 1572872 | tf_op jit(solution)/shard_map/ppermute | solution.py:15
  29.4 17.7 %collective-permute-start.2 = (bf16[256,1024]{1,0:T(8,128)(2,1)}, bf16[256,1024]{1,0:T(8,128)(2,1)S(1)}, u32[]{:S(2)}, u32[]{:S(2)}) collective-permute-start(bf16[256,1024]{1,0:T(8,128)(2,1)} %collective-permute-done.1), channel_id=1, source_target_pairs={{0,2},{2,0},{4,6},{6,4},{8,10},{10,8},{12,14},{14,12},{1,3},{3,1},... | collective-permute-start | bytes 1572872 | tf_op jit(solution)/shard_map/ppermute | solution.py:20
  43.1 14.4 %collective-permute-start.4 = (bf16[256,1024]{1,0:T(8,128)(2,1)S(1)}, bf16[256,1024]{1,0:T(8,128)(2,1)S(1)}, u32[]{:S(2)}, u32[]{:S(2)}) collective-permute-start(bf16[256,1024]{1,0:T(8,128)(2,1)S(1)} %collective-permute-done.3), channel_id=1, source_target_pairs={{0,2},{2,0},{4,6},{6,4},{8,10},{10,8},{12,14},{14,12},{1,3},{3,1},... | collective-permute-start | bytes 1572872 | tf_op jit(solution)/shard_map/ppermute | solution.py:20
  45.2 24.7 %collective-permute-start.6 = (bf16[256,2048]{1,0:T(8,128)(2,1)S(1)}, bf16[256,2048]{1,0:T(8,128)(2,1)S(1)}, u32[]{:S(2)}, u32[]{:S(2)}) collective-permute-start(bf16[256,2048]{1,0:T(8,128)(2,1)S(1)} %constant_dynamic-update-slice_fusion.2), channel_id=1, source_target_pairs={{4,0},{6,2},{8,4},{10,6},{12,8},{14,10},{5,1},{7,3},{9,5},{11,7},{... | collective-permute-start | bytes 3145736 | tf_op jit(solution)/shard_map/ppermute | solution.py:15
  47.8 23.6 %copy-start.4 = (bf16[512,2048]{1,0:T(8,128)(2,1)}, bf16[512,2048]{1,0:T(8,128)(2,1)S(1)}, u32[]{:S(2)}) copy-start(bf16[512,2048]{1,0:T(8,128)(2,1)S(1)} %convolution_convert_fusion.3) | copy-start | bytes 6291460
  57.5 13.2 %collective-permute-start.5 = (bf16[256,2048]{1,0:T(8,128)(2,1)S(1)}, bf16[256,2048]{1,0:T(8,128)(2,1)S(1)}, u32[]{:S(2)}, u32[]{:S(2)}) collective-permute-start(bf16[256,2048]{1,0:T(8,128)(2,1)S(1)} %constant_dynamic-update-slice_fusion), channel_id=1, source_target_pairs={{6,2},{10,6},{14,10},{7,3},{11,7},{15,11},{22,18},{26,22},{30,26},... | collective-permute-start | bytes 3145736 | tf_op jit(solution)/shard_map/ppermute | solution.py:42
  63.6 35.6 %collective-permute-start.7 = (bf16[2,128,2048]{2,1,0:T(8,128)(2,1)S(1)}, bf16[2,128,2048]{2,1,0:T(8,128)(2,1)S(1)}, u32[]{:S(2)}, u32[]{:S(2)}) collective-permute-start(bf16[2,128,2048]{2,1,0:T(8,128)(2,1)S(1)} %bitcast.100), channel_id=1, source_target_pairs={{0,2},{2,0},{4,6},{6,4},{8,10},{10,8},{12,14},{14,12},{1,3},{3,1},... | collective-permute-start | bytes 3145736 | tf_op jit(solution)/shard_map/ppermute | solution.py:20
  70.7 2.5 %copy-start.8 = (bf16[512,2048]{1,0:T(8,128)(2,1)}, bf16[512,2048]{1,0:T(8,128)(2,1)S(1)}, u32[]{:S(2)}) copy-start(bf16[512,2048]{1,0:T(8,128)(2,1)S(1)} %convolution_convert_fusion.1) | copy-start | bytes 6291460
  71.4 1.8 %copy-start.2 = (bf16[512,2048]{1,0:T(8,128)(2,1)}, bf16[512,2048]{1,0:T(8,128)(2,1)S(1)}, u32[]{:S(2)}) copy-start(bf16[512,2048]{1,0:T(8,128)(2,1)S(1)} %convolution_convert_fusion.2) | copy-start | bytes 6291460
  75.9 42.5 %collective-permute-start.8 = (bf16[2,128,2048]{2,1,0:T(8,128)(2,1)S(1)}, bf16[2,128,2048]{2,1,0:T(8,128)(2,1)S(1)}, u32[]{:S(2)}, u32[]{:S(2)}) collective-permute-start(bf16[2,128,2048]{2,1,0:T(8,128)(2,1)S(1)} %bitcast.101), channel_id=1, source_target_pairs={{0,2},{2,0},{4,6},{6,4},{8,10},{10,8},{12,14},{14,12},{1,3},{3,1},... | collective-permute-start | bytes 3145736 | tf_op jit(solution)/shard_map/ppermute | solution.py:20
  120.3 1.8 %copy-start.13 = (f32[33,64]{1,0:T(8,128)S(1)}, f32[33,64]{1,0:T(8,128)}, u32[]{:S(2)}) copy-start(f32[33,64]{1,0:T(8,128)} %param.10) | copy-start | bytes 25348
  120.3 1.8 %copy-start.15 = (f32[64]{0:T(128)S(1)}, f32[64]{0:T(128)}, u32[]{:S(2)}) copy-start(f32[64]{0:T(128)} %param.13) | copy-start | bytes 772
  120.3 1.9 %copy-start.16 = (f32[64]{0:T(128)S(1)}, f32[64]{0:T(128)}, u32[]{:S(2)}) copy-start(f32[64]{0:T(128)} %param.11) | copy-start | bytes 772
  120.3 4.4 %copy-start.12 = (f32[64,64]{1,0:T(8,128)S(1)}, f32[64,64]{1,0:T(8,128)}, u32[]{:S(2)}) copy-start(f32[64,64]{1,0:T(8,128)} %param.12) | copy-start | bytes 49156
  120.4 6.6 %copy-start.17 = (f32[64,2048]{1,0:T(8,128)S(1)}, f32[64,2048]{1,0:T(8,128)}, u32[]{:S(2)}) copy-start(f32[64,2048]{1,0:T(8,128)} %param.14) | copy-start | bytes 1572868
  134.5 2.4 %copy-start.3 = (bf16[512,2048]{1,0:T(8,128)(2,1)S(1)}, bf16[512,2048]{1,0:T(8,128)(2,1)}, u32[]{:S(2)}) copy-start(bf16[512,2048]{1,0:T(8,128)(2,1)} %copy-done.2) | copy-start | bytes 6291460
  134.5 2.4 %copy-start.5 = (bf16[512,2048]{1,0:T(8,128)(2,1)S(1)}, bf16[512,2048]{1,0:T(8,128)(2,1)}, u32[]{:S(2)}) copy-start(bf16[512,2048]{1,0:T(8,128)(2,1)} %copy-done.4) | copy-start | bytes 6291460
  134.5 2.9 %copy-start.7 = (bf16[512,2048]{1,0:T(8,128)(2,1)S(1)}, bf16[512,2048]{1,0:T(8,128)(2,1)}, u32[]{:S(2)}) copy-start(bf16[512,2048]{1,0:T(8,128)(2,1)} %copy-done.6) | copy-start | bytes 6291460
  134.5 3.5 %copy-start.9 = (bf16[512,2048]{1,0:T(8,128)(2,1)S(1)}, bf16[512,2048]{1,0:T(8,128)(2,1)}, u32[]{:S(2)}) copy-start(bf16[512,2048]{1,0:T(8,128)(2,1)} %copy-done.8) | copy-start | bytes 6291460
  146.9 19.3 %copy-start.1 = (bf16[256,2048]{1,0:T(8,128)(2,1)S(1)}, bf16[256,2048]{1,0:T(8,128)(2,1)}, u32[]{:S(2)}) copy-start(bf16[256,2048]{1,0:T(8,128)(2,1)} %param.8) | copy-start | bytes 3145732
Sparse Core Ops, SparseCore 0:
  120.5 43.5 reduce-scatter.1

commit v12 on v11

--- a/solution.py
+++ b/solution.py
@@ -172,7 +172,6 @@
         -1, inv_both.shape[1]
     )
     mine_rows = []
-    theirs_rows = []
     for lag_block in range(LAG_BLOCKS):
         term_re, term_im = conj_product(
             input_re.astype(jnp.float32),
@@ -181,17 +180,18 @@
             pair_list[lag_block][1],
             dc_row,
         )
-        stacked = jnp.concatenate([term_re, term_im], axis=0).astype(jnp.bfloat16)
-        theirs_rows.append(
-            jnp.dot(inv_theirs, stacked, preferred_element_type=jnp.float32).astype(jnp.bfloat16)
-        )
-        mine_rows.append(jnp.dot(inv_mine, stacked, preferred_element_type=jnp.float32))
+        mine_rows.append(jnp.concatenate([term_re, term_im], axis=0).astype(jnp.bfloat16))
     parts = 2 if row_count % 2 == 0 else 1
     reduced = []
     for part in range(parts):
         low, high = part * LAG_BLOCKS // parts, (part + 1) * LAG_BLOCKS // parts
-        mine = jnp.concatenate(mine_rows[low:high], axis=0).reshape(-1, share, chan_width)
-        theirs = jnp.concatenate(theirs_rows[low:high], axis=0).reshape(-1, share, chan_width)
+        stacked = jnp.stack(mine_rows[low:high], axis=0)
+        theirs = jnp.einsum(
+            "rk,jkc->jrc", inv_theirs, stacked, preferred_element_type=jnp.float32
+        ).astype(jnp.bfloat16).reshape(-1, share, chan_width)
+        mine = jnp.einsum(
+            "rk,jkc->jrc", inv_mine, stacked, preferred_element_type=jnp.float32
+        ).reshape(-1, share, chan_width)
         reduced.append(mine + swap_pairs(theirs, SEQ_AXES, 0, 1).astype(jnp.float32))
     by_row = lax.psum_scatter(
         jnp.concatenate(reduced, axis=0).astype(jnp.bfloat16), "row", scatter_dimension=0, tiled=True

time: 173 us -> 176 us (1.017)
  matrix products: 24.2 us -> 28.1 us
  other arithmetic: 25.7 us -> 23.4 us
    another operation x6 -> x0, other arithmetic: 7.37 us -> none
    concatenate x4 -> x5, other arithmetic: 0.63 us -> 6.7 us  [the longest x4 6.68 us: on_device(): jnp.concatenate([term_re, term_im], axis=0).astype(jnp.bfloat16)]
    dot_general x8 -> x4, matrix products: 3.55 us -> 6.25 us  [the longest x2 3.13 us: on_device(): jnp.einsum('rk,jkc->jrc', inv_theirs, stacked, preferred_element_type=jnp...]
  transfers between devices with their start and end apart: 10 -> 10, of which waited for: 7 -> 6; matrix products, arithmetic and copies ran while one was open for 29% -> 28% of each run, Pallas kernels for 0% -> 0%
where the time goes in v12:
time: 176 us
  waiting for transfers between devices  70.2 us (40%)
  starting transfers between devices  34.7 us (20%)
  matrix products  28.1 us (16%)
  other arithmetic  23.4 us (13%)
  between operations  14.6 us (8%)
  local copies, waits for them, and re-layouts  4.69 us (3%)
    ppermute x5, starting transfers between devices, swap_pairs(): lax.ppermute(value, axis, [(source, source ^ 1) for source in range(from_...  29.9 us
    ppermute x5, waiting for transfers between devices, swap_pairs(): lax.ppermute(value, axis, [(source, source ^ 1) for source in range(from_...  28.4 us
    ppermute x3, waiting for transfers between devices, from_behind(): lax.ppermute(value, axis, [(source, source + steps) for source in range(l...  26.4 us
    reduce_scatter x1, waiting for transfers between devices, on_device(): lax.psum_scatter(jnp.concatenate(reduced, axis=0).astype(jnp.bfloat16), '...  15.5 us
    dot_general x1, matrix products, filter_taps(): jnp.dot(second_act, w_out, precision=lax.Precision.HIGHEST, preferred_ele...  7.54 us
    concatenate x4, other arithmetic, on_device(): jnp.concatenate([term_re, term_im], axis=0).astype(jnp.bfloat16)  6.68 us
    dot_general x6, matrix products, slab_spectrum(): jnp.dot(jnp.concatenate([fwd_re, fwd_im], axis=0), slab_data, preferred_e...  5.57 us
    convert_element_type x1, other arithmetic, on_device(): mix_im = sum_im.astype(jnp.bfloat16)  4.54 us
  transfers between devices with their start and end apart: 10, of which 6 were waited for; matrix products, arithmetic and copies ran while one was open for 28% of the time, Pallas kernels for 0%

profile of v12, /device:TPU:0, one launch (start us, length us, event | category | flops | bytes accessed | tf_op | source)
XLA Modules:
  0.0 175.7 jit_solution(5473420958678416533)
XLA Ops:
  7.2 0.0 copy-start
  7.2 0.0 copy-start.9
  7.2 0.0 reduce-scatter.2.cloned.1.call-start
  7.2 1.4 collective-permute-start
  8.7 2.1 %fusion.105 = (bf16[256,1024]{1,0:T(8,128)(2,1)S(1)}, bf16[256,1024]{1,0:T(8,128)(2,1)}) fusion(bf16[256,2048]{1,0:T(8,128)(2,1)} %param.9), kind=kLoop, calls=%fused_computation.212 | loop fusion | bytes 2097152 | tf_op jit(solution)/shard_map/slice | solution.py:34
  10.7 1.3 collective-permute-start.1
  12.0 1.0 fusion.90
  13.1 1.3 multiply_convert_fusion.2
  14.4 1.0 select_convert_fusion
  15.4 0.0 copy-done.9
  15.5 0.7 convolution_convert_fusion.5
  16.2 0.0 copy-start.5
  16.2 11.6 %collective-permute-done.1 = bf16[256,1024]{1,0:T(8,128)(2,1)S(1)} collective-permute-done((bf16[256,1024]{1,0:T(8,128)(2,1)}, bf16[256,1024]{1,0:T(8,128)(2,1)S(1)}, u32[]{:S(2)}, u32[]{:S(2)}) %collective-permute-start.1) | collective-permute-done | bytes 524320 | tf_op jit(solution)/shard_map/ppermute | solution.py:15
  27.8 1.3 collective-permute-start.3
  29.1 3.4 %collective-permute-start.2 = (bf16[256,1024]{1,0:T(8,128)(2,1)S(1)}, bf16[256,1024]{1,0:T(8,128)(2,1)S(1)}, u32[]{:S(2)}, u32[]{:S(2)}) collective-permute-start(bf16[256,1024]{1,0:T(8,128)(2,1)S(1)} %collective-permute-done.1), channel_id=1, source_target_pairs={{0,2},{2,0},{4,6},{6,4},{8,10},{10,8},{12,14},{14,12},{1,3},{3,1},... | collective-permute-start | bytes 1572872 | tf_op jit(solution)/shard_map/ppermute | solution.py:20
  32.5 0.0 copy-done
  32.5 0.7 convolution_convert_fusion
  33.3 9.6 %collective-permute-done.3 = bf16[256,1024]{1,0:T(8,128)(2,1)S(1)} collective-permute-done((bf16[256,1024]{1,0:T(8,128)(2,1)S(1)}, bf16[256,1024]{1,0:T(8,128)(2,1)S(1)}, u32[]{:S(2)}, u32[]{:S(2)}) %collective-permute-start.3) | collective-permute-done | bytes 524320 | tf_op jit(solution)/shard_map/ppermute | solution.py:15
  42.9 2.9 %collective-permute-start.4 = (bf16[256,1024]{1,0:T(8,128)(2,1)S(1)}, bf16[256,1024]{1,0:T(8,128)(2,1)S(1)}, u32[]{:S(2)}, u32[]{:S(2)}) collective-permute-start(bf16[256,1024]{1,0:T(8,128)(2,1)S(1)} %collective-permute-done.3), channel_id=1, source_target_pairs={{0,2},{2,0},{4,6},{6,4},{8,10},{10,8},{12,14},{14,12},{1,3},{3,1},... | collective-permute-start | bytes 1572872 | tf_op jit(solution)/shard_map/ppermute | solution.py:20
  45.9 1.3 collective-permute-start.6
  47.1 0.0 collective-permute-done.2
  47.2 0.7 convolution_convert_fusion.3
  47.9 0.0 copy-start.3
  47.9 9.5 %collective-permute-done.4 = bf16[256,1024]{1,0:T(8,128)(2,1)S(1)} collective-permute-done((bf16[256,1024]{1,0:T(8,128)(2,1)S(1)}, bf16[256,1024]{1,0:T(8,128)(2,1)S(1)}, u32[]{:S(2)}, u32[]{:S(2)}) %collective-permute-start.4) | collective-permute-done | bytes 524320 | tf_op jit(solution)/shard_map/ppermute | solution.py:20
  57.5 0.9 collective-permute-start.5
  58.4 0.0 collective-permute-done
  58.4 2.0 %convolution_convert_fusion.4 = bf16[512,2048]{1,0:T(8,128)(2,1)S(1)} fusion(bf16[256,2048]{1,0:T(8,128)(2,1)} %collective-permute-done, bf16[256,2048]{1,0:T(8,128)(2,1)S(1)} %constant_dynamic-update-slice_fusion, pred[]{:T(512)S(6)} %eq.98, bf16[256,256]{1,0:T(8,128)(2,1)S(1)} %select_convert_fusion, bf16[256,256]{1,0:T(8,128)(2,1)S(1)} %fusion.90), kind=kOutput, calls=%fused_computation.24 | convolution fusion | flops 538968064 | bytes 4456449 | tf_op jit(solution)/shard_map/dot_general | solution.py:107
  60.4 1.7 fusion.52
  62.1 0.0 copy-done.5
  62.1 1.7 fusion.53
  63.7 1.6 fusion
  65.3 0.1 collective-permute-start.7
  65.4 5.2 %collective-permute-done.6 = bf16[256,2048]{1,0:T(8,128)(2,1)S(1)} collective-permute-done((bf16[256,2048]{1,0:T(8,128)(2,1)S(1)}, bf16[256,2048]{1,0:T(8,128)(2,1)S(1)}, u32[]{:S(2)}, u32[]{:S(2)}) %collective-permute-start.6) | collective-permute-done | bytes 1048608 | tf_op jit(solution)/shard_map/ppermute | solution.py:15
  70.6 0.7 convolution_convert_fusion.1
  71.3 0.0 collective-permute-done.5
  71.3 0.7 convolution_convert_fusion.2
  72.1 0.0 copy-done.3
  72.1 0.0 copy-start.1
  72.1 1.7 fusion.51
  73.8 1.7 fusion.50
  75.5 0.0 copy-start.12
  75.5 1.6 fusion.1
  77.1 22.1 %collective-permute-start.8 = (bf16[2,128,2048]{1,2,0:T(8,128)(2,1)S(1)}, bf16[2,128,2048]{1,2,0:T(8,128)(2,1)S(1)}, u32[]{:S(2)}, u32[]{:S(2)}) collective-permute-start(bf16[2,128,2048]{1,2,0:T(8,128)(2,1)S(1)} %fusion.1), channel_id=1, source_target_pairs={{0,2},{2,0},{4,6},{6,4},{8,10},{10,8},{12,14},{14,12},{1,3},{3,1},... | collective-permute-start | bytes 3145736 | tf_op jit(solution)/shard_map/ppermute | solution.py:20
  99.2 0.0 collective-permute-done.7
  99.2 1.6 add_convert_fusion.1
  100.8 18.8 %collective-permute-done.8 = bf16[2,128,2048]{1,2,0:T(8,128)(2,1)S(1)} collective-permute-done((bf16[2,128,2048]{1,2,0:T(8,128)(2,1)S(1)}, bf16[2,128,2048]{1,2,0:T(8,128)(2,1)S(1)}, u32[]{:S(2)}, u32[]{:S(2)}) %collective-permute-start.8) | collective-permute-done | bytes 1048608 | tf_op jit(solution)/shard_map/ppermute | solution.py:20
  119.6 1.5 add_convert_fusion
  121.2 1.6 pad_maximum_fusion
  122.7 0.0 reduce-scatter.2.cloned.1.call-update
  122.8 0.0 copy-start.15
  122.8 0.3 fusion.98
  123.1 1.4 multiply_convert_fusion.3
  124.6 2.5 %fusion.49 = f32[1024,64]{1,0:T(8,128)S(1)} fusion(f32[33,64]{1,0:T(8,128)S(1)} %copy-done.11, f32[64]{0:T(128)S(1)} %copy-done.14, f32[64]{0:T(128)S(1)} %copy-done.13, f32[1024,16]{0,1:T(8,128)S(1)} %get-tuple-element.25, f32[1024,16]{0,1:T(8,128)S(1)} %get-tuple-element.24, f32[1024,1]{0,1:T(1,128)S(1)} %convert_multiply_fusion.38), kind=kOutput, calls=%fused_computation.113 | convolution fusion | flops 26150912 | bytes 406272 | tf_op jit(solution)/shard_map/dot_general | solution.py:80
  127.1 2.2 %fusion.47 = f32[1024,64]{1,0:T(8,128)S(1)} fusion(f32[1024,64]{1,0:T(8,128)S(1)} %fusion.49, f32[64,64]{1,0:T(8,128)S(1)} %copy-done.10, f32[64]{0:T(128)S(1)} %copy-done.13), kind=kOutput, calls=%fused_computation.111 | convolution fusion | flops 50397184 | bytes 540928 | tf_op jit(solution)/shard_map/dot_general | solution.py:88
  129.3 7.5 %multiply_convert_fusion = bf16[1024,2048]{1,0:T(8,128)(2,1)S(1)} fusion(f32[1024,64]{1,0:T(8,128)S(1)} %fusion.47, f32[64,2048]{1,0:T(8,128)S(1)} %copy-done.15, f32[1024]{0:T(1024)S(1)} %iota_convert_fusion, f32[2048]{0:T(1024)S(1)} %neg.7), kind=kOutput, calls=%fused_computation.1 | convolution fusion | flops 1616904192 | bytes 4993024 | tf_op jit(solution)/shard_map/dot_general | solution.py:92
  136.9 2.4 %convert_bitcast_fusion = bf16[4,512,2048]{2,1,0:T(8,128)(2,1)S(1)} fusion(bf16[4,256,2048]{2,1,0:T(8,128)(2,1)S(1)} %bitcast.117, bf16[256,256]{1,0:T(8,128)(2,1)S(1)} %select_convert_fusion, bf16[256,256]{1,0:T(8,128)(2,1)S(1)} %fusion.90), kind=kOutput, calls=%fused_computation | convolution fusion | flops 2152202240 | bytes 12845056 | tf_op jit(solution)/shard_map/fs,jsc->jfc/dot_general | solution.py:115
  139.3 0.5 copy-done.6
  139.8 0.6 copy-done.8
  140.4 4.3 %fusion.8 = bf16[256,2048]{1,0:T(8,128)(2,1)S(1)} fusion(f32[256]{0:T(256)S(1)} %compare_select_fusion.1, pred[256]{0:T(512)(128)(4,1)S(1)} %iota_compare_fusion, bf16[4,512,2048]{2,1,0:T(8,128)(2,1)S(1)} %convert_bitcast_fusion, bf16[512,2048]{1,0:T(8,128)(2,1)S(1)} %copy-done.8, bf16[512,2048]{1,0:T(8,128)(2,1)S(1)} %copy-done.6, ...), kind=kLoop, calls=%fused_computation.67 | loop fusion | flops 28311552 | bytes 19924224 | tf_op jit(solution)/shard_map/convert_element_type | solution.py:159
  144.7 4.5 %fusion.14 = bf16[256,2048]{1,0:T(8,128)(2,1)S(1)} fusion(f32[256]{0:T(256)S(1)} %compare_select_fusion.1, pred[256]{0:T(512)(128)(4,1)S(1)} %iota_compare_fusion, bf16[4,512,2048]{2,1,0:T(8,128)(2,1)S(1)} %convert_bitcast_fusion, bf16[512,2048]{1,0:T(8,128)(2,1)S(1)} %copy-done.8, bf16[512,2048]{1,0:T(8,128)(2,1)S(1)} %copy-done.6, ...), kind=kLoop, calls=%fused_computation.73 | loop fusion | flops 30408704 | bytes 19924224 | tf_op jit(solution)/shard_map/convert_element_type | solution.py:160
  149.3 1.7 convolution_convert_fusion.8
  150.9 15.5 %reduce-scatter.2.cloned.1.call-done = bf16[1,128,2048]{1,2,0:T(8,128)(2,1)} async-done(((bf16[4,128,2048]{1,2,0:T(8,128)(2,1)}), bf16[1,128,2048]{1,2,0:T(8,128)(2,1)}) %reduce-scatter.2.cloned.1.call-update) | async-done | bytes 524304 | tf_op jit(solution)/shard_map/reduce_scatter | solution.py:196
  166.4 1.1 bitcast_convert_fusion
  167.6 1.3 copy.19
  (33 shorter events, 0.2 us)
Async XLA Ops:
  7.2 25.4 %copy-start = (bf16[256,2048]{1,0:T(8,128)(2,1)S(1)}, bf16[256,2048]{1,0:T(8,128)(2,1)}, u32[]{:S(2)}) copy-start(bf16[256,2048]{1,0:T(8,128)(2,1)} %param.8) | copy-start | bytes 3145732
  7.2 8.3 %copy-start.9 = (bf16[256,2048]{1,0:T(8,128)(2,1)S(1)}, bf16[256,2048]{1,0:T(8,128)(2,1)}, u32[]{:S(2)}) copy-start(bf16[256,2048]{1,0:T(8,128)(2,1)} %param.9) | copy-start | bytes 3145732
  7.2 159.2 %reduce-scatter.2.cloned.1.call-start = ((), (), s32[]{:S(2)}) async-start(), calls=%async_computation.1 | async-start | bytes 2621440 | tf_op jit(solution)/shard_map/reduce_scatter | solution.py:196
  7.2 51.2 %collective-permute-start = (bf16[256,2048]{1,0:T(8,128)(2,1)}, bf16[256,2048]{1,0:T(8,128)(2,1)}, u32[]{:S(2)}, u32[]{:S(2)}) collective-permute-start(bf16[256,2048]{1,0:T(8,128)(2,1)} %param.9), channel_id=1, source_target_pairs={{2,0},{6,4},{10,8},{14,12},{3,1},{7,5},{11,9},{15,13},{18,16},{22,... | collective-permute-start | bytes 3145736 | tf_op jit(solution)/shard_map/ppermute | solution.py:20
  10.7 17.0 %collective-permute-start.1 = (bf16[256,1024]{1,0:T(8,128)(2,1)}, bf16[256,1024]{1,0:T(8,128)(2,1)S(1)}, u32[]{:S(2)}, u32[]{:S(2)}) collective-permute-start(bf16[256,1024]{1,0:T(8,128)(2,1)} %get-tuple-element.19), channel_id=1, source_target_pairs={{4,0},{6,2},{8,4},{10,6},{12,8},{14,10},{5,1},{7,3},{9,5},{11,7},{... | collective-permute-start | bytes 1572872 | tf_op jit(solution)/shard_map/ppermute | solution.py:15
  16.2 45.9 %copy-start.5 = (bf16[512,2048]{1,0:T(8,128)(2,1)}, bf16[512,2048]{1,0:T(8,128)(2,1)S(1)}, u32[]{:S(2)}) copy-start(bf16[512,2048]{1,0:T(8,128)(2,1)S(1)} %convolution_convert_fusion.5) | copy-start | bytes 6291460
  27.8 15.1 %collective-permute-start.3 = (bf16[256,1024]{1,0:T(8,128)(2,1)S(1)}, bf16[256,1024]{1,0:T(8,128)(2,1)S(1)}, u32[]{:S(2)}, u32[]{:S(2)}) collective-permute-start(bf16[256,1024]{1,0:T(8,128)(2,1)S(1)} %get-tuple-element.5), channel_id=1, source_target_pairs={{4,0},{6,2},{8,4},{10,6},{12,8},{14,10},{5,1},{7,3},{9,5},{11,7},{... | collective-permute-start | bytes 1572872 | tf_op jit(solution)/shard_map/ppermute | solution.py:15
  29.1 18.1 %collective-permute-start.2 = (bf16[256,1024]{1,0:T(8,128)(2,1)S(1)}, bf16[256,1024]{1,0:T(8,128)(2,1)S(1)}, u32[]{:S(2)}, u32[]{:S(2)}) collective-permute-start(bf16[256,1024]{1,0:T(8,128)(2,1)S(1)} %collective-permute-done.1), channel_id=1, source_target_pairs={{0,2},{2,0},{4,6},{6,4},{8,10},{10,8},{12,14},{14,12},{1,3},{3,1},... | collective-permute-start | bytes 1572872 | tf_op jit(solution)/shard_map/ppermute | solution.py:20
  42.9 14.6 %collective-permute-start.4 = (bf16[256,1024]{1,0:T(8,128)(2,1)S(1)}, bf16[256,1024]{1,0:T(8,128)(2,1)S(1)}, u32[]{:S(2)}, u32[]{:S(2)}) collective-permute-start(bf16[256,1024]{1,0:T(8,128)(2,1)S(1)} %collective-permute-done.3), channel_id=1, source_target_pairs={{0,2},{2,0},{4,6},{6,4},{8,10},{10,8},{12,14},{14,12},{1,3},{3,1},... | collective-permute-start | bytes 1572872 | tf_op jit(solution)/shard_map/ppermute | solution.py:20
  45.9 24.7 %collective-permute-start.6 = (bf16[256,2048]{1,0:T(8,128)(2,1)S(1)}, bf16[256,2048]{1,0:T(8,128)(2,1)S(1)}, u32[]{:S(2)}, u32[]{:S(2)}) collective-permute-start(bf16[256,2048]{1,0:T(8,128)(2,1)S(1)} %constant_dynamic-update-slice_fusion.2), channel_id=1, source_target_pairs={{4,0},{6,2},{8,4},{10,6},{12,8},{14,10},{5,1},{7,3},{9,5},{11,7},{... | collective-permute-start | bytes 3145736 | tf_op jit(solution)/shard_map/ppermute | solution.py:15
  47.9 24.1 %copy-start.3 = (bf16[512,2048]{1,0:T(8,128)(2,1)}, bf16[512,2048]{1,0:T(8,128)(2,1)S(1)}, u32[]{:S(2)}) copy-start(bf16[512,2048]{1,0:T(8,128)(2,1)S(1)} %convolution_convert_fusion.3) | copy-start | bytes 6291460
  57.5 13.8 %collective-permute-start.5 = (bf16[256,2048]{1,0:T(8,128)(2,1)S(1)}, bf16[256,2048]{1,0:T(8,128)(2,1)S(1)}, u32[]{:S(2)}, u32[]{:S(2)}) collective-permute-start(bf16[256,2048]{1,0:T(8,128)(2,1)S(1)} %constant_dynamic-update-slice_fusion), channel_id=1, source_target_pairs={{6,2},{10,6},{14,10},{7,3},{11,7},{15,11},{22,18},{26,22},{30,26},... | collective-permute-start | bytes 3145736 | tf_op jit(solution)/shard_map/ppermute | solution.py:42
  65.3 33.9 %collective-permute-start.7 = (bf16[2,128,2048]{1,2,0:T(8,128)(2,1)S(1)}, bf16[2,128,2048]{1,2,0:T(8,128)(2,1)S(1)}, u32[]{:S(2)}, u32[]{:S(2)}) collective-permute-start(bf16[2,128,2048]{1,2,0:T(8,128)(2,1)S(1)} %fusion), channel_id=1, source_target_pairs={{0,2},{2,0},{4,6},{6,4},{8,10},{10,8},{12,14},{14,12},{1,3},{3,1},... | collective-permute-start | bytes 3145736 | tf_op jit(solution)/shard_map/ppermute | solution.py:20
  71.3 2.5 %copy-start.7 = (bf16[512,2048]{1,0:T(8,128)(2,1)}, bf16[512,2048]{1,0:T(8,128)(2,1)S(1)}, u32[]{:S(2)}) copy-start(bf16[512,2048]{1,0:T(8,128)(2,1)S(1)} %convolution_convert_fusion.1) | copy-start | bytes 6291460
  72.1 1.7 copy-start.1
  75.5 23.7 %copy-start.12 = (f32[2048]{0:T(1024)S(1)}, f32[2048]{0:T(1024)}, u32[]{:S(2)}) copy-start(f32[2048]{0:T(1024)} %param.15) | copy-start | bytes 24580
  77.1 42.5 %collective-permute-start.8 = (bf16[2,128,2048]{1,2,0:T(8,128)(2,1)S(1)}, bf16[2,128,2048]{1,2,0:T(8,128)(2,1)S(1)}, u32[]{:S(2)}, u32[]{:S(2)}) collective-permute-start(bf16[2,128,2048]{1,2,0:T(8,128)(2,1)S(1)} %fusion.1), channel_id=1, source_target_pairs={{0,2},{2,0},{4,6},{6,4},{8,10},{10,8},{12,14},{14,12},{1,3},{3,1},... | collective-permute-start | bytes 3145736 | tf_op jit(solution)/shard_map/ppermute | solution.py:20
  122.7 1.8 %copy-start.11 = (f32[33,64]{1,0:T(8,128)S(1)}, f32[33,64]{1,0:T(8,128)}, u32[]{:S(2)}) copy-start(f32[33,64]{1,0:T(8,128)} %param.10) | copy-start | bytes 25348
  122.7 1.8 %copy-start.13 = (f32[64]{0:T(128)S(1)}, f32[64]{0:T(128)}, u32[]{:S(2)}) copy-start(f32[64]{0:T(128)} %param.13) | copy-start | bytes 772
  122.7 1.9 %copy-start.14 = (f32[64]{0:T(128)S(1)}, f32[64]{0:T(128)}, u32[]{:S(2)}) copy-start(f32[64]{0:T(128)} %param.11) | copy-start | bytes 772
  122.7 4.4 %copy-start.10 = (f32[64,64]{1,0:T(8,128)S(1)}, f32[64,64]{1,0:T(8,128)}, u32[]{:S(2)}) copy-start(f32[64,64]{1,0:T(8,128)} %param.12) | copy-start | bytes 49156
  122.8 6.5 %copy-start.15 = (f32[64,2048]{1,0:T(8,128)S(1)}, f32[64,2048]{1,0:T(8,128)}, u32[]{:S(2)}) copy-start(f32[64,2048]{1,0:T(8,128)} %param.14) | copy-start | bytes 1572868
  136.9 2.4 %copy-start.2 = (bf16[512,2048]{1,0:T(8,128)(2,1)S(1)}, bf16[512,2048]{1,0:T(8,128)(2,1)}, u32[]{:S(2)}) copy-start(bf16[512,2048]{1,0:T(8,128)(2,1)} %copy-done.1) | copy-start | bytes 6291460
  136.9 2.4 %copy-start.4 = (bf16[512,2048]{1,0:T(8,128)(2,1)S(1)}, bf16[512,2048]{1,0:T(8,128)(2,1)}, u32[]{:S(2)}) copy-start(bf16[512,2048]{1,0:T(8,128)(2,1)} %copy-done.3) | copy-start | bytes 6291460
  136.9 2.9 %copy-start.6 = (bf16[512,2048]{1,0:T(8,128)(2,1)S(1)}, bf16[512,2048]{1,0:T(8,128)(2,1)}, u32[]{:S(2)}) copy-start(bf16[512,2048]{1,0:T(8,128)(2,1)} %copy-done.5) | copy-start | bytes 6291460
  136.9 3.5 %copy-start.8 = (bf16[512,2048]{1,0:T(8,128)(2,1)S(1)}, bf16[512,2048]{1,0:T(8,128)(2,1)}, u32[]{:S(2)}) copy-start(bf16[512,2048]{1,0:T(8,128)(2,1)} %copy-done.7) | copy-start | bytes 6291460
Sparse Core Ops, SparseCore 0:
  122.9 43.5 reduce-scatter.1
